TPU v7x, 512 devices: a whole 4x4x16 slice. The times are simulated.
512 devices in a mesh: leaf: 8 (over y_hi, x), level: 64 (over y_lo, z, core).
Axes of the slice: x: 4, y: 4 (y_hi: 2, y_lo: 2; y = y_hi * 2 + y_lo), z: 16, core: 2. Of those that a mesh axis runs over, the one named last changes fastest.
Arguments:
- points: bfloat16 [524288, 64], P(('leaf', 'level')), may hold values from -1.6953125 to 1.6953125
- sketch_matrix: bfloat16 [524288, 64], P(('leaf', 'level')), may hold values from -6 to 6
- leaf_order: int32 [512, 1024], P(('leaf', 'level')), may hold values from 0 to 1023, each once within a row
Outputs:
- products: float32 [524288, 256], P(('leaf', 'level'))
- gram_out: float32 [512, 4, 64, 64], P(('leaf', 'level'))
Inputs may be any that keep to these rules, and one draw needn't show every extreme that they name: `leaf_order`: each row is a permutation of 0 to 1023.
All inputs are finite; a program needn't handle non-finite values.
Results may differ from a plain program's by a relative error of at most 0.0029.
Values may be sent and summed in bfloat16 or wider, within the bound.
No kernel may reach another device: no remote copies, remote signals or barrier semaphores. Data moves between devices by JAX's collectives and lax.ppermute only.
A program may use at most 64 MiB of HBM per device.

v0:
```python
import math

import jax
import jax.numpy as jnp
from jax import lax
from jax.sharding import PartitionSpec as P


def swapped(value, axis, stride):
    mask = 2**stride
    pairs = [(source, source ^ mask) for source in range(lax.axis_size(axis))]
    return lax.ppermute(value, axis, pairs)


def squares_of(coords):
    return jnp.sum(jnp.square(coords.astype(jnp.float32)), axis=-1)


def kernel_product(row_pts, row_sq, col_pts, col_sketch):
    width = row_pts.shape[1]
    col_sq = squares_of(col_pts)
    cross = lax.dot_general(
        row_pts, col_pts, (((1,), (1,)), ((), ())), preferred_element_type=jnp.float32
    )
    distance = row_sq[:, None] + col_sq[None, :] - 2.0 * cross
    kernel = jnp.exp((2.0 * width - distance) * (2.0 / width)).astype(jnp.bfloat16)
    return jnp.dot(kernel, col_sketch, preferred_element_type=jnp.float32)


def sketch(row_pts, row_sq, col_pts, col_sketch):
    rows_n = row_pts.shape[0]
    pieces = col_pts.shape[0] // rows_n
    blocked_pts = col_pts.reshape(pieces, rows_n, col_pts.shape[1])
    blocked_sketch = col_sketch.reshape(pieces, rows_n, col_sketch.shape[1])

    def absorb(running, piece):
        return (running + kernel_product(row_pts, row_sq, piece[0], piece[1]), None)

    start_value = jnp.zeros((rows_n, col_sketch.shape[1]), jnp.float32)
    running, _ = lax.scan(absorb, start_value, (blocked_pts, blocked_sketch))
    return running / math.sqrt(col_pts.shape[0])


def per_device(points, sketch_matrix, leaf_order):
    located = jnp.take(points, leaf_order[0], axis=0)
    row_sq = squares_of(located)
    rows_n = located.shape[0]
    leaf_bits = lax.axis_size("leaf").bit_length() - 1
    leaf_pos = lax.axis_index("leaf")
    own_pts = located
    own_sketch = sketch_matrix
    results = []
    for tier_num in range(leaf_bits):
        sib_pts, sib_sketch = swapped((own_pts, own_sketch), "leaf", tier_num)
        results.append(sketch(located, row_sq, sib_pts, sib_sketch))
        upper_half = leaf_pos >> tier_num & 1 == 1
        own_pts = jnp.where(
            upper_half, jnp.concatenate([sib_pts, own_pts]), jnp.concatenate([own_pts, sib_pts])
        )
        own_sketch = jnp.where(
            upper_half,
            jnp.concatenate([sib_sketch, own_sketch]),
            jnp.concatenate([own_sketch, sib_sketch]),
        )
    far_pts, far_sketch = swapped((own_pts, own_sketch), "level", 0)
    results.append(sketch(located, row_sq, far_pts, far_sketch))
    partial_grams = [
        jnp.dot(
            product.T, product, precision=lax.Precision.HIGHEST, preferred_element_type=jnp.float32
        )
        for product in results
    ]
    summed = []
    for tier_num in range(len(partial_grams)):
        local = partial_grams[tier_num]
        for bit_num in range(tier_num):
            local = local + swapped(local, "leaf", bit_num)
        summed.append(local)
    stacked = jnp.stack(summed)
    divisors = jnp.asarray(
        [float((1 << tier_num) * rows_n) for tier_num in range(len(partial_grams))], jnp.float32
    )
    stacked = stacked / divisors[:, None, None]
    return (jnp.concatenate(results, axis=1), stacked[None])


def solution(mesh):
    in_specs = (P(("leaf", "level"), None), P(("leaf", "level"), None), P(("leaf", "level"), None))
    out_specs = (P(("leaf", "level"), None), P(("leaf", "level"), None, None, None))
    return jax.shard_map(
        per_device, mesh=mesh, in_specs=in_specs, out_specs=out_specs, check_vma=False
    )
```

profile of v0, /device:TPU:504, one launch (start us, length us, event | category | flops | bytes accessed | tf_op | source)
XLA Modules:
  0.0 165.4 jit_solution(7753825887232468495)
XLA Ops:
  3.1 3.2 %gather_fusion = bf16[1024,64]{1,0:T(8,128)(2,1)S(1)} fusion(bf16[1024,64]{1,0:T(8,128)(2,1)S(1)} %copy.16, s32[1024]{0:T(1024)S(1)} %broadcast_clamp_fusion), kind=kCustom, calls=%fused_computation | custom fusion | bytes 266240 | tf_op jit(solution)/shard_map/jit(_take)/gather | solution.py:45
  6.7 3.4 %collective-permute-start = (bf16[1024,64]{1,0:T(8,128)(2,1)S(1)}, bf16[1024,64]{1,0:T(8,128)(2,1)S(1)}, u32[]{:S(2)}, u32[]{:S(2)}) collective-permute-start(bf16[1024,64]{1,0:T(8,128)(2,1)S(1)} %get-tuple-element.401), channel_id=1, source_target_pairs={{0,64},{64,0},{128,192},{192,128},{256,320},{320,256},{384,448},{4... | collective-permute-start | bytes 393224 | tf_op jit(solution)/shard_map/ppermute | solution.py:12
  10.3 2.4 %collective-permute-start.1 = (bf16[1024,64]{1,0:T(8,128)(2,1)S(1)}, bf16[1024,64]{1,0:T(8,128)(2,1)S(1)}, u32[]{:S(2)}, u32[]{:S(2)}) collective-permute-start(bf16[1024,64]{1,0:T(8,128)(2,1)S(1)} %copy.17), channel_id=1, source_target_pairs={{0,64},{64,0},{128,192},{192,128},{256,320},{320,256},{384,448},{4... | collective-permute-start | bytes 393224 | tf_op jit(solution)/shard_map/ppermute | solution.py:12
  12.8 5.0 %collective-permute-done = bf16[1024,64]{1,0:T(8,128)(2,1)S(1)} collective-permute-done((bf16[1024,64]{1,0:T(8,128)(2,1)S(1)}, bf16[1024,64]{1,0:T(8,128)(2,1)S(1)}, u32[]{:S(2)}, u32[]{:S(2)}) %collective-permute-start) | collective-permute-done | bytes 131104 | tf_op jit(solution)/shard_map/ppermute | solution.py:12
  18.0 4.9 %collective-permute-start.2 = (bf16[2048,64]{1,0:T(8,128)(2,1)S(1)}, bf16[2048,64]{1,0:T(8,128)(2,1)S(1)}, u32[]{:S(2)}, u32[]{:S(2)}) collective-permute-start(bf16[2048,64]{1,0:T(8,128)(2,1)S(1)} %maximum_select_fusion.4), channel_id=1, source_target_pairs={{0,128},{64,192},{128,0},{192,64},{256,384},{320,448},{384,256},{4... | collective-permute-start | bytes 786440 | tf_op jit(solution)/shard_map/ppermute | solution.py:12
  23.2 5.4 %collective-permute-start.3 = (bf16[2048,64]{1,0:T(8,128)(2,1)S(1)}, bf16[2048,64]{1,0:T(8,128)(2,1)S(1)}, u32[]{:S(2)}, u32[]{:S(2)}) collective-permute-start(bf16[2048,64]{1,0:T(8,128)(2,1)S(1)} %maximum_select_fusion.5), channel_id=1, source_target_pairs={{0,128},{64,192},{128,0},{192,64},{256,384},{320,448},{384,256},{4... | collective-permute-start | bytes 786440 | tf_op jit(solution)/shard_map/ppermute | solution.py:12
  28.8 1.7 %fusion.52 = f32[1024,64]{0,1:T(8,128)S(1)} fusion(bf16[1024,64]{1,0:T(8,128)(2,1)S(1)} %collective-permute-done.1, bf16[1024,64]{1,0:T(8,128)(2,1)S(1)} %get-tuple-element.401, bf16[1024,64]{1,0:T(8,128)(2,1)S(1)} %collective-permute-done, f32[1024]{0:T(1024)S(1)} %multiply_reduce_fusion.3, f32[1024]{0:T(1024)S(1)} %get-tuple-element.399), kind=kOutput, calls=%fused_computation.53 | convolution fusion | flops 274792448 | bytes 663552 | tf_op jit(solution)/shard_map/while/body/eval_jaxpr/dot_general | solution.py:27
  30.8 6.0 %collective-permute-done.2 = bf16[2048,64]{1,0:T(8,128)(2,1)S(1)} collective-permute-done((bf16[2048,64]{1,0:T(8,128)(2,1)S(1)}, bf16[2048,64]{1,0:T(8,128)(2,1)S(1)}, u32[]{:S(2)}, u32[]{:S(2)}) %collective-permute-start.2) | collective-permute-done | bytes 262176 | tf_op jit(solution)/shard_map/ppermute | solution.py:12
  36.8 10.1 %collective-permute-done.3 = bf16[2048,64]{1,0:T(8,128)(2,1)S(1)} collective-permute-done((bf16[2048,64]{1,0:T(8,128)(2,1)S(1)}, bf16[2048,64]{1,0:T(8,128)(2,1)S(1)}, u32[]{:S(2)}, u32[]{:S(2)}) %collective-permute-start.3) | collective-permute-done | bytes 262176 | tf_op jit(solution)/shard_map/ppermute | solution.py:12
  47.0 3.6 %while.37 = (s32[]{:T(128)}, f32[1024,64]{0,1:T(8,128)S(1)}, f32[1024]{0:T(1024)S(1)}, bf16[2,1024,64]{2,1,0:T(8,128)(2,1)S(1)}, bf16[1024,64]{1,0:T(8,128)(2,1)...) while((s32[]{:T(128)}, f32[1024,64]{0,1:T(8,128)S(1)}, f32[1024]{0:T(1024)S(1)}, ...), condition=%wide.region_4.5_spmd.clone, body=%wide.region_2.4_spmd.clone.sunk | while | flops 275053568 | bytes 1455722 | solution.py:40
  47.2 1.6 fusion.82
  49.0 1.6 fusion.82
  51.3 2.1 %collective-permute-start.8 = (f32[64,64]{1,0:T(8,128)S(1)}, f32[64,64]{1,0:T(8,128)S(1)}, u32[]{:S(2)}, u32[]{:S(2)}) collective-permute-start(f32[64,64]{1,0:T(8,128)S(1)} %fusion.56), channel_id=1, source_target_pairs={{0,64},{64,0},{128,192},{192,128},{256,320},{320,256},{384,448},{4... | collective-permute-start | bytes 49160 | tf_op jit(solution)/shard_map/ppermute | solution.py:12
  55.0 3.3 %collective-permute-start.5 = (bf16[4096,64]{0,1:T(8,128)(2,1)}, bf16[4096,64]{0,1:T(8,128)(2,1)}, u32[]{:S(2)}, u32[]{:S(2)}) collective-permute-start(bf16[4096,64]{0,1:T(8,128)(2,1)} %copy.21), channel_id=1, source_target_pairs={{0,256},{64,320},{128,384},{192,448},{256,0},{320,64},{384,128},{4... | collective-permute-start | bytes 1572872 | tf_op jit(solution)/shard_map/ppermute | solution.py:12
  60.5 4.2 %collective-permute-start.4 = (bf16[4096,64]{0,1:T(8,128)(2,1)}, bf16[4096,64]{0,1:T(8,128)(2,1)}, u32[]{:S(2)}, u32[]{:S(2)}) collective-permute-start(bf16[4096,64]{0,1:T(8,128)(2,1)} %copy.20), channel_id=1, source_target_pairs={{0,256},{64,320},{128,384},{192,448},{256,0},{320,64},{384,128},{4... | collective-permute-start | bytes 1572872 | tf_op jit(solution)/shard_map/ppermute | solution.py:12
  64.8 8.9 %collective-permute-done.5 = bf16[4096,64]{0,1:T(8,128)(2,1)} collective-permute-done((bf16[4096,64]{0,1:T(8,128)(2,1)}, bf16[4096,64]{0,1:T(8,128)(2,1)}, u32[]{:S(2)}, u32[]{:S(2)}) %collective-permute-start.5) | collective-permute-done | bytes 524320 | tf_op jit(solution)/shard_map/ppermute | solution.py:12
  75.1 2.1 %maximum_select_fusion.1 = bf16[8192,64]{1,0:T(8,128)(2,1)} fusion(bf16[4096,64]{1,0:T(8,128)(2,1)S(1)} %maximum_select_fusion.3, bf16[4096,64]{1,0:T(8,128)(2,1)S(1)} %copy.34, pred[]{:T(512)S(6)} %eq.11), kind=kLoop, calls=%fused_computation.51 | loop fusion | flops 4718592 | bytes 2097153 | tf_op jit(solution)/shard_map/jit(_where)/select_n | solution.py:60
  77.3 2.7 %copy.29 = bf16[8192,64]{0,1:T(8,128)(2,1)} copy(bf16[8192,64]{1,0:T(8,128)(2,1)} %maximum_select_fusion.1) | data formatting | bytes 2097152 | tf_op jit(solution)/shard_map/jit(_where)/select_n | solution.py:60
  79.9 2.7 %collective-permute-done.4 = bf16[4096,64]{0,1:T(8,128)(2,1)} collective-permute-done((bf16[4096,64]{0,1:T(8,128)(2,1)}, bf16[4096,64]{0,1:T(8,128)(2,1)}, u32[]{:S(2)}, u32[]{:S(2)}) %collective-permute-start.4) | collective-permute-done | bytes 524320 | tf_op jit(solution)/shard_map/ppermute | solution.py:12
  84.2 2.1 %maximum_select_fusion = bf16[8192,64]{1,0:T(8,128)(2,1)} fusion(bf16[4096,64]{1,0:T(8,128)(2,1)S(1)} %maximum_select_fusion.2, bf16[4096,64]{1,0:T(8,128)(2,1)S(1)} %copy.33, pred[]{:T(512)S(6)} %eq.11), kind=kLoop, calls=%fused_computation.50 | loop fusion | flops 4718592 | bytes 2097153 | tf_op jit(solution)/shard_map/jit(_where)/select_n | solution.py:57
  86.3 2.8 %copy.26 = bf16[8192,64]{0,1:T(8,128)(2,1)} copy(bf16[8192,64]{1,0:T(8,128)(2,1)} %maximum_select_fusion) | data formatting | bytes 2097152 | tf_op jit(solution)/shard_map/jit(_where)/select_n | solution.py:57
  89.1 1.9 %collective-permute-start.6 = (bf16[8192,64]{0,1:T(8,128)(2,1)}, bf16[8192,64]{0,1:T(8,128)(2,1)}, u32[]{:S(2)}, u32[]{:S(2)}) collective-permute-start(bf16[8192,64]{0,1:T(8,128)(2,1)} %copy.26), channel_id=1, source_target_pairs={{0,1},{1,0},{2,3},{3,2},{4,5},{5,4},{6,7},{7,6},{8,9},{9,8},{10,11... | collective-permute-start | bytes 3145736 | tf_op jit(solution)/shard_map/ppermute | solution.py:12
  91.0 2.6 %collective-permute-start.7 = (bf16[8192,64]{0,1:T(8,128)(2,1)S(1)}, bf16[8192,64]{0,1:T(8,128)(2,1)}, u32[]{:S(2)}, u32[]{:S(2)}) collective-permute-start(bf16[8192,64]{0,1:T(8,128)(2,1)S(1)} %copy-done), channel_id=1, source_target_pairs={{0,1},{1,0},{2,3},{3,2},{4,5},{5,4},{6,7},{7,6},{8,9},{9,8},{10,11... | collective-permute-start | bytes 3145736 | tf_op jit(solution)/shard_map/ppermute | solution.py:12
  93.6 13.8 %while.38 = (s32[]{:T(128)}, f32[1024,64]{0,1:T(8,128)}, f32[1024]{0:T(1024)S(1)}, bf16[4,1024,64]{2,1,0:T(8,128)(2,1)S(1)}, bf16[1024,64]{1,0:T(8,128)(2,1)}, /...) while((s32[]{:T(128)}, f32[1024,64]{0,1:T(8,128)}, f32[1024]{0:T(1024)S(1)}, ...), condition=%wide.region_7.8_spmd.clone, body=%wide.region_5.7_spmd.clone.sunk | while | flops 275053568 | bytes 1324650 | solution.py:40
  93.8 3.2 %fusion.86 = f32[1024,64]{0,1:T(8,128)} fusion(bf16[1024,64]{1,0:T(8,128)(2,1)} %get-tuple-element.393, f32[1024]{0:T(1024)S(1)} %multiply_reduce_fusion.9, f32[1024]{0:T(1024)S(1)} %get-tuple-element.391, f32[1024,64]{0,1:T(8,128)} %get-tuple-element.382, bf16[4,1024,64]{2,1,0:T(8,128)(2,1)S(1)} %get-tuple-element.394, s32[]{:T(128)S(6)} %copy.45, ...), kind=kOutput, calls=%fused_computation.23.clone.1 | convolution fusion | flops 274857984 | bytes 1189376 | tf_op jit(solution)/shard_map/while/body/eval_jaxpr/dot_general | solution.py:27
  97.2 3.3 %fusion.86 = f32[1024,64]{0,1:T(8,128)} fusion(bf16[1024,64]{1,0:T(8,128)(2,1)} %get-tuple-element.393, f32[1024]{0:T(1024)S(1)} %multiply_reduce_fusion.9, f32[1024]{0:T(1024)S(1)} %get-tuple-element.391, f32[1024,64]{0,1:T(8,128)} %get-tuple-element.382, bf16[4,1024,64]{2,1,0:T(8,128)(2,1)S(1)} %get-tuple-element.394, s32[]{:T(128)S(6)} %copy.45, ...), kind=kOutput, calls=%fused_computation.23.clone.1 | convolution fusion | flops 274857984 | bytes 1189376 | tf_op jit(solution)/shard_map/while/body/eval_jaxpr/dot_general | solution.py:27
  100.7 3.3 %fusion.86 = f32[1024,64]{0,1:T(8,128)} fusion(bf16[1024,64]{1,0:T(8,128)(2,1)} %get-tuple-element.393, f32[1024]{0:T(1024)S(1)} %multiply_reduce_fusion.9, f32[1024]{0:T(1024)S(1)} %get-tuple-element.391, f32[1024,64]{0,1:T(8,128)} %get-tuple-element.382, bf16[4,1024,64]{2,1,0:T(8,128)(2,1)S(1)} %get-tuple-element.394, s32[]{:T(128)S(6)} %copy.45, ...), kind=kOutput, calls=%fused_computation.23.clone.1 | convolution fusion | flops 274857984 | bytes 1189376 | tf_op jit(solution)/shard_map/while/body/eval_jaxpr/dot_general | solution.py:27
  104.2 3.3 %fusion.86 = f32[1024,64]{0,1:T(8,128)} fusion(bf16[1024,64]{1,0:T(8,128)(2,1)} %get-tuple-element.393, f32[1024]{0:T(1024)S(1)} %multiply_reduce_fusion.9, f32[1024]{0:T(1024)S(1)} %get-tuple-element.391, f32[1024,64]{0,1:T(8,128)} %get-tuple-element.382, bf16[4,1024,64]{2,1,0:T(8,128)(2,1)S(1)} %get-tuple-element.394, s32[]{:T(128)S(6)} %copy.45, ...), kind=kOutput, calls=%fused_computation.23.clone.1 | convolution fusion | flops 274857984 | bytes 1189376 | tf_op jit(solution)/shard_map/while/body/eval_jaxpr/dot_general | solution.py:27
  108.9 3.6 %collective-permute-start.9 = (f32[64,64]{1,0:T(8,128)S(1)}, f32[64,64]{1,0:T(8,128)S(1)}, u32[]{:S(2)}, u32[]{:S(2)}) collective-permute-start(f32[64,64]{1,0:T(8,128)S(1)} %fusion.57), channel_id=1, source_target_pairs={{0,64},{64,0},{128,192},{192,128},{256,320},{320,256},{384,448},{4... | collective-permute-start | bytes 49160 | tf_op jit(solution)/shard_map/ppermute | solution.py:12
  112.5 1.7 %broadcast_multiply_fusion.1 = f32[1024,64]{0,1:T(8,128)} fusion(f32[1024,64]{0,1:T(8,128)} %get-tuple-element.117), kind=kLoop, calls=%fused_computation.65 | loop fusion | flops 65536 | bytes 524288 | tf_op jit(solution)/shard_map/div | solution.py:41
  114.7 1.9 %collective-permute-start.10 = (f32[64,64]{1,0:T(8,128)S(1)}, f32[64,64]{1,0:T(8,128)S(1)}, u32[]{:S(2)}, u32[]{:S(2)}) collective-permute-start(f32[64,64]{1,0:T(8,128)S(1)} %add.128), channel_id=1, source_target_pairs={{0,128},{64,192},{128,0},{192,64},{256,384},{320,448},{384,256},{4... | collective-permute-start | bytes 49160 | tf_op jit(solution)/shard_map/ppermute | solution.py:12
  116.6 2.0 %copy.35 = bf16[8192,64]{1,0:T(8,128)(2,1)S(1)} copy(bf16[8192,64]{0,1:T(8,128)(2,1)} %collective-permute-done.6) | data formatting | bytes 2097152
  118.7 2.8 %copy.36 = bf16[8192,64]{1,0:T(8,128)(2,1)} copy(bf16[8192,64]{0,1:T(8,128)(2,1)} %collective-permute-done.7) | data formatting | bytes 2097152
  121.5 22.0 %while.39 = (s32[]{:T(128)}, f32[1024,64]{0,1:T(8,128)S(1)}, f32[1024]{0:T(1024)S(1)}, bf16[8,1024,64]{2,1,0:T(8,128)(2,1)S(1)}, bf16[1024,64]{1,0:T(8,128)(2,1)...) while((s32[]{:T(128)}, f32[1024,64]{0,1:T(8,128)S(1)}, f32[1024]{0:T(1024)S(1)}, ...), condition=%wide.region_10.11_spmd.clone, body=%wide.region_8.10_spmd.clone.sunk | while | flops 275053568 | bytes 1455722 | solution.py:40
  121.7 2.5 %fusion.90 = f32[1024,64]{0,1:T(8,128)S(1)} fusion(bf16[1024,64]{1,0:T(8,128)(2,1)S(1)} %get-tuple-element.369, f32[1024]{0:T(1024)S(1)} %multiply_reduce_fusion.10, f32[1024]{0:T(1024)S(1)} %get-tuple-element.367, f32[1024,64]{0,1:T(8,128)S(1)} %get-tuple-element.358, bf16[8,1024,64]{2,1,0:T(8,128)(2,1)} %get-tuple-element.370, s32[]{:T(128)S(6)} %copy.39, ...), kind=kOutput, calls=%fused_computation.39.clone.1 | convolution fusion | flops 274857984 | bytes 1320448 | tf_op jit(solution)/shard_map/while/body/eval_jaxpr/dot_general | solution.py:27
  124.5 2.5 %fusion.90 = f32[1024,64]{0,1:T(8,128)S(1)} fusion(bf16[1024,64]{1,0:T(8,128)(2,1)S(1)} %get-tuple-element.369, f32[1024]{0:T(1024)S(1)} %multiply_reduce_fusion.10, f32[1024]{0:T(1024)S(1)} %get-tuple-element.367, f32[1024,64]{0,1:T(8,128)S(1)} %get-tuple-element.358, bf16[8,1024,64]{2,1,0:T(8,128)(2,1)} %get-tuple-element.370, s32[]{:T(128)S(6)} %copy.39, ...), kind=kOutput, calls=%fused_computation.39.clone.1 | convolution fusion | flops 274857984 | bytes 1320448 | tf_op jit(solution)/shard_map/while/body/eval_jaxpr/dot_general | solution.py:27
  127.2 2.5 %fusion.90 = f32[1024,64]{0,1:T(8,128)S(1)} fusion(bf16[1024,64]{1,0:T(8,128)(2,1)S(1)} %get-tuple-element.369, f32[1024]{0:T(1024)S(1)} %multiply_reduce_fusion.10, f32[1024]{0:T(1024)S(1)} %get-tuple-element.367, f32[1024,64]{0,1:T(8,128)S(1)} %get-tuple-element.358, bf16[8,1024,64]{2,1,0:T(8,128)(2,1)} %get-tuple-element.370, s32[]{:T(128)S(6)} %copy.39, ...), kind=kOutput, calls=%fused_computation.39.clone.1 | convolution fusion | flops 274857984 | bytes 1320448 | tf_op jit(solution)/shard_map/while/body/eval_jaxpr/dot_general | solution.py:27
  130.0 2.5 %fusion.90 = f32[1024,64]{0,1:T(8,128)S(1)} fusion(bf16[1024,64]{1,0:T(8,128)(2,1)S(1)} %get-tuple-element.369, f32[1024]{0:T(1024)S(1)} %multiply_reduce_fusion.10, f32[1024]{0:T(1024)S(1)} %get-tuple-element.367, f32[1024,64]{0,1:T(8,128)S(1)} %get-tuple-element.358, bf16[8,1024,64]{2,1,0:T(8,128)(2,1)} %get-tuple-element.370, s32[]{:T(128)S(6)} %copy.39, ...), kind=kOutput, calls=%fused_computation.39.clone.1 | convolution fusion | flops 274857984 | bytes 1320448 | tf_op jit(solution)/shard_map/while/body/eval_jaxpr/dot_general | solution.py:27
  132.7 2.5 %fusion.90 = f32[1024,64]{0,1:T(8,128)S(1)} fusion(bf16[1024,64]{1,0:T(8,128)(2,1)S(1)} %get-tuple-element.369, f32[1024]{0:T(1024)S(1)} %multiply_reduce_fusion.10, f32[1024]{0:T(1024)S(1)} %get-tuple-element.367, f32[1024,64]{0,1:T(8,128)S(1)} %get-tuple-element.358, bf16[8,1024,64]{2,1,0:T(8,128)(2,1)} %get-tuple-element.370, s32[]{:T(128)S(6)} %copy.39, ...), kind=kOutput, calls=%fused_computation.39.clone.1 | convolution fusion | flops 274857984 | bytes 1320448 | tf_op jit(solution)/shard_map/while/body/eval_jaxpr/dot_general | solution.py:27
  135.5 2.5 %fusion.90 = f32[1024,64]{0,1:T(8,128)S(1)} fusion(bf16[1024,64]{1,0:T(8,128)(2,1)S(1)} %get-tuple-element.369, f32[1024]{0:T(1024)S(1)} %multiply_reduce_fusion.10, f32[1024]{0:T(1024)S(1)} %get-tuple-element.367, f32[1024,64]{0,1:T(8,128)S(1)} %get-tuple-element.358, bf16[8,1024,64]{2,1,0:T(8,128)(2,1)} %get-tuple-element.370, s32[]{:T(128)S(6)} %copy.39, ...), kind=kOutput, calls=%fused_computation.39.clone.1 | convolution fusion | flops 274857984 | bytes 1320448 | tf_op jit(solution)/shard_map/while/body/eval_jaxpr/dot_general | solution.py:27
  138.2 2.5 %fusion.90 = f32[1024,64]{0,1:T(8,128)S(1)} fusion(bf16[1024,64]{1,0:T(8,128)(2,1)S(1)} %get-tuple-element.369, f32[1024]{0:T(1024)S(1)} %multiply_reduce_fusion.10, f32[1024]{0:T(1024)S(1)} %get-tuple-element.367, f32[1024,64]{0,1:T(8,128)S(1)} %get-tuple-element.358, bf16[8,1024,64]{2,1,0:T(8,128)(2,1)} %get-tuple-element.370, s32[]{:T(128)S(6)} %copy.39, ...), kind=kOutput, calls=%fused_computation.39.clone.1 | convolution fusion | flops 274857984 | bytes 1320448 | tf_op jit(solution)/shard_map/while/body/eval_jaxpr/dot_general | solution.py:27
  141.0 2.5 %fusion.90 = f32[1024,64]{0,1:T(8,128)S(1)} fusion(bf16[1024,64]{1,0:T(8,128)(2,1)S(1)} %get-tuple-element.369, f32[1024]{0:T(1024)S(1)} %multiply_reduce_fusion.10, f32[1024]{0:T(1024)S(1)} %get-tuple-element.367, f32[1024,64]{0,1:T(8,128)S(1)} %get-tuple-element.358, bf16[8,1024,64]{2,1,0:T(8,128)(2,1)} %get-tuple-element.370, s32[]{:T(128)S(6)} %copy.39, ...), kind=kOutput, calls=%fused_computation.39.clone.1 | convolution fusion | flops 274857984 | bytes 1320448 | tf_op jit(solution)/shard_map/while/body/eval_jaxpr/dot_general | solution.py:27
  143.9 3.6 %collective-permute-start.11 = (f32[64,64]{1,0:T(8,128)S(1)}, f32[64,64]{1,0:T(8,128)S(1)}, u32[]{:S(2)}, u32[]{:S(2)}) collective-permute-start(f32[64,64]{1,0:T(8,128)S(1)} %fusion.58), channel_id=1, source_target_pairs={{0,64},{64,0},{128,192},{192,128},{256,320},{320,256},{384,448},{4... | collective-permute-start | bytes 49160 | tf_op jit(solution)/shard_map/ppermute | solution.py:12
  147.6 2.1 %collective-permute-done.11 = f32[64,64]{1,0:T(8,128)S(1)} collective-permute-done((f32[64,64]{1,0:T(8,128)S(1)}, f32[64,64]{1,0:T(8,128)S(1)}, u32[]{:S(2)}, u32[]{:S(2)}) %collective-permute-start.11) | collective-permute-done | bytes 16416 | tf_op jit(solution)/shard_map/ppermute | solution.py:12
  149.7 5.7 %collective-permute-start.12 = (f32[64,64]{1,0:T(8,128)S(1)}, f32[64,64]{1,0:T(8,128)S(1)}, u32[]{:S(2)}, u32[]{:S(2)}) collective-permute-start(f32[64,64]{1,0:T(8,128)S(1)} %add.130), channel_id=1, source_target_pairs={{0,128},{64,192},{128,0},{192,64},{256,384},{320,448},{384,256},{4... | collective-permute-start | bytes 49160 | tf_op jit(solution)/shard_map/ppermute | solution.py:12
  155.5 1.8 %collective-permute-done.12 = f32[64,64]{1,0:T(8,128)S(1)} collective-permute-done((f32[64,64]{1,0:T(8,128)S(1)}, f32[64,64]{1,0:T(8,128)S(1)}, u32[]{:S(2)}, u32[]{:S(2)}) %collective-permute-start.12) | collective-permute-done | bytes 16416 | tf_op jit(solution)/shard_map/ppermute | solution.py:12
  157.3 3.1 %collective-permute-start.13 = (f32[64,64]{1,0:T(8,128)S(1)}, f32[64,64]{1,0:T(8,128)S(1)}, u32[]{:S(2)}, u32[]{:S(2)}) collective-permute-start(f32[64,64]{1,0:T(8,128)S(1)} %add.131), channel_id=1, source_target_pairs={{0,256},{64,320},{128,384},{192,448},{256,0},{320,64},{384,128},{4... | collective-permute-start | bytes 49160 | tf_op jit(solution)/shard_map/ppermute | solution.py:12
  161.9 2.7 %collective-permute-done.13 = f32[64,64]{1,0:T(8,128)S(1)} collective-permute-done((f32[64,64]{1,0:T(8,128)S(1)}, f32[64,64]{1,0:T(8,128)S(1)}, u32[]{:S(2)}, u32[]{:S(2)}) %collective-permute-start.13) | collective-permute-done | bytes 16416 | tf_op jit(solution)/shard_map/ppermute | solution.py:12
  (73 shorter events, 19.1 us)
Async XLA Ops:
  0.6 9.5 %copy-start.8 = (bf16[1024,64]{0,1:T(8,128)(2,1)S(1)}, bf16[1024,64]{0,1:T(8,128)(2,1)}, u32[]{:S(2)}) copy-start(bf16[1024,64]{0,1:T(8,128)(2,1)} %param.11) | copy-start | bytes 393220
  6.7 11.1 %collective-permute-start = (bf16[1024,64]{1,0:T(8,128)(2,1)S(1)}, bf16[1024,64]{1,0:T(8,128)(2,1)S(1)}, u32[]{:S(2)}, u32[]{:S(2)}) collective-permute-start(bf16[1024,64]{1,0:T(8,128)(2,1)S(1)} %get-tuple-element.401), channel_id=1, source_target_pairs={{0,64},{64,0},{128,192},{192,128},{256,320},{320,256},{384,448},{4... | collective-permute-start | bytes 393224 | tf_op jit(solution)/shard_map/ppermute | solution.py:12
  10.3 12.6 %collective-permute-start.1 = (bf16[1024,64]{1,0:T(8,128)(2,1)S(1)}, bf16[1024,64]{1,0:T(8,128)(2,1)S(1)}, u32[]{:S(2)}, u32[]{:S(2)}) collective-permute-start(bf16[1024,64]{1,0:T(8,128)(2,1)S(1)} %copy.17), channel_id=1, source_target_pairs={{0,64},{64,0},{128,192},{192,128},{256,320},{320,256},{384,448},{4... | collective-permute-start | bytes 393224 | tf_op jit(solution)/shard_map/ppermute | solution.py:12
  18.0 18.8 %collective-permute-start.2 = (bf16[2048,64]{1,0:T(8,128)(2,1)S(1)}, bf16[2048,64]{1,0:T(8,128)(2,1)S(1)}, u32[]{:S(2)}, u32[]{:S(2)}) collective-permute-start(bf16[2048,64]{1,0:T(8,128)(2,1)S(1)} %maximum_select_fusion.4), channel_id=1, source_target_pairs={{0,128},{64,192},{128,0},{192,64},{256,384},{320,448},{384,256},{4... | collective-permute-start | bytes 786440 | tf_op jit(solution)/shard_map/ppermute | solution.py:12
  23.2 23.8 %collective-permute-start.3 = (bf16[2048,64]{1,0:T(8,128)(2,1)S(1)}, bf16[2048,64]{1,0:T(8,128)(2,1)S(1)}, u32[]{:S(2)}, u32[]{:S(2)}) collective-permute-start(bf16[2048,64]{1,0:T(8,128)(2,1)S(1)} %maximum_select_fusion.5), channel_id=1, source_target_pairs={{0,128},{64,192},{128,0},{192,64},{256,384},{320,448},{384,256},{4... | collective-permute-start | bytes 786440 | tf_op jit(solution)/shard_map/ppermute | solution.py:12
  50.5 0.7 copy-start.2
  50.6 0.8 copy-start.4
  51.3 13.4 %collective-permute-start.8 = (f32[64,64]{1,0:T(8,128)S(1)}, f32[64,64]{1,0:T(8,128)S(1)}, u32[]{:S(2)}, u32[]{:S(2)}) collective-permute-start(f32[64,64]{1,0:T(8,128)S(1)} %fusion.56), channel_id=1, source_target_pairs={{0,64},{64,0},{128,192},{192,128},{256,320},{320,256},{384,448},{4... | collective-permute-start | bytes 49160 | tf_op jit(solution)/shard_map/ppermute | solution.py:12
  55.0 3.7 %copy-start.3 = (f32[1024,64]{0,1:T(8,128)S(1)}, f32[1024,64]{0,1:T(8,128)}, u32[]{:S(2)}) copy-start(f32[1024,64]{0,1:T(8,128)} %copy-done.2) | copy-start | bytes 786436
  55.0 18.6 %collective-permute-start.5 = (bf16[4096,64]{0,1:T(8,128)(2,1)}, bf16[4096,64]{0,1:T(8,128)(2,1)}, u32[]{:S(2)}, u32[]{:S(2)}) collective-permute-start(bf16[4096,64]{0,1:T(8,128)(2,1)} %copy.21), channel_id=1, source_target_pairs={{0,256},{64,320},{128,384},{192,448},{256,0},{320,64},{384,128},{4... | collective-permute-start | bytes 1572872 | tf_op jit(solution)/shard_map/ppermute | solution.py:12
  60.5 22.1 %collective-permute-start.4 = (bf16[4096,64]{0,1:T(8,128)(2,1)}, bf16[4096,64]{0,1:T(8,128)(2,1)}, u32[]{:S(2)}, u32[]{:S(2)}) collective-permute-start(bf16[4096,64]{0,1:T(8,128)(2,1)} %copy.20), channel_id=1, source_target_pairs={{0,256},{64,320},{128,384},{192,448},{256,0},{320,64},{384,128},{4... | collective-permute-start | bytes 1572872 | tf_op jit(solution)/shard_map/ppermute | solution.py:12
  86.3 4.7 %copy-start = (bf16[8192,64]{0,1:T(8,128)(2,1)S(1)}, bf16[8192,64]{0,1:T(8,128)(2,1)}, u32[]{:S(2)}) copy-start(bf16[8192,64]{0,1:T(8,128)(2,1)} %copy.29) | copy-start | bytes 3145732
  89.1 27.5 %collective-permute-start.6 = (bf16[8192,64]{0,1:T(8,128)(2,1)}, bf16[8192,64]{0,1:T(8,128)(2,1)}, u32[]{:S(2)}, u32[]{:S(2)}) collective-permute-start(bf16[8192,64]{0,1:T(8,128)(2,1)} %copy.26), channel_id=1, source_target_pairs={{0,1},{1,0},{2,3},{3,2},{4,5},{5,4},{6,7},{7,6},{8,9},{9,8},{10,11... | collective-permute-start | bytes 3145736 | tf_op jit(solution)/shard_map/ppermute | solution.py:12
  91.0 27.6 %collective-permute-start.7 = (bf16[8192,64]{0,1:T(8,128)(2,1)S(1)}, bf16[8192,64]{0,1:T(8,128)(2,1)}, u32[]{:S(2)}, u32[]{:S(2)}) collective-permute-start(bf16[8192,64]{0,1:T(8,128)(2,1)S(1)} %copy-done), channel_id=1, source_target_pairs={{0,1},{1,0},{2,3},{3,2},{4,5},{5,4},{6,7},{7,6},{8,9},{9,8},{10,11... | collective-permute-start | bytes 3145736 | tf_op jit(solution)/shard_map/ppermute | solution.py:12
  108.9 5.8 %collective-permute-start.9 = (f32[64,64]{1,0:T(8,128)S(1)}, f32[64,64]{1,0:T(8,128)S(1)}, u32[]{:S(2)}, u32[]{:S(2)}) collective-permute-start(f32[64,64]{1,0:T(8,128)S(1)} %fusion.57), channel_id=1, source_target_pairs={{0,64},{64,0},{128,192},{192,128},{256,320},{320,256},{384,448},{4... | collective-permute-start | bytes 49160 | tf_op jit(solution)/shard_map/ppermute | solution.py:12
  114.7 32.9 %collective-permute-start.10 = (f32[64,64]{1,0:T(8,128)S(1)}, f32[64,64]{1,0:T(8,128)S(1)}, u32[]{:S(2)}, u32[]{:S(2)}) collective-permute-start(f32[64,64]{1,0:T(8,128)S(1)} %add.128), channel_id=1, source_target_pairs={{0,128},{64,192},{128,0},{192,64},{256,384},{320,448},{384,256},{4... | collective-permute-start | bytes 49160 | tf_op jit(solution)/shard_map/ppermute | solution.py:12
  118.6 2.8 %copy-start.1 = (f32[1024,64]{0,1:T(8,128)S(1)}, f32[1024,64]{0,1:T(8,128)}, u32[]{:S(2)}) copy-start(f32[1024,64]{0,1:T(8,128)} %custom-call.2) | copy-start | bytes 786436
  118.7 2.8 %copy-start.5 = (bf16[1024,64]{1,0:T(8,128)(2,1)S(1)}, bf16[1024,64]{1,0:T(8,128)(2,1)}, u32[]{:S(2)}) copy-start(bf16[1024,64]{1,0:T(8,128)(2,1)} %get-tuple-element.429) | copy-start | bytes 393220
  121.5 39.0 %copy-start.6 = (f32[1024,64]{0,1:T(8,128)S(1)}, f32[1024,64]{0,1:T(8,128)}, u32[]{:S(2)}) copy-start(f32[1024,64]{0,1:T(8,128)} %broadcast_multiply_fusion.2) | copy-start | bytes 786436
  121.5 39.0 %copy-start.7 = (f32[1024,64]{0,1:T(8,128)S(1)}, f32[1024,64]{0,1:T(8,128)}, u32[]{:S(2)}) copy-start(f32[1024,64]{0,1:T(8,128)} %broadcast_multiply_fusion.1) | copy-start | bytes 786436
  143.9 5.8 %collective-permute-start.11 = (f32[64,64]{1,0:T(8,128)S(1)}, f32[64,64]{1,0:T(8,128)S(1)}, u32[]{:S(2)}, u32[]{:S(2)}) collective-permute-start(f32[64,64]{1,0:T(8,128)S(1)} %fusion.58), channel_id=1, source_target_pairs={{0,64},{64,0},{128,192},{192,128},{256,320},{320,256},{384,448},{4... | collective-permute-start | bytes 49160 | tf_op jit(solution)/shard_map/ppermute | solution.py:12
  149.7 7.6 %collective-permute-start.12 = (f32[64,64]{1,0:T(8,128)S(1)}, f32[64,64]{1,0:T(8,128)S(1)}, u32[]{:S(2)}, u32[]{:S(2)}) collective-permute-start(f32[64,64]{1,0:T(8,128)S(1)} %add.130), channel_id=1, source_target_pairs={{0,128},{64,192},{128,0},{192,64},{256,384},{320,448},{384,256},{4... | collective-permute-start | bytes 49160 | tf_op jit(solution)/shard_map/ppermute | solution.py:12
  157.3 7.3 %copy-start.9 = (f32[4]{0:T(128)S(1)}, f32[4]{0:T(128)}, u32[]{:S(2)}) copy-start(f32[4]{0:T(128)} %constant.111) | copy-start | bytes 52
  157.3 7.3 %collective-permute-start.13 = (f32[64,64]{1,0:T(8,128)S(1)}, f32[64,64]{1,0:T(8,128)S(1)}, u32[]{:S(2)}, u32[]{:S(2)}) collective-permute-start(f32[64,64]{1,0:T(8,128)S(1)} %add.131), channel_id=1, source_target_pairs={{0,256},{64,320},{128,384},{192,448},{256,0},{320,64},{384,128},{4... | collective-permute-start | bytes 49160 | tf_op jit(solution)/shard_map/ppermute | solution.py:12
where the time goes:
time: 168 us; the launch traced here: 165 us
  starting transfers between devices  48.3 us (29%)
  matrix products  40.2 us (24%)
  waiting for transfers between devices  39.9 us (24%)
  local copies, waits for them, and re-layouts  21.7 us (13%)
  other arithmetic  13.8 us (8%)
    ppermute x14, starting transfers between devices, swapped(): return lax.ppermute(value, axis, pairs)  48.3 us
    ppermute x14, waiting for transfers between devices, swapped(): return lax.ppermute(value, axis, pairs)  39.9 us
    dot_general x15, matrix products, kernel_product(): return jnp.dot(kernel, col_sketch, preferred_element_type=jnp.float32)  37.8 us
    unnamed x27, local copies, waits for them, and re-layouts  10.8 us
    select_n x2, local copies, waits for them, and re-layouts, per_device(): jnp.where(upper_half, jnp.concatenate([sib_pts, own_pts]), jnp.concatenat...  3.89 us
    select_n x2, local copies, waits for them, and re-layouts, per_device(): jnp.where(upper_half, jnp.concatenate([sib_sketch, own_sketch]), jnp.conc...  3.8 us
    reduce_sum x16, other arithmetic, squares_of(): return jnp.sum(jnp.square(coords.astype(jnp.float32)), axis=-1)  3.58 us
  transfers between devices with their start and end apart: 14, of which 9 were waited for; matrix products, arithmetic and copies ran while one was open for 35% of the time, Pallas kernels for 0%

commit v1 on v0

v1 whole, which is shorter than its diff:
```python
import math

import jax
import jax.numpy as jnp
from jax import lax
from jax.sharding import Mesh, PartitionSpec as P


def squares_of(coords):
    return jnp.sum(jnp.square(coords.astype(jnp.float32)), axis=-1)


def tier_product(row_pts, row_sq, cols, dim):
    col_pts = cols[:, :dim]
    col_sketch = cols[:, dim:]
    col_sq = squares_of(col_pts)
    cross = lax.dot_general(
        row_pts, col_pts, (((1,), (1,)), ((), ())), preferred_element_type=jnp.float32
    )
    distance = row_sq[:, None] + col_sq[None, :] - 2.0 * cross
    kernel = jnp.exp((2.0 * dim - distance) * (2.0 / dim)).astype(jnp.bfloat16)
    out = jnp.dot(kernel, col_sketch, preferred_element_type=jnp.float32)
    return out / math.sqrt(cols.shape[0])


def per_device(points, sketch_matrix, leaf_order):
    dim = points.shape[1]
    located = jnp.take(points, leaf_order[0], axis=0)
    rows_n = located.shape[0]
    row_sq = squares_of(located)
    packed = jnp.concatenate([located, sketch_matrix], axis=1)
    n_leaf = lax.axis_size("leaf")
    leaf_bits = n_leaf.bit_length() - 1
    gathered = lax.all_gather(packed, ("leaf", "pair"))
    blocks = gathered.reshape(n_leaf, 2, rows_n, packed.shape[1])
    leaf_pos = lax.axis_index("leaf")
    pair_pos = lax.axis_index("pair")
    near = lax.dynamic_index_in_dim(blocks, pair_pos, axis=1, keepdims=False)
    far = lax.dynamic_index_in_dim(blocks, 1 - pair_pos, axis=1, keepdims=False)
    results = []
    for tier_num in range(leaf_bits):
        half = 1 << tier_num
        start = ((leaf_pos >> tier_num) ^ 1) << tier_num
        sib = lax.dynamic_slice_in_dim(near, start, half, axis=0)
        results.append(tier_product(located, row_sq, sib.reshape(half * rows_n, -1), dim))
    results.append(tier_product(located, row_sq, far.reshape(n_leaf * rows_n, -1), dim))
    partial_grams = jnp.stack(
        [
            jnp.dot(p.T, p, precision=lax.Precision.HIGHEST, preferred_element_type=jnp.float32)
            for p in results
        ]
    )
    all_grams = lax.all_gather(partial_grams[1:], "leaf")
    leaf_ids = jnp.arange(n_leaf, dtype=jnp.int32)
    summed = [partial_grams[0]]
    for tier_num in range(1, len(results)):
        member = (leaf_ids >> tier_num) == (leaf_pos >> tier_num)
        picked = jnp.where(member[:, None, None], all_grams[:, tier_num - 1], 0.0)
        summed.append(jnp.sum(picked, axis=0))
    stacked = jnp.stack(summed)
    divisors = jnp.asarray(
        [float((1 << tier_num) * rows_n) for tier_num in range(len(results))], jnp.float32
    )
    stacked = stacked / divisors[:, None, None]
    return (jnp.concatenate(results, axis=1), stacked[None])


def solution(mesh):
    n_leaf = mesh.shape["leaf"]
    n_level = mesh.shape["level"]
    fine = Mesh(mesh.devices.reshape(n_leaf, n_level // 2, 2), ("leaf", "lvl", "pair"))
    axes = ("leaf", "lvl", "pair")
    in_specs = (P(axes, None), P(axes, None), P(axes, None))
    out_specs = (P(axes, None), P(axes, None, None, None))
    return jax.shard_map(
        per_device, mesh=fine, in_specs=in_specs, out_specs=out_specs, check_vma=False
    )
```

time: 168 us -> 172 us (1.024)
  the two profiles are of different devices: /device:TPU:504 before, /device:TPU:6 now
where the time goes in v1:
time: 172 us
  waiting for transfers between devices  75.8 us (44%)
  blocking collectives  35.8 us (21%)
  matrix products  27.7 us (16%)
  between operations  14.3 us (8%)
  local copies, waits for them, and re-layouts  12.4 us (7%)
  other arithmetic  5.94 us (3%)
    all_gather x1, waiting for transfers between devices, per_device(): gathered = lax.all_gather(packed, ('leaf', 'pair'))  75.8 us
    all_gather x1, blocking collectives, per_device(): all_grams = lax.all_gather(partial_grams[1:], 'leaf')  35.8 us
    dot_general x4, matrix products, tier_product(): out = jnp.dot(kernel, col_sketch, preferred_element_type=jnp.float32)  26.2 us
    unnamed x9, local copies, waits for them, and re-layouts  4.14 us
  transfers between devices with their start and end apart: 1, of which 1 were waited for; matrix products, arithmetic and copies ran while one was open for 0% of the time, Pallas kernels for 0%

profile of v1, /device:TPU:6, one launch (start us, length us, event | category | flops | bytes accessed | tf_op | source)
XLA Modules:
  0.0 171.9 jit_solution(8619462166320664099)
XLA Ops:
  7.2 0.0 all-gather.4.cloned.1.call-start
  7.2 1.1 copy.17
  8.3 1.1 copy.16
  9.4 0.7 compare_select_fusion
  10.1 0.7 compare_and_fusion
  10.8 3.2 %gather_fusion = bf16[1024,64]{1,0:T(8,128)(2,1)S(1)} fusion(bf16[1024,64]{1,0:T(8,128)(2,1)S(1)} %copy.16, s32[1024]{0:T(1024)S(1)} %broadcast_clamp_fusion), kind=kCustom, calls=%fused_computation | custom fusion | bytes 266240 | tf_op jit(solution)/shard_map/jit(_take)/gather | solution.py:28
  14.0 0.4 multiply_reduce_fusion.4
  14.3 0.0 copy-start
  14.4 0.7 copy-done
  15.0 0.8 pad_maximum_fusion.1
  15.9 0.0 all-gather.4.cloned.1.call-update
  16.0 75.8 %all-gather.4.cloned.1.call-done = bf16[16384,128]{1,0:T(8,128)(2,1)} async-done(((bf16[1024,128]{1,0:T(8,128)(2,1)}), bf16[16384,128]{1,0:T(8,128)(2,1)}) %all-gather.4.cloned.1.call-update) | async-done | bytes 4194320 | tf_op jit(solution)/shard_map/all_gather | solution.py:34
  91.8 1.7 %constant_dynamic-slice_fusion = bf16[8,1,1024,128]{3,2,1,0:T(8,128)(2,1)S(1)} fusion(bf16[8,2,1024,128]{3,2,1,0:T(8,128)(2,1)} %bitcast.60, s32[]{:T(128)S(6)} %select_n.65), kind=kLoop, calls=%fused_computation.50 | loop fusion | bytes 4194308 | tf_op jit(solution)/shard_map/jit(dynamic_index_in_dim)/dynamic_slice | solution.py:39
  93.5 1.2 multiply_reduce_fusion
  94.7 1.3 constant_dynamic-slice_fusion.1
  96.0 0.6 multiply_reduce_fusion.1
  96.6 14.1 %fusion.9 = f32[1024,64]{0,1:T(8,128)S(1)} fusion(bf16[8192,128]{1,0:T(8,128)(2,1)S(1)} %bitcast.57, f32[8192]{0:T(1024)S(1)} %multiply_reduce_fusion, f32[1024]{0:T(1024)S(1)} %get-tuple-element.11, bf16[1024,64]{1,0:T(8,128)(2,1)} %copy-done), kind=kOutput, calls=%fused_computation.14 | convolution fusion | flops 2197880832 | bytes 4624384 | tf_op jit(solution)/shard_map/dot_general | solution.py:22
  110.7 0.0 copy-start.1
  110.7 7.3 %fusion.16 = f32[1024,64]{0,1:T(8,128)S(1)} fusion(bf16[1024,64]{1,0:T(8,128)(2,1)} %copy-done, f32[4096]{0:T(1024)S(1)} %multiply_reduce_fusion.1, f32[1024]{0:T(1024)S(1)} %get-tuple-element.11, bf16[4096,128]{1,0:T(8,128)(2,1)S(1)} %bitcast.59), kind=kOutput, calls=%fused_computation.17 | convolution fusion | flops 1098973184 | bytes 2510848 | tf_op jit(solution)/shard_map/dot_general | solution.py:22
  118.0 1.1 constant_dynamic-slice_fusion.2
  119.1 0.3 multiply_reduce_fusion.2
  119.4 0.0 copy-done.1
  119.4 3.1 %fusion.15 = f32[1024,64]{0,1:T(8,128)S(1)} fusion(bf16[1024,64]{1,0:T(8,128)(2,1)S(1)} %copy-done.1, f32[2048]{0:T(1024)S(1)} %multiply_reduce_fusion.2, f32[1024]{0:T(1024)S(1)} %get-tuple-element.11, bf16[2048,128]{1,0:T(8,128)(2,1)S(1)} %bitcast.66), kind=kOutput, calls=%fused_computation.16 | convolution fusion | flops 549519360 | bytes 1585152 | tf_op jit(solution)/shard_map/dot_general | solution.py:22
  122.6 1.0 dynamic-slice_bitcast_fusion
  123.6 0.2 multiply_reduce_fusion.3
  123.8 1.7 fusion.14
  125.5 0.0 copy-start.2
  125.5 0.4 convolution_bitcast_fusion
  125.8 0.4 convolution_bitcast_fusion.1
  126.2 0.4 convolution_bitcast_fusion.2
  126.6 0.1 pad_maximum_fusion
  126.7 0.4 convolution_bitcast_fusion.3
  127.1 1.3 copy.20
  128.4 35.8 %all-gather.1 = f32[24,64,64]{2,1,0:T(8,128)S(1)} all-gather(f32[3,64,64]{2,1,0:T(8,128)S(1)} %pad_maximum_fusion.2), channel_id=3, replica_groups=mesh['leaf'=8,'lvl'=32,'pair'=2] {'leaf'}, dimensions={0}, use_global_device_ids=true | all-gather | bytes 442368 | tf_op jit(solution)/shard_map/all_gather | solution.py:53
  164.2 0.1 fusion.28
  164.3 0.0 copy-done.2
  164.3 0.7 maximum_multiply_fusion
  (4 shorter events, 0.0 us)
Async XLA Ops:
  7.2 84.6 %all-gather.4.cloned.1.call-start = ((), (), s32[]{:S(2)}) async-start(), calls=%async_computation | async-start | bytes 4456448 | tf_op jit(solution)/shard_map/all_gather | solution.py:34
  14.3 0.7 copy-start
  110.7 8.7 %copy-start.1 = (bf16[1024,64]{1,0:T(8,128)(2,1)S(1)}, bf16[1024,64]{1,0:T(8,128)(2,1)}, u32[]{:S(2)}) copy-start(bf16[1024,64]{1,0:T(8,128)(2,1)} %copy-done) | copy-start | bytes 393220
  125.5 38.9 %copy-start.2 = (f32[4]{0:T(128)S(1)}, f32[4]{0:T(128)}, u32[]{:S(2)}) copy-start(f32[4]{0:T(128)} %constant.140) | copy-start | bytes 52
Sparse Core Ops, SparseCore 0:
  16.0 75.6 all-gather.3

commit v2 on v1

v2 whole, which is shorter than its diff:
```python
import math

import jax
import jax.numpy as jnp
from jax import lax
from jax.sharding import Mesh, PartitionSpec as P


def swapped(value, axis, stride):
    mask = 2**stride
    pairs = [(source, source ^ mask) for source in range(lax.axis_size(axis))]
    return lax.ppermute(value, axis, pairs)


def squares_of(coords):
    return jnp.sum(jnp.square(coords.astype(jnp.float32)), axis=-1)


def raw_product(row_pts, row_sq, cols, dim):
    col_pts = cols[:, :dim]
    col_sketch = cols[:, dim:]
    col_sq = squares_of(col_pts)
    cross = lax.dot_general(
        row_pts, col_pts, (((1,), (1,)), ((), ())), preferred_element_type=jnp.float32
    )
    distance = row_sq[:, None] + col_sq[None, :] - 2.0 * cross
    kernel = jnp.exp((2.0 * dim - distance) * (2.0 / dim)).astype(jnp.bfloat16)
    return jnp.dot(kernel, col_sketch, preferred_element_type=jnp.float32)


def gram_of(product):
    return jnp.dot(
        product.T, product, precision=lax.Precision.HIGHEST, preferred_element_type=jnp.float32
    )


def per_device(points, sketch_matrix, leaf_order):
    dim = points.shape[1]
    located = jnp.take(points, leaf_order[0], axis=0)
    rows_n = located.shape[0]
    row_sq = squares_of(located)
    packed = jnp.concatenate([located, sketch_matrix], axis=1)
    leaf_bits = lax.axis_size("leaf").bit_length() - 1
    far_pieces = [swapped(packed, "pair", 0)]
    cluster = packed
    results = []
    grams = []
    for tier_num in range(leaf_bits):
        sib = swapped(cluster, "leaf", tier_num)
        far_pieces.append(swapped(sib, "pair", 0))
        product = raw_product(located, row_sq, sib, dim) / math.sqrt(sib.shape[0])
        results.append(product)
        local = gram_of(product)
        for bit_num in range(tier_num):
            local = local + swapped(local, "leaf", bit_num)
        grams.append(local)
        cluster = jnp.concatenate([cluster, sib])
    far_total = None
    far_rows = 0
    for piece in far_pieces:
        part = raw_product(located, row_sq, piece, dim)
        far_total = part if far_total is None else far_total + part
        far_rows += piece.shape[0]
    product = far_total / math.sqrt(far_rows)
    results.append(product)
    local = gram_of(product)
    for bit_num in range(leaf_bits):
        local = local + swapped(local, "leaf", bit_num)
    grams.append(local)
    stacked = jnp.stack(grams)
    divisors = jnp.asarray(
        [float((1 << tier_num) * rows_n) for tier_num in range(len(grams))], jnp.float32
    )
    stacked = stacked / divisors[:, None, None]
    return (jnp.concatenate(results, axis=1), stacked[None])


def solution(mesh):
    n_leaf = mesh.shape["leaf"]
    n_level = mesh.shape["level"]
    fine = Mesh(mesh.devices.reshape(n_leaf, n_level // 2, 2), ("leaf", "lvl", "pair"))
    axes = ("leaf", "lvl", "pair")
    in_specs = (P(axes, None), P(axes, None), P(axes, None))
    out_specs = (P(axes, None), P(axes, None, None, None))
    return jax.shard_map(
        per_device, mesh=fine, in_specs=in_specs, out_specs=out_specs, check_vma=False
    )
```

time: 172 us -> 117 us (0.68)
  the two profiles are of different devices: /device:TPU:6 before, /device:TPU:504 now
where the time goes in v2:
time: 117 us
  starting transfers between devices  38.9 us (33%)
  waiting for transfers between devices  33.9 us (29%)
  matrix products  28.3 us (24%)
  other arithmetic  7.83 us (7%)
  local copies, waits for them, and re-layouts  6.68 us (6%)
    ppermute x13, starting transfers between devices, swapped(): return lax.ppermute(value, axis, pairs)  38.9 us
    ppermute x13, waiting for transfers between devices, swapped(): return lax.ppermute(value, axis, pairs)  33.9 us
    dot_general x7, matrix products, raw_product(): return jnp.dot(kernel, col_sketch, preferred_element_type=jnp.float32)  26.8 us
    reduce_sum x8, other arithmetic, squares_of(): return jnp.sum(jnp.square(coords.astype(jnp.float32)), axis=-1)  4.13 us
    unnamed x9, local copies, waits for them, and re-layouts  3.47 us
    gather x1, local copies, waits for them, and re-layouts, per_device(): located = jnp.take(points, leaf_order[0], axis=0)  3.21 us
  transfers between devices with their start and end apart: 13, of which 6 were waited for; matrix products, arithmetic and copies ran while one was open for 30% of the time, Pallas kernels for 0%

profile of v2, /device:TPU:504, one launch (start us, length us, event | category | flops | bytes accessed | tf_op | source)
XLA Modules:
  0.0 116.5 jit_solution(6961208611978436972)
XLA Ops:
  0.6 1.1 copy.9
  1.7 0.7 compare_select_fusion
  2.4 0.7 compare_and_fusion
  3.1 1.1 copy.10
  4.2 3.2 %gather_fusion = bf16[1024,64]{1,0:T(8,128)(2,1)S(1)} fusion(bf16[1024,64]{1,0:T(8,128)(2,1)S(1)} %copy.9, s32[1024]{0:T(1024)S(1)} %broadcast_clamp_fusion), kind=kCustom, calls=%fused_computation | custom fusion | bytes 266240 | tf_op jit(solution)/shard_map/jit(_take)/gather | solution.py:39
  7.4 0.4 multiply_reduce_fusion.7
  7.8 0.1 pad_maximum_fusion.3
  7.9 3.4 %collective-permute-start = (bf16[1024,128]{1,0:T(8,128)(2,1)S(1)}, bf16[1024,128]{1,0:T(8,128)(2,1)S(1)}, u32[]{:S(2)}, u32[]{:S(2)}) collective-permute-start(bf16[1024,128]{1,0:T(8,128)(2,1)S(1)} %pad_maximum_fusion.3), channel_id=1, source_target_pairs={{0,64},{64,0},{128,192},{192,128},{256,320},{320,256},{384,448},{4... | collective-permute-start | bytes 786440 | tf_op jit(solution)/shard_map/ppermute | solution.py:12
  11.3 1.9 %collective-permute-start.3 = (bf16[1024,128]{1,0:T(8,128)(2,1)S(1)}, bf16[1024,128]{1,0:T(8,128)(2,1)S(1)}, u32[]{:S(2)}, u32[]{:S(2)}) collective-permute-start(bf16[1024,128]{1,0:T(8,128)(2,1)S(1)} %pad_maximum_fusion.3), channel_id=1, source_target_pairs={{0,1},{1,0},{2,3},{3,2},{4,5},{5,4},{6,7},{7,6},{8,9},{9,8},{10,11... | collective-permute-start | bytes 786440 | tf_op jit(solution)/shard_map/ppermute | solution.py:12
  13.3 4.6 %collective-permute-done = bf16[1024,128]{1,0:T(8,128)(2,1)S(1)} collective-permute-done((bf16[1024,128]{1,0:T(8,128)(2,1)S(1)}, bf16[1024,128]{1,0:T(8,128)(2,1)S(1)}, u32[]{:S(2)}, u32[]{:S(2)}) %collective-permute-start) | collective-permute-done | bytes 262176 | tf_op jit(solution)/shard_map/ppermute | solution.py:12
  17.9 0.1 pad_maximum_fusion.2
  18.0 4.9 %collective-permute-start.1 = (bf16[2048,128]{1,0:T(8,128)(2,1)S(1)}, bf16[2048,128]{1,0:T(8,128)(2,1)S(1)}, u32[]{:S(2)}, u32[]{:S(2)}) collective-permute-start(bf16[2048,128]{1,0:T(8,128)(2,1)S(1)} %pad_maximum_fusion.2), channel_id=1, source_target_pairs={{0,128},{64,192},{128,0},{192,64},{256,384},{320,448},{384,256},{4... | collective-permute-start | bytes 1572872 | tf_op jit(solution)/shard_map/ppermute | solution.py:12
  23.0 1.9 %collective-permute-start.4 = (bf16[1024,128]{1,0:T(8,128)(2,1)S(1)}, bf16[1024,128]{1,0:T(8,128)(2,1)S(1)}, u32[]{:S(2)}, u32[]{:S(2)}) collective-permute-start(bf16[1024,128]{1,0:T(8,128)(2,1)S(1)} %collective-permute-done), channel_id=1, source_target_pairs={{0,1},{1,0},{2,3},{3,2},{4,5},{5,4},{6,7},{7,6},{8,9},{9,8},{10,11... | collective-permute-start | bytes 786440 | tf_op jit(solution)/shard_map/ppermute | solution.py:12
  24.9 0.2 multiply_reduce_fusion.6
  25.1 1.7 %fusion.7 = f32[1024,64]{0,1:T(8,128)S(1)} fusion(bf16[1024,64]{1,0:T(8,128)(2,1)S(1)} %get-tuple-element.7, f32[1024]{0:T(1024)S(1)} %multiply_reduce_fusion.6, f32[1024]{0:T(1024)S(1)} %get-tuple-element.6, bf16[1024,128]{1,0:T(8,128)(2,1)S(1)} %collective-permute-done), kind=kOutput, calls=%fused_computation.17 | convolution fusion | flops 274792448 | bytes 1056768 | tf_op jit(solution)/shard_map/dot_general | solution.py:28
  26.8 0.2 multiply_reduce_fusion.5
  27.0 0.4 convolution_bitcast_fusion
  27.4 2.4 %fusion.5 = f32[1024,64]{0,1:T(8,128)} fusion(bf16[1024,64]{1,0:T(8,128)(2,1)S(1)} %get-tuple-element.7, f32[1024]{0:T(1024)S(1)} %multiply_reduce_fusion.5, f32[1024]{0:T(1024)S(1)} %get-tuple-element.6, bf16[1024,128]{1,0:T(8,128)(2,1)S(1)} %collective-permute-done.3), kind=kOutput, calls=%fused_computation.15 | convolution fusion | flops 274726912 | bytes 1056768 | tf_op jit(solution)/shard_map/dot_general | solution.py:28
  29.8 4.4 %collective-permute-done.1 = bf16[2048,128]{1,0:T(8,128)(2,1)S(1)} collective-permute-done((bf16[2048,128]{1,0:T(8,128)(2,1)S(1)}, bf16[2048,128]{1,0:T(8,128)(2,1)S(1)}, u32[]{:S(2)}, u32[]{:S(2)}) %collective-permute-start.1) | collective-permute-done | bytes 524320 | tf_op jit(solution)/shard_map/ppermute | solution.py:12
  34.2 1.1 pad_maximum_fusion
  35.3 3.1 %collective-permute-start.2 = (bf16[4096,128]{1,0:T(8,128)(2,1)}, bf16[4096,128]{1,0:T(8,128)(2,1)S(1)}, u32[]{:S(2)}, u32[]{:S(2)}) collective-permute-start(bf16[4096,128]{1,0:T(8,128)(2,1)} %pad_maximum_fusion), channel_id=1, source_target_pairs={{0,256},{64,320},{128,384},{192,448},{256,0},{320,64},{384,128},{4... | collective-permute-start | bytes 3145736 | tf_op jit(solution)/shard_map/ppermute | solution.py:12
  38.5 0.2 multiply_reduce_fusion.4
  38.7 1.9 %collective-permute-start.5 = (bf16[2048,128]{1,0:T(8,128)(2,1)S(1)}, bf16[2048,128]{1,0:T(8,128)(2,1)S(1)}, u32[]{:S(2)}, u32[]{:S(2)}) collective-permute-start(bf16[2048,128]{1,0:T(8,128)(2,1)S(1)} %collective-permute-done.1), channel_id=1, source_target_pairs={{0,1},{1,0},{2,3},{3,2},{4,5},{5,4},{6,7},{7,6},{8,9},{9,8},{10,11... | collective-permute-start | bytes 1572872 | tf_op jit(solution)/shard_map/ppermute | solution.py:12
  40.6 0.3 multiply_reduce_fusion.3
  41.0 3.1 %fusion.8 = f32[1024,64]{0,1:T(8,128)S(1)} fusion(bf16[1024,64]{1,0:T(8,128)(2,1)S(1)} %get-tuple-element.7, f32[2048]{0:T(1024)S(1)} %multiply_reduce_fusion.3, f32[1024]{0:T(1024)S(1)} %get-tuple-element.6, bf16[2048,128]{1,0:T(8,128)(2,1)S(1)} %collective-permute-done.1), kind=kOutput, calls=%fused_computation.18 | convolution fusion | flops 549519360 | bytes 1585152 | tf_op jit(solution)/shard_map/dot_general | solution.py:28
  44.1 0.4 fusion.56
  44.5 3.4 %collective-permute-start.7 = (f32[64,64]{1,0:T(8,128)S(1)}, f32[64,64]{1,0:T(8,128)S(1)}, u32[]{:S(2)}, u32[]{:S(2)}) collective-permute-start(f32[64,64]{1,0:T(8,128)S(1)} %fusion.56), channel_id=1, source_target_pairs={{0,64},{64,0},{128,192},{192,128},{256,320},{320,256},{384,448},{4... | collective-permute-start | bytes 49160 | tf_op jit(solution)/shard_map/ppermute | solution.py:12
  47.9 0.3 multiply_reduce_fusion.2
  48.3 13.8 %collective-permute-done.2 = bf16[4096,128]{1,0:T(8,128)(2,1)S(1)} collective-permute-done((bf16[4096,128]{1,0:T(8,128)(2,1)}, bf16[4096,128]{1,0:T(8,128)(2,1)S(1)}, u32[]{:S(2)}, u32[]{:S(2)}) %collective-permute-start.2) | collective-permute-done | bytes 1048608 | tf_op jit(solution)/shard_map/ppermute | solution.py:12
  62.1 2.1 %collective-permute-start.6 = (bf16[4096,128]{1,0:T(8,128)(2,1)S(1)}, bf16[4096,128]{1,0:T(8,128)(2,1)}, u32[]{:S(2)}, u32[]{:S(2)}) collective-permute-start(bf16[4096,128]{1,0:T(8,128)(2,1)S(1)} %collective-permute-done.2), channel_id=1, source_target_pairs={{0,1},{1,0},{2,3},{3,2},{4,5},{5,4},{6,7},{7,6},{8,9},{9,8},{10,11... | collective-permute-start | bytes 3145736 | tf_op jit(solution)/shard_map/ppermute | solution.py:12
  64.2 0.6 multiply_reduce_fusion.1
  64.8 6.2 %fusion.9 = f32[1024,64]{0,1:T(8,128)S(1)} fusion(bf16[1024,64]{1,0:T(8,128)(2,1)S(1)} %get-tuple-element.7, f32[4096]{0:T(1024)S(1)} %multiply_reduce_fusion.1, f32[1024]{0:T(1024)S(1)} %get-tuple-element.6, bf16[4096,128]{1,0:T(8,128)(2,1)S(1)} %collective-permute-done.2), kind=kOutput, calls=%fused_computation.19 | convolution fusion | flops 1098973184 | bytes 2641920 | tf_op jit(solution)/shard_map/dot_general | solution.py:28
  71.1 0.4 fusion.57
  71.4 3.4 %collective-permute-start.8 = (f32[64,64]{1,0:T(8,128)S(1)}, f32[64,64]{1,0:T(8,128)S(1)}, u32[]{:S(2)}, u32[]{:S(2)}) collective-permute-start(f32[64,64]{1,0:T(8,128)S(1)} %fusion.57), channel_id=1, source_target_pairs={{0,64},{64,0},{128,192},{192,128},{256,320},{320,256},{384,448},{4... | collective-permute-start | bytes 49160 | tf_op jit(solution)/shard_map/ppermute | solution.py:12
  74.9 3.8 %fusion.3 = f32[1024,64]{0,1:T(8,128)} fusion(bf16[1024,64]{1,0:T(8,128)(2,1)S(1)} %get-tuple-element.7, f32[2048]{0:T(1024)S(1)} %multiply_reduce_fusion.2, f32[1024]{0:T(1024)S(1)} %get-tuple-element.6, bf16[2048,128]{1,0:T(8,128)(2,1)S(1)} %collective-permute-done.5), kind=kOutput, calls=%fused_computation.13 | convolution fusion | flops 549453824 | bytes 1585152 | tf_op jit(solution)/shard_map/dot_general | solution.py:28
  78.7 4.9 %collective-permute-start.9 = (f32[64,64]{1,0:T(8,128)S(1)}, f32[64,64]{1,0:T(8,128)S(1)}, u32[]{:S(2)}, u32[]{:S(2)}) collective-permute-start(f32[64,64]{1,0:T(8,128)S(1)} %add.156), channel_id=1, source_target_pairs={{0,128},{64,192},{128,0},{192,64},{256,384},{320,448},{384,256},{4... | collective-permute-start | bytes 49160 | tf_op jit(solution)/shard_map/ppermute | solution.py:12
  83.6 1.8 %multiply_reduce_fusion = f32[4096]{0:T(1024)S(1)} fusion(bf16[4096,128]{1,0:T(8,128)(2,1)} %collective-permute-done.6), kind=kLoop, calls=%fused_computation.8 | loop fusion | flops 782336 | bytes 540672 | tf_op jit(solution)/shard_map/reduce_sum | solution.py:16
  85.5 7.8 %fusion.1 = f32[1024,64]{0,1:T(8,128)S(1)} fusion(bf16[1024,64]{1,0:T(8,128)(2,1)S(1)} %get-tuple-element.7, f32[4096]{0:T(1024)S(1)} %multiply_reduce_fusion, f32[1024]{0:T(1024)S(1)} %get-tuple-element.6, bf16[4096,128]{1,0:T(8,128)(2,1)} %collective-permute-done.6), kind=kOutput, calls=%fused_computation.11 | convolution fusion | flops 1098907648 | bytes 2510848 | tf_op jit(solution)/shard_map/dot_general | solution.py:28
  93.3 1.7 %fusion.13 = f32[1024,64]{0,1:T(8,128)S(1)} fusion(f32[1024,64]{0,1:T(8,128)S(1)} %fusion.1, f32[1024,64]{0,1:T(8,128)S(1)} %copy-done.2, f32[1024,64]{0,1:T(8,128)S(1)} %copy-done.1, bf16[1024,64]{1,0:T(8,128)(2,1)S(1)} %get-tuple-element.7, f32[1024]{0:T(1024)S(1)} %multiply_reduce_fusion.4, f32[1024]{0:T(1024)S(1)} %get-tuple-element.6, ...), kind=kOutput, calls=%fused_computation.23 | convolution fusion | flops 274989056 | bytes 1843200 | tf_op jit(solution)/shard_map/dot_general | solution.py:28
  95.0 0.4 fusion.58
  95.4 2.1 %collective-permute-start.10 = (f32[64,64]{1,0:T(8,128)S(1)}, f32[64,64]{1,0:T(8,128)S(1)}, u32[]{:S(2)}, u32[]{:S(2)}) collective-permute-start(f32[64,64]{1,0:T(8,128)S(1)} %fusion.58), channel_id=1, source_target_pairs={{0,64},{64,0},{128,192},{192,128},{256,320},{320,256},{384,448},{4... | collective-permute-start | bytes 49160 | tf_op jit(solution)/shard_map/ppermute | solution.py:12
  97.5 3.7 %collective-permute-done.10 = f32[64,64]{1,0:T(8,128)S(1)} collective-permute-done((f32[64,64]{1,0:T(8,128)S(1)}, f32[64,64]{1,0:T(8,128)S(1)}, u32[]{:S(2)}, u32[]{:S(2)}) %collective-permute-start.10) | collective-permute-done | bytes 16416 | tf_op jit(solution)/shard_map/ppermute | solution.py:12
  101.2 2.7 %collective-permute-start.11 = (f32[64,64]{1,0:T(8,128)S(1)}, f32[64,64]{1,0:T(8,128)S(1)}, u32[]{:S(2)}, u32[]{:S(2)}) collective-permute-start(f32[64,64]{1,0:T(8,128)S(1)} %add.158), channel_id=1, source_target_pairs={{0,128},{64,192},{128,0},{192,64},{256,384},{320,448},{384,256},{4... | collective-permute-start | bytes 49160 | tf_op jit(solution)/shard_map/ppermute | solution.py:12
  103.9 4.6 %collective-permute-done.11 = f32[64,64]{1,0:T(8,128)S(1)} collective-permute-done((f32[64,64]{1,0:T(8,128)S(1)}, f32[64,64]{1,0:T(8,128)S(1)}, u32[]{:S(2)}, u32[]{:S(2)}) %collective-permute-start.11) | collective-permute-done | bytes 16416 | tf_op jit(solution)/shard_map/ppermute | solution.py:12
  108.5 3.1 %collective-permute-start.12 = (f32[64,64]{1,0:T(8,128)S(1)}, f32[64,64]{1,0:T(8,128)S(1)}, u32[]{:S(2)}, u32[]{:S(2)}) collective-permute-start(f32[64,64]{1,0:T(8,128)S(1)} %add.159), channel_id=1, source_target_pairs={{0,256},{64,320},{128,384},{192,448},{256,0},{320,64},{384,128},{4... | collective-permute-start | bytes 49160 | tf_op jit(solution)/shard_map/ppermute | solution.py:12
  111.8 1.3 %copy.11 = f32[1024,256]{1,0:T(8,128)} copy(f32[1024,256]{0,1:T(8,128)S(1)} %pad_maximum_fusion.1) | data formatting | bytes 2097152
  113.1 2.7 %collective-permute-done.12 = f32[64,64]{1,0:T(8,128)S(1)} collective-permute-done((f32[64,64]{1,0:T(8,128)S(1)}, f32[64,64]{1,0:T(8,128)S(1)}, u32[]{:S(2)}, u32[]{:S(2)}) %collective-permute-start.12) | collective-permute-done | bytes 16416 | tf_op jit(solution)/shard_map/ppermute | solution.py:12
  115.8 0.7 maximum_multiply_fusion
  (21 shorter events, 0.2 us)
Async XLA Ops:
  7.9 9.9 %collective-permute-start = (bf16[1024,128]{1,0:T(8,128)(2,1)S(1)}, bf16[1024,128]{1,0:T(8,128)(2,1)S(1)}, u32[]{:S(2)}, u32[]{:S(2)}) collective-permute-start(bf16[1024,128]{1,0:T(8,128)(2,1)S(1)} %pad_maximum_fusion.3), channel_id=1, source_target_pairs={{0,64},{64,0},{128,192},{192,128},{256,320},{320,256},{384,448},{4... | collective-permute-start | bytes 786440 | tf_op jit(solution)/shard_map/ppermute | solution.py:12
  11.3 15.5 %collective-permute-start.3 = (bf16[1024,128]{1,0:T(8,128)(2,1)S(1)}, bf16[1024,128]{1,0:T(8,128)(2,1)S(1)}, u32[]{:S(2)}, u32[]{:S(2)}) collective-permute-start(bf16[1024,128]{1,0:T(8,128)(2,1)S(1)} %pad_maximum_fusion.3), channel_id=1, source_target_pairs={{0,1},{1,0},{2,3},{3,2},{4,5},{5,4},{6,7},{7,6},{8,9},{9,8},{10,11... | collective-permute-start | bytes 786440 | tf_op jit(solution)/shard_map/ppermute | solution.py:12
  18.0 16.2 %collective-permute-start.1 = (bf16[2048,128]{1,0:T(8,128)(2,1)S(1)}, bf16[2048,128]{1,0:T(8,128)(2,1)S(1)}, u32[]{:S(2)}, u32[]{:S(2)}) collective-permute-start(bf16[2048,128]{1,0:T(8,128)(2,1)S(1)} %pad_maximum_fusion.2), channel_id=1, source_target_pairs={{0,128},{64,192},{128,0},{192,64},{256,384},{320,448},{384,256},{4... | collective-permute-start | bytes 1572872 | tf_op jit(solution)/shard_map/ppermute | solution.py:12
  23.0 15.5 %collective-permute-start.4 = (bf16[1024,128]{1,0:T(8,128)(2,1)S(1)}, bf16[1024,128]{1,0:T(8,128)(2,1)S(1)}, u32[]{:S(2)}, u32[]{:S(2)}) collective-permute-start(bf16[1024,128]{1,0:T(8,128)(2,1)S(1)} %collective-permute-done), channel_id=1, source_target_pairs={{0,1},{1,0},{2,3},{3,2},{4,5},{5,4},{6,7},{7,6},{8,9},{9,8},{10,11... | collective-permute-start | bytes 786440 | tf_op jit(solution)/shard_map/ppermute | solution.py:12
  35.3 26.8 %collective-permute-start.2 = (bf16[4096,128]{1,0:T(8,128)(2,1)}, bf16[4096,128]{1,0:T(8,128)(2,1)S(1)}, u32[]{:S(2)}, u32[]{:S(2)}) collective-permute-start(bf16[4096,128]{1,0:T(8,128)(2,1)} %pad_maximum_fusion), channel_id=1, source_target_pairs={{0,256},{64,320},{128,384},{192,448},{256,0},{320,64},{384,128},{4... | collective-permute-start | bytes 3145736 | tf_op jit(solution)/shard_map/ppermute | solution.py:12
  38.7 9.2 %collective-permute-start.5 = (bf16[2048,128]{1,0:T(8,128)(2,1)S(1)}, bf16[2048,128]{1,0:T(8,128)(2,1)S(1)}, u32[]{:S(2)}, u32[]{:S(2)}) collective-permute-start(bf16[2048,128]{1,0:T(8,128)(2,1)S(1)} %collective-permute-done.1), channel_id=1, source_target_pairs={{0,1},{1,0},{2,3},{3,2},{4,5},{5,4},{6,7},{7,6},{8,9},{9,8},{10,11... | collective-permute-start | bytes 1572872 | tf_op jit(solution)/shard_map/ppermute | solution.py:12
  44.5 53.0 %collective-permute-start.7 = (f32[64,64]{1,0:T(8,128)S(1)}, f32[64,64]{1,0:T(8,128)S(1)}, u32[]{:S(2)}, u32[]{:S(2)}) collective-permute-start(f32[64,64]{1,0:T(8,128)S(1)} %fusion.56), channel_id=1, source_target_pairs={{0,64},{64,0},{128,192},{192,128},{256,320},{320,256},{384,448},{4... | collective-permute-start | bytes 49160 | tf_op jit(solution)/shard_map/ppermute | solution.py:12
  62.1 21.5 %collective-permute-start.6 = (bf16[4096,128]{1,0:T(8,128)(2,1)S(1)}, bf16[4096,128]{1,0:T(8,128)(2,1)}, u32[]{:S(2)}, u32[]{:S(2)}) collective-permute-start(bf16[4096,128]{1,0:T(8,128)(2,1)S(1)} %collective-permute-done.2), channel_id=1, source_target_pairs={{0,1},{1,0},{2,3},{3,2},{4,5},{5,4},{6,7},{7,6},{8,9},{9,8},{10,11... | collective-permute-start | bytes 3145736 | tf_op jit(solution)/shard_map/ppermute | solution.py:12
  71.4 7.3 %collective-permute-start.8 = (f32[64,64]{1,0:T(8,128)S(1)}, f32[64,64]{1,0:T(8,128)S(1)}, u32[]{:S(2)}, u32[]{:S(2)}) collective-permute-start(f32[64,64]{1,0:T(8,128)S(1)} %fusion.57), channel_id=1, source_target_pairs={{0,64},{64,0},{128,192},{192,128},{256,320},{320,256},{384,448},{4... | collective-permute-start | bytes 49160 | tf_op jit(solution)/shard_map/ppermute | solution.py:12
  78.7 25.2 %collective-permute-start.9 = (f32[64,64]{1,0:T(8,128)S(1)}, f32[64,64]{1,0:T(8,128)S(1)}, u32[]{:S(2)}, u32[]{:S(2)}) collective-permute-start(f32[64,64]{1,0:T(8,128)S(1)} %add.156), channel_id=1, source_target_pairs={{0,128},{64,192},{128,0},{192,64},{256,384},{320,448},{384,256},{4... | collective-permute-start | bytes 49160 | tf_op jit(solution)/shard_map/ppermute | solution.py:12
  85.5 7.9 %copy-start.1 = (f32[1024,64]{0,1:T(8,128)S(1)}, f32[1024,64]{0,1:T(8,128)}, u32[]{:S(2)}) copy-start(f32[1024,64]{0,1:T(8,128)} %fusion.5) | copy-start | bytes 786436
  85.5 7.9 %copy-start.2 = (f32[1024,64]{0,1:T(8,128)S(1)}, f32[1024,64]{0,1:T(8,128)}, u32[]{:S(2)}) copy-start(f32[1024,64]{0,1:T(8,128)} %fusion.3) | copy-start | bytes 786436
  95.4 5.8 %collective-permute-start.10 = (f32[64,64]{1,0:T(8,128)S(1)}, f32[64,64]{1,0:T(8,128)S(1)}, u32[]{:S(2)}, u32[]{:S(2)}) collective-permute-start(f32[64,64]{1,0:T(8,128)S(1)} %fusion.58), channel_id=1, source_target_pairs={{0,64},{64,0},{128,192},{192,128},{256,320},{320,256},{384,448},{4... | collective-permute-start | bytes 49160 | tf_op jit(solution)/shard_map/ppermute | solution.py:12
  101.2 7.3 %collective-permute-start.11 = (f32[64,64]{1,0:T(8,128)S(1)}, f32[64,64]{1,0:T(8,128)S(1)}, u32[]{:S(2)}, u32[]{:S(2)}) collective-permute-start(f32[64,64]{1,0:T(8,128)S(1)} %add.158), channel_id=1, source_target_pairs={{0,128},{64,192},{128,0},{192,64},{256,384},{320,448},{384,256},{4... | collective-permute-start | bytes 49160 | tf_op jit(solution)/shard_map/ppermute | solution.py:12
  108.5 7.3 %collective-permute-start.12 = (f32[64,64]{1,0:T(8,128)S(1)}, f32[64,64]{1,0:T(8,128)S(1)}, u32[]{:S(2)}, u32[]{:S(2)}) collective-permute-start(f32[64,64]{1,0:T(8,128)S(1)} %add.159), channel_id=1, source_target_pairs={{0,256},{64,320},{128,384},{192,448},{256,0},{320,64},{384,128},{4... | collective-permute-start | bytes 49160 | tf_op jit(solution)/shard_map/ppermute | solution.py:12
  111.7 4.1 %copy-start = (f32[4]{0:T(128)S(1)}, f32[4]{0:T(128)}, u32[]{:S(2)}) copy-start(f32[4]{0:T(128)} %constant.45) | copy-start | bytes 52

commit v3 on v2

--- a/solution.py
+++ b/solution.py
@@ -36,24 +36,27 @@
 
 def per_device(points, sketch_matrix, leaf_order):
     dim = points.shape[1]
-    located = jnp.take(points, leaf_order[0], axis=0)
-    rows_n = located.shape[0]
+    rows_n = points.shape[0]
+    picks = leaf_order[0][:, None] == jnp.arange(rows_n, dtype=leaf_order.dtype)[None, :]
+    located = jnp.dot(
+        picks.astype(points.dtype), points, preferred_element_type=jnp.float32
+    ).astype(points.dtype)
     row_sq = squares_of(located)
     packed = jnp.concatenate([located, sketch_matrix], axis=1)
     leaf_bits = lax.axis_size("leaf").bit_length() - 1
-    far_pieces = [swapped(packed, "pair", 0)]
+    far_pieces = []
     cluster = packed
     results = []
     grams = []
     for tier_num in range(leaf_bits):
         sib = swapped(cluster, "leaf", tier_num)
-        far_pieces.append(swapped(sib, "pair", 0))
+        if tier_num == 0:
+            far_pieces.append(swapped(jnp.concatenate([packed, sib]), "pair", 0))
+        else:
+            far_pieces.append(swapped(sib, "pair", 0))
         product = raw_product(located, row_sq, sib, dim) / math.sqrt(sib.shape[0])
         results.append(product)
-        local = gram_of(product)
-        for bit_num in range(tier_num):
-            local = local + swapped(local, "leaf", bit_num)
-        grams.append(local)
+        grams.append(gram_of(product))
         cluster = jnp.concatenate([cluster, sib])
     far_total = None
     far_rows = 0
@@ -63,11 +66,22 @@
         far_rows += piece.shape[0]
     product = far_total / math.sqrt(far_rows)
     results.append(product)
-    local = gram_of(product)
-    for bit_num in range(leaf_bits):
-        local = local + swapped(local, "leaf", bit_num)
-    grams.append(local)
-    stacked = jnp.stack(grams)
+    grams.append(gram_of(product))
+    n_tiers = len(grams)
+    done = [grams[0]]
+    for tier_num in range(1, n_tiers - 1):
+        if tier_num == n_tiers - 2:
+            break
+        local = grams[tier_num]
+        for bit_num in range(tier_num):
+            local = local + swapped(local, "leaf", bit_num)
+        done.append(local)
+    tail = jnp.stack(grams[n_tiers - 2:])
+    for bit_num in range(n_tiers - 2):
+        tail = tail + swapped(tail, "leaf", bit_num)
+    last = tail[1] + swapped(tail[1], "leaf", n_tiers - 2)
+    done.extend([tail[0], last])
+    stacked = jnp.stack(done)
     divisors = jnp.asarray(
         [float((1 << tier_num) * rows_n) for tier_num in range(len(grams))], jnp.float32
     )

time: 117 us -> 101 us (0.86)
  starting transfers between devices: 38.9 us -> 31.3 us
  local copies, waits for them, and re-layouts: 6.68 us -> 2.22 us
  other arithmetic: 7.83 us -> 4.48 us
  waiting for transfers between devices: 33.9 us -> 30.8 us
  matrix products: 28.3 us -> 30.7 us
    ppermute x13 -> x10, starting transfers between devices: 38.9 us -> 31.3 us  [swapped(): return lax.ppermute(value, axis, pairs)]
    gather x1 -> x0, local copies, waits for them, and re-layouts: 3.21 us -> none  [per_device(): located = jnp.take(points, leaf_order[0], axis=0)]
    ppermute x13 -> x10, waiting for transfers between devices: 33.9 us -> 30.8 us  [swapped(): return lax.ppermute(value, axis, pairs)]
    dot_general x0 -> x1, matrix products: none -> 1.71 us  [per_device(): jnp.dot(picks.astype(points.dtype), points, preferred_element_type=jnp.fl...]
    unnamed x9, local copies, waits for them, and re-layouts: 3.47 us -> 2.22 us
    dot_general x7 -> x6, matrix products: 26.8 us -> 27.5 us  [raw_product(): return jnp.dot(kernel, col_sketch, preferred_element_type=jnp.float32)]
    reduce_sum x8 -> x6, other arithmetic: 4.13 us -> 3.47 us  [squares_of(): return jnp.sum(jnp.square(coords.astype(jnp.float32)), axis=-1)]
  transfers between devices with their start and end apart: 13 -> 10, of which waited for: 6 -> 6; matrix products, arithmetic and copies ran while one was open for 30% -> 23% of each run, Pallas kernels for 0% -> 0%
where the time goes in v3:
time: 101 us; the launch traced here: 100 us
  starting transfers between devices  31.3 us (31%)
  waiting for transfers between devices  30.8 us (30%)
  matrix products  30.7 us (30%)
  other arithmetic  4.48 us (4%)
  local copies, waits for them, and re-layouts  2.22 us (2%)
    ppermute x10, starting transfers between devices, swapped(): return lax.ppermute(value, axis, pairs)  31.3 us
    ppermute x10, waiting for transfers between devices, swapped(): return lax.ppermute(value, axis, pairs)  30.8 us
    dot_general x6, matrix products, raw_product(): return jnp.dot(kernel, col_sketch, preferred_element_type=jnp.float32)  27.5 us
    reduce_sum x6, other arithmetic, squares_of(): return jnp.sum(jnp.square(coords.astype(jnp.float32)), axis=-1)  3.47 us
    unnamed x9, local copies, waits for them, and re-layouts  2.22 us
  transfers between devices with their start and end apart: 10, of which 6 were waited for; matrix products, arithmetic and copies ran while one was open for 23% of the time, Pallas kernels for 0%

profile of v3, /device:TPU:504, one launch (start us, length us, event | category | flops | bytes accessed | tf_op | source)
XLA Modules:
  0.0 100.4 jit_solution(16220966406227082943)
XLA Ops:
  0.6 0.0 copy-start
  0.6 0.0 copy-start.1
  0.7 0.9 copy-done
  1.5 1.7 %multiply_reduce_fusion.6 = (f32[1024]{0:T(1024)S(1)}, bf16[1024,64]{0,1:T(8,128)(2,1)S(1)}) fusion(bf16[1024,64]{0,1:T(8,128)(2,1)S(1)} %copy-done, s32[1024]{0:T(1024)} %bitcast.32), kind=kOutput, calls=%fused_computation.42 | convolution fusion | flops 135527424 | bytes 270336 | tf_op jit(solution)/shard_map/dot_general | solution.py:41
  3.3 0.0 copy-done.1
  3.3 3.4 %collective-permute-start = (bf16[1024,128]{0,1:T(8,128)(2,1)S(1)}, bf16[1024,128]{0,1:T(8,128)(2,1)S(1)}, u32[]{:S(2)}, u32[]{:S(2)}) collective-permute-start(bf16[1024,128]{0,1:T(8,128)(2,1)S(1)} %pad_maximum_fusion.3), channel_id=1, source_target_pairs={{0,64},{64,0},{128,192},{192,128},{256,320},{320,256},{384,448},{4... | collective-permute-start | bytes 786440 | tf_op jit(solution)/shard_map/ppermute | solution.py:12
  6.7 6.5 %collective-permute-done = bf16[1024,128]{0,1:T(8,128)(2,1)S(1)} collective-permute-done((bf16[1024,128]{0,1:T(8,128)(2,1)S(1)}, bf16[1024,128]{0,1:T(8,128)(2,1)S(1)}, u32[]{:S(2)}, u32[]{:S(2)}) %collective-permute-start) | collective-permute-done | bytes 262176 | tf_op jit(solution)/shard_map/ppermute | solution.py:12
  13.3 4.9 %collective-permute-start.1 = (bf16[2048,128]{0,1:T(8,128)(2,1)S(1)}, bf16[2048,128]{0,1:T(8,128)(2,1)S(1)}, u32[]{:S(2)}, u32[]{:S(2)}) collective-permute-start(bf16[2048,128]{0,1:T(8,128)(2,1)S(1)} %pad_maximum_fusion.2), channel_id=1, source_target_pairs={{0,128},{64,192},{128,0},{192,64},{256,384},{320,448},{384,256},{4... | collective-permute-start | bytes 1572872 | tf_op jit(solution)/shard_map/ppermute | solution.py:12
  18.2 1.9 %collective-permute-start.3 = (bf16[2048,128]{0,1:T(8,128)(2,1)S(1)}, bf16[2048,128]{0,1:T(8,128)(2,1)}, u32[]{:S(2)}, u32[]{:S(2)}) collective-permute-start(bf16[2048,128]{0,1:T(8,128)(2,1)S(1)} %pad_maximum_fusion.2), channel_id=1, source_target_pairs={{0,1},{1,0},{2,3},{3,2},{4,5},{5,4},{6,7},{7,6},{8,9},{9,8},{10,11... | collective-permute-start | bytes 1572872 | tf_op jit(solution)/shard_map/ppermute | solution.py:12
  20.2 1.7 %fusion.8 = f32[1024,64]{0,1:T(8,128)S(1)} fusion(bf16[1024,64]{0,1:T(8,128)(2,1)S(1)} %get-tuple-element.7, f32[1024]{0:T(1024)S(1)} %multiply_reduce_fusion.5, f32[1024]{0:T(1024)S(1)} %get-tuple-element.6, bf16[1024,128]{0,1:T(8,128)(2,1)S(1)} %collective-permute-done), kind=kOutput, calls=%fused_computation.15 | convolution fusion | flops 274792448 | bytes 663552 | tf_op jit(solution)/shard_map/dot_general | solution.py:28
  21.9 0.4 convolution_bitcast_fusion.2
  22.2 7.2 %collective-permute-done.1 = bf16[2048,128]{0,1:T(8,128)(2,1)S(1)} collective-permute-done((bf16[2048,128]{0,1:T(8,128)(2,1)S(1)}, bf16[2048,128]{0,1:T(8,128)(2,1)S(1)}, u32[]{:S(2)}, u32[]{:S(2)}) %collective-permute-start.1) | collective-permute-done | bytes 524320 | tf_op jit(solution)/shard_map/ppermute | solution.py:12
  29.5 0.1 pad_maximum_fusion
  29.6 3.1 %collective-permute-start.2 = (bf16[4096,128]{0,1:T(8,128)(2,1)S(1)}, bf16[4096,128]{0,1:T(8,128)(2,1)}, u32[]{:S(2)}, u32[]{:S(2)}) collective-permute-start(bf16[4096,128]{0,1:T(8,128)(2,1)S(1)} %pad_maximum_fusion), channel_id=1, source_target_pairs={{0,256},{64,320},{128,384},{192,448},{256,0},{320,64},{384,128},{4... | collective-permute-start | bytes 3145736 | tf_op jit(solution)/shard_map/ppermute | solution.py:12
  32.7 1.9 %collective-permute-start.4 = (bf16[2048,128]{0,1:T(8,128)(2,1)S(1)}, bf16[2048,128]{0,1:T(8,128)(2,1)}, u32[]{:S(2)}, u32[]{:S(2)}) collective-permute-start(bf16[2048,128]{0,1:T(8,128)(2,1)S(1)} %collective-permute-done.1), channel_id=1, source_target_pairs={{0,1},{1,0},{2,3},{3,2},{4,5},{5,4},{6,7},{7,6},{8,9},{9,8},{10,11... | collective-permute-start | bytes 1572872 | tf_op jit(solution)/shard_map/ppermute | solution.py:12
  34.6 0.0 collective-permute-done.3
  34.7 1.0 %multiply_reduce_fusion.3 = f32[2048]{0:T(1024)S(1)} fusion(bf16[2048,128]{0,1:T(8,128)(2,1)} %collective-permute-done.3), kind=kLoop, calls=%fused_computation.33 | loop fusion | flops 391168 | bytes 270336 | tf_op jit(solution)/shard_map/reduce_sum | solution.py:16
  35.7 4.9 %fusion.5 = f32[1024,64]{0,1:T(8,128)} fusion(bf16[1024,64]{0,1:T(8,128)(2,1)S(1)} %get-tuple-element.7, f32[2048]{0:T(1024)S(1)} %multiply_reduce_fusion.3, f32[1024]{0:T(1024)S(1)} %get-tuple-element.6, bf16[2048,128]{0,1:T(8,128)(2,1)} %collective-permute-done.3), kind=kOutput, calls=%fused_computation.12 | convolution fusion | flops 549453824 | bytes 929792 | tf_op jit(solution)/shard_map/dot_general | solution.py:28
  40.6 0.1 multiply_reduce_fusion.4
  40.6 3.2 %fusion.9 = f32[1024,64]{0,1:T(8,128)S(1)} fusion(bf16[1024,64]{0,1:T(8,128)(2,1)S(1)} %get-tuple-element.7, f32[2048]{0:T(1024)S(1)} %multiply_reduce_fusion.4, f32[1024]{0:T(1024)S(1)} %get-tuple-element.6, bf16[2048,128]{0,1:T(8,128)(2,1)S(1)} %collective-permute-done.1), kind=kOutput, calls=%fused_computation.16 | convolution fusion | flops 549519360 | bytes 929792 | tf_op jit(solution)/shard_map/dot_general | solution.py:28
  43.8 0.0 collective-permute-done.4
  43.8 1.0 %multiply_reduce_fusion.2 = f32[2048]{0:T(1024)S(1)} fusion(bf16[2048,128]{0,1:T(8,128)(2,1)} %collective-permute-done.4), kind=kLoop, calls=%fused_computation.32 | loop fusion | flops 391168 | bytes 270336 | tf_op jit(solution)/shard_map/reduce_sum | solution.py:16
  44.8 11.4 %collective-permute-done.2 = bf16[4096,128]{0,1:T(8,128)(2,1)} collective-permute-done((bf16[4096,128]{0,1:T(8,128)(2,1)S(1)}, bf16[4096,128]{0,1:T(8,128)(2,1)}, u32[]{:S(2)}, u32[]{:S(2)}) %collective-permute-start.2) | collective-permute-done | bytes 1048608 | tf_op jit(solution)/shard_map/ppermute | solution.py:12
  56.3 2.1 %collective-permute-start.5 = (bf16[4096,128]{0,1:T(8,128)(2,1)}, bf16[4096,128]{0,1:T(8,128)(2,1)S(1)}, u32[]{:S(2)}, u32[]{:S(2)}) collective-permute-start(bf16[4096,128]{0,1:T(8,128)(2,1)} %collective-permute-done.2), channel_id=1, source_target_pairs={{0,1},{1,0},{2,3},{3,2},{4,5},{5,4},{6,7},{7,6},{8,9},{9,8},{10,11... | collective-permute-start | bytes 3145736 | tf_op jit(solution)/shard_map/ppermute | solution.py:12
  58.4 1.2 %multiply_reduce_fusion.1 = f32[4096]{0:T(1024)S(1)} fusion(bf16[4096,128]{0,1:T(8,128)(2,1)} %collective-permute-done.2), kind=kLoop, calls=%fused_computation.28 | loop fusion | flops 782336 | bytes 540672 | tf_op jit(solution)/shard_map/reduce_sum | solution.py:16
  59.5 7.3 %fusion.10 = f32[1024,64]{0,1:T(8,128)S(1)} fusion(bf16[1024,64]{0,1:T(8,128)(2,1)S(1)} %get-tuple-element.7, f32[4096]{0:T(1024)S(1)} %multiply_reduce_fusion.1, f32[1024]{0:T(1024)S(1)} %get-tuple-element.6, bf16[4096,128]{0,1:T(8,128)(2,1)} %collective-permute-done.2), kind=kOutput, calls=%fused_computation.17 | convolution fusion | flops 1098973184 | bytes 1462272 | tf_op jit(solution)/shard_map/dot_general | solution.py:28
  66.8 0.4 convolution_bitcast_fusion.1
  67.2 0.0 collective-permute-done.5
  67.2 0.1 multiply_reduce_fusion
  67.3 0.0 copy-start.3
  67.3 6.1 %fusion.3 = f32[1024,64]{0,1:T(8,128)S(1)} fusion(bf16[1024,64]{0,1:T(8,128)(2,1)S(1)} %get-tuple-element.7, f32[4096]{0:T(1024)S(1)} %multiply_reduce_fusion, f32[1024]{0:T(1024)S(1)} %get-tuple-element.6, bf16[4096,128]{0,1:T(8,128)(2,1)S(1)} %collective-permute-done.5), kind=kOutput, calls=%fused_computation.10 | convolution fusion | flops 1098907648 | bytes 1462272 | tf_op jit(solution)/shard_map/dot_general | solution.py:28
  73.4 0.0 copy-done.3
  73.4 4.4 %fusion.13 = f32[1024,64]{0,1:T(8,128)S(1)} fusion(f32[1024,64]{0,1:T(8,128)S(1)} %fusion.3, f32[1024,64]{0,1:T(8,128)S(1)} %copy-done.3, bf16[1024,64]{0,1:T(8,128)(2,1)S(1)} %get-tuple-element.7, f32[2048]{0:T(1024)S(1)} %multiply_reduce_fusion.2, f32[1024]{0:T(1024)S(1)} %get-tuple-element.6, bf16[2048,128]{0,1:T(8,128)(2,1)} %collective-permute-done.4), kind=kOutput, calls=%fused_computation.20 | convolution fusion | flops 549650432 | bytes 1454080 | tf_op jit(solution)/shard_map/dot_general | solution.py:28
  77.9 0.4 convolution_bitcast_fusion
  78.2 3.4 %collective-permute-start.7 = (f32[2,64,64]{2,1,0:T(8,128)S(1)}, f32[2,64,64]{2,1,0:T(8,128)S(1)}, u32[]{:S(2)}, u32[]{:S(2)}) collective-permute-start(f32[2,64,64]{2,1,0:T(8,128)S(1)} %pad_maximum_fusion.4), channel_id=1, source_target_pairs={{0,64},{64,0},{128,192},{192,128},{256,320},{320,256},{384,448},{4... | collective-permute-start | bytes 98312 | tf_op jit(solution)/shard_map/ppermute | solution.py:12
  81.7 0.4 fusion.52
  82.0 2.4 %collective-permute-start.6 = (f32[64,64]{1,0:T(8,128)S(1)}, f32[64,64]{1,0:T(8,128)S(1)}, u32[]{:S(2)}, u32[]{:S(2)}) collective-permute-start(f32[64,64]{1,0:T(8,128)S(1)} %fusion.52), channel_id=1, source_target_pairs={{0,64},{64,0},{128,192},{192,128},{256,320},{320,256},{384,448},{4... | collective-permute-start | bytes 49160 | tf_op jit(solution)/shard_map/ppermute | solution.py:12
  84.5 0.2 collective-permute-done.7
  84.7 4.9 %collective-permute-start.8 = (f32[2,64,64]{2,1,0:T(8,128)S(1)}, f32[2,64,64]{2,1,0:T(8,128)S(1)}, u32[]{:S(2)}, u32[]{:S(2)}) collective-permute-start(f32[2,64,64]{2,1,0:T(8,128)S(1)} %fusion.51), channel_id=1, source_target_pairs={{0,128},{64,192},{128,0},{192,64},{256,384},{320,448},{384,256},{4... | collective-permute-start | bytes 98312 | tf_op jit(solution)/shard_map/ppermute | solution.py:12
  89.6 0.0 collective-permute-done.6
  89.6 2.7 %collective-permute-done.8 = f32[2,64,64]{2,1,0:T(8,128)S(1)} collective-permute-done((f32[2,64,64]{2,1,0:T(8,128)S(1)}, f32[2,64,64]{2,1,0:T(8,128)S(1)}, u32[]{:S(2)}, u32[]{:S(2)}) %collective-permute-start.8) | collective-permute-done | bytes 32800 | tf_op jit(solution)/shard_map/ppermute | solution.py:12
  92.4 3.2 %collective-permute-start.9 = (f32[64,64]{1,0:T(8,128)S(1)}, f32[64,64]{1,0:T(8,128)S(1)}, u32[]{:S(2)}, u32[]{:S(2)}) collective-permute-start(f32[64,64]{1,0:T(8,128)S(1)} %get-tuple-element.5), channel_id=1, source_target_pairs={{0,256},{64,320},{128,384},{192,448},{256,0},{320,64},{384,128},{4... | collective-permute-start | bytes 49160 | tf_op jit(solution)/shard_map/ppermute | solution.py:12
  95.5 0.1 pad_maximum_fusion.1
  95.6 0.0 copy-start.2
  95.7 1.3 %copy.6 = f32[1024,256]{1,0:T(8,128)} copy(f32[1024,256]{0,1:T(8,128)S(1)} %pad_maximum_fusion.1) | data formatting | bytes 2097152
  97.0 2.7 %collective-permute-done.9 = f32[64,64]{1,0:T(8,128)S(1)} collective-permute-done((f32[64,64]{1,0:T(8,128)S(1)}, f32[64,64]{1,0:T(8,128)S(1)}, u32[]{:S(2)}, u32[]{:S(2)}) %collective-permute-start.9) | collective-permute-done | bytes 16416 | tf_op jit(solution)/shard_map/ppermute | solution.py:12
  99.7 0.0 copy-done.2
  99.7 0.7 maximum_multiply_fusion
  (9 shorter events, 0.1 us)
Async XLA Ops:
  0.6 0.9 copy-start
  0.6 2.6 %copy-start.1 = (bf16[1024,64]{0,1:T(8,128)(2,1)S(1)}, bf16[1024,64]{0,1:T(8,128)(2,1)}, u32[]{:S(2)}) copy-start(bf16[1024,64]{0,1:T(8,128)(2,1)} %param.5) | copy-start | bytes 393220
  3.3 9.9 %collective-permute-start = (bf16[1024,128]{0,1:T(8,128)(2,1)S(1)}, bf16[1024,128]{0,1:T(8,128)(2,1)S(1)}, u32[]{:S(2)}, u32[]{:S(2)}) collective-permute-start(bf16[1024,128]{0,1:T(8,128)(2,1)S(1)} %pad_maximum_fusion.3), channel_id=1, source_target_pairs={{0,64},{64,0},{128,192},{192,128},{256,320},{320,256},{384,448},{4... | collective-permute-start | bytes 786440 | tf_op jit(solution)/shard_map/ppermute | solution.py:12
  13.3 16.2 %collective-permute-start.1 = (bf16[2048,128]{0,1:T(8,128)(2,1)S(1)}, bf16[2048,128]{0,1:T(8,128)(2,1)S(1)}, u32[]{:S(2)}, u32[]{:S(2)}) collective-permute-start(bf16[2048,128]{0,1:T(8,128)(2,1)S(1)} %pad_maximum_fusion.2), channel_id=1, source_target_pairs={{0,128},{64,192},{128,0},{192,64},{256,384},{320,448},{384,256},{4... | collective-permute-start | bytes 1572872 | tf_op jit(solution)/shard_map/ppermute | solution.py:12
  18.2 16.4 %collective-permute-start.3 = (bf16[2048,128]{0,1:T(8,128)(2,1)S(1)}, bf16[2048,128]{0,1:T(8,128)(2,1)}, u32[]{:S(2)}, u32[]{:S(2)}) collective-permute-start(bf16[2048,128]{0,1:T(8,128)(2,1)S(1)} %pad_maximum_fusion.2), channel_id=1, source_target_pairs={{0,1},{1,0},{2,3},{3,2},{4,5},{5,4},{6,7},{7,6},{8,9},{9,8},{10,11... | collective-permute-start | bytes 1572872 | tf_op jit(solution)/shard_map/ppermute | solution.py:12
  29.6 26.7 %collective-permute-start.2 = (bf16[4096,128]{0,1:T(8,128)(2,1)S(1)}, bf16[4096,128]{0,1:T(8,128)(2,1)}, u32[]{:S(2)}, u32[]{:S(2)}) collective-permute-start(bf16[4096,128]{0,1:T(8,128)(2,1)S(1)} %pad_maximum_fusion), channel_id=1, source_target_pairs={{0,256},{64,320},{128,384},{192,448},{256,0},{320,64},{384,128},{4... | collective-permute-start | bytes 3145736 | tf_op jit(solution)/shard_map/ppermute | solution.py:12
  32.7 11.1 %collective-permute-start.4 = (bf16[2048,128]{0,1:T(8,128)(2,1)S(1)}, bf16[2048,128]{0,1:T(8,128)(2,1)}, u32[]{:S(2)}, u32[]{:S(2)}) collective-permute-start(bf16[2048,128]{0,1:T(8,128)(2,1)S(1)} %collective-permute-done.1), channel_id=1, source_target_pairs={{0,1},{1,0},{2,3},{3,2},{4,5},{5,4},{6,7},{7,6},{8,9},{9,8},{10,11... | collective-permute-start | bytes 1572872 | tf_op jit(solution)/shard_map/ppermute | solution.py:12
  56.3 10.9 %collective-permute-start.5 = (bf16[4096,128]{0,1:T(8,128)(2,1)}, bf16[4096,128]{0,1:T(8,128)(2,1)S(1)}, u32[]{:S(2)}, u32[]{:S(2)}) collective-permute-start(bf16[4096,128]{0,1:T(8,128)(2,1)} %collective-permute-done.2), channel_id=1, source_target_pairs={{0,1},{1,0},{2,3},{3,2},{4,5},{5,4},{6,7},{7,6},{8,9},{9,8},{10,11... | collective-permute-start | bytes 3145736 | tf_op jit(solution)/shard_map/ppermute | solution.py:12
  67.3 6.1 %copy-start.3 = (f32[1024,64]{0,1:T(8,128)S(1)}, f32[1024,64]{0,1:T(8,128)}, u32[]{:S(2)}) copy-start(f32[1024,64]{0,1:T(8,128)} %fusion.5) | copy-start | bytes 786436
  78.2 6.4 %collective-permute-start.7 = (f32[2,64,64]{2,1,0:T(8,128)S(1)}, f32[2,64,64]{2,1,0:T(8,128)S(1)}, u32[]{:S(2)}, u32[]{:S(2)}) collective-permute-start(f32[2,64,64]{2,1,0:T(8,128)S(1)} %pad_maximum_fusion.4), channel_id=1, source_target_pairs={{0,64},{64,0},{128,192},{192,128},{256,320},{320,256},{384,448},{4... | collective-permute-start | bytes 98312 | tf_op jit(solution)/shard_map/ppermute | solution.py:12
  82.0 7.6 %collective-permute-start.6 = (f32[64,64]{1,0:T(8,128)S(1)}, f32[64,64]{1,0:T(8,128)S(1)}, u32[]{:S(2)}, u32[]{:S(2)}) collective-permute-start(f32[64,64]{1,0:T(8,128)S(1)} %fusion.52), channel_id=1, source_target_pairs={{0,64},{64,0},{128,192},{192,128},{256,320},{320,256},{384,448},{4... | collective-permute-start | bytes 49160 | tf_op jit(solution)/shard_map/ppermute | solution.py:12
  84.7 7.7 %collective-permute-start.8 = (f32[2,64,64]{2,1,0:T(8,128)S(1)}, f32[2,64,64]{2,1,0:T(8,128)S(1)}, u32[]{:S(2)}, u32[]{:S(2)}) collective-permute-start(f32[2,64,64]{2,1,0:T(8,128)S(1)} %fusion.51), channel_id=1, source_target_pairs={{0,128},{64,192},{128,0},{192,64},{256,384},{320,448},{384,256},{4... | collective-permute-start | bytes 98312 | tf_op jit(solution)/shard_map/ppermute | solution.py:12
  92.4 7.3 %collective-permute-start.9 = (f32[64,64]{1,0:T(8,128)S(1)}, f32[64,64]{1,0:T(8,128)S(1)}, u32[]{:S(2)}, u32[]{:S(2)}) collective-permute-start(f32[64,64]{1,0:T(8,128)S(1)} %get-tuple-element.5), channel_id=1, source_target_pairs={{0,256},{64,320},{128,384},{192,448},{256,0},{320,64},{384,128},{4... | collective-permute-start | bytes 49160 | tf_op jit(solution)/shard_map/ppermute | solution.py:12
  95.6 4.0 %copy-start.2 = (f32[4]{0:T(128)S(1)}, f32[4]{0:T(128)}, u32[]{:S(2)}) copy-start(f32[4]{0:T(128)} %constant.7) | copy-start | bytes 52

commit v4 on v3

--- a/solution.py
+++ b/solution.py
@@ -44,27 +44,39 @@
     row_sq = squares_of(located)
     packed = jnp.concatenate([located, sketch_matrix], axis=1)
     leaf_bits = lax.axis_size("leaf").bit_length() - 1
-    far_pieces = []
+    top = leaf_bits - 1
+    y_rows = swapped(located, "leaf", top)
+    y_sq = squares_of(y_rows)
     cluster = packed
+    other_pieces = []
     results = []
     grams = []
-    for tier_num in range(leaf_bits):
+    for tier_num in range(top):
         sib = swapped(cluster, "leaf", tier_num)
         if tier_num == 0:
-            far_pieces.append(swapped(jnp.concatenate([packed, sib]), "pair", 0))
+            other_pieces.append(swapped(jnp.concatenate([packed, sib]), "pair", 0))
         else:
-            far_pieces.append(swapped(sib, "pair", 0))
+            other_pieces.append(swapped(sib, "pair", 0))
         product = raw_product(located, row_sq, sib, dim) / math.sqrt(sib.shape[0])
         results.append(product)
         grams.append(gram_of(product))
         cluster = jnp.concatenate([cluster, sib])
-    far_total = None
+    partner_near = raw_product(y_rows, y_sq, cluster, dim)
+    partner_far = None
+    for piece in other_pieces:
+        part = raw_product(y_rows, y_sq, piece, dim)
+        partner_far = part if partner_far is None else partner_far + part
+    back = swapped(jnp.stack([partner_near, partner_far]), "leaf", top)
+    product = back[0] / math.sqrt(cluster.shape[0])
+    results.append(product)
+    grams.append(gram_of(product))
+    own_far = None
     far_rows = 0
-    for piece in far_pieces:
+    for piece in other_pieces:
         part = raw_product(located, row_sq, piece, dim)
-        far_total = part if far_total is None else far_total + part
+        own_far = part if own_far is None else own_far + part
         far_rows += piece.shape[0]
-    product = far_total / math.sqrt(far_rows)
+    product = (own_far + back[1]) / math.sqrt(2 * far_rows)
     results.append(product)
     grams.append(gram_of(product))
     n_tiers = len(grams)

time: 101 us -> 99.2 us (0.982); the launches traced: 100 us -> 97.4 us
  other arithmetic: 4.48 us -> 2.44 us
  waiting for transfers between devices: 30.8 us -> 29.6 us
    reduce_sum x6, other arithmetic: 3.47 us -> 1.38 us  [squares_of(): return jnp.sum(jnp.square(coords.astype(jnp.float32)), axis=-1)]
    ppermute x10, waiting for transfers between devices: 30.8 us -> 29.6 us  [swapped(): return lax.ppermute(value, axis, pairs)]
    dot_general x6 -> x7, matrix products: 27.5 us -> 26.9 us  [raw_product(): return jnp.dot(kernel, col_sketch, preferred_element_type=jnp.float32)]
    unnamed x9 -> x13, local copies, waits for them, and re-layouts: 2.22 us -> 2.83 us
  transfers between devices with their start and end apart: 10 -> 10, of which waited for: 6 -> 6; matrix products, arithmetic and copies ran while one was open for 23% -> 27% of each run, Pallas kernels for 0% -> 0%
where the time goes in v4:
time: 99.2 us; the launch traced here: 97.4 us
  starting transfers between devices  30.9 us (31%)
  matrix products  30.6 us (31%)
  waiting for transfers between devices  29.6 us (30%)
  local copies, waits for them, and re-layouts  2.83 us (3%)
  other arithmetic  2.44 us (2%)
    ppermute x10, starting transfers between devices, swapped(): return lax.ppermute(value, axis, pairs)  30.9 us
    ppermute x10, waiting for transfers between devices, swapped(): return lax.ppermute(value, axis, pairs)  29.6 us
    dot_general x7, matrix products, raw_product(): return jnp.dot(kernel, col_sketch, preferred_element_type=jnp.float32)  26.9 us
    unnamed x13, local copies, waits for them, and re-layouts  2.83 us
    dot_general x4, matrix products, gram_of(): jnp.dot(product.T, product, precision=lax.Precision.HIGHEST, preferred_el...  2.05 us
  transfers between devices with their start and end apart: 10, of which 6 were waited for; matrix products, arithmetic and copies ran while one was open for 27% of the time, Pallas kernels for 0%

profile of v4, /device:TPU:504, one launch (start us, length us, event | category | flops | bytes accessed | tf_op | source)
XLA Modules:
  0.0 97.4 jit_solution(5336502749043475538)
XLA Ops:
  0.6 0.0 copy-start
  0.6 0.0 copy-start.1
  0.7 0.9 copy-done
  1.5 1.7 %multiply_reduce_fusion.6 = (f32[1024]{0:T(1024)S(1)}, bf16[1024,64]{0,1:T(8,128)(2,1)S(1)}) fusion(bf16[1024,64]{0,1:T(8,128)(2,1)S(1)} %copy-done, s32[1024]{0:T(1024)} %bitcast.42), kind=kOutput, calls=%fused_computation.45 | convolution fusion | flops 135527424 | bytes 270336 | tf_op jit(solution)/shard_map/dot_general | solution.py:41
  3.3 0.0 copy-done.1
  3.3 3.4 %collective-permute-start = (bf16[1024,128]{0,1:T(8,128)(2,1)S(1)}, bf16[1024,128]{0,1:T(8,128)(2,1)S(1)}, u32[]{:S(2)}, u32[]{:S(2)}) collective-permute-start(bf16[1024,128]{0,1:T(8,128)(2,1)S(1)} %pad_maximum_fusion.4), channel_id=1, source_target_pairs={{0,64},{64,0},{128,192},{192,128},{256,320},{320,256},{384,448},{4... | collective-permute-start | bytes 786440 | tf_op jit(solution)/shard_map/ppermute | solution.py:12
  6.7 3.1 %collective-permute-start.2 = (bf16[1024,64]{0,1:T(8,128)(2,1)S(1)}, bf16[1024,64]{0,1:T(8,128)(2,1)S(1)}, u32[]{:S(2)}, u32[]{:S(2)}) collective-permute-start(bf16[1024,64]{0,1:T(8,128)(2,1)S(1)} %get-tuple-element.7), channel_id=1, source_target_pairs={{0,256},{64,320},{128,384},{192,448},{256,0},{320,64},{384,128},{4... | collective-permute-start | bytes 393224 | tf_op jit(solution)/shard_map/ppermute | solution.py:12
  9.8 5.2 %collective-permute-done.2 = bf16[1024,64]{0,1:T(8,128)(2,1)S(1)} collective-permute-done((bf16[1024,64]{0,1:T(8,128)(2,1)S(1)}, bf16[1024,64]{0,1:T(8,128)(2,1)S(1)}, u32[]{:S(2)}, u32[]{:S(2)}) %collective-permute-start.2) | collective-permute-done | bytes 131104 | tf_op jit(solution)/shard_map/ppermute | solution.py:12
  15.1 0.0 collective-permute-done
  15.1 0.6 copy-done.2
  15.8 4.6 %collective-permute-start.1 = (bf16[2048,128]{0,1:T(8,128)(2,1)S(1)}, bf16[2048,128]{0,1:T(8,128)(2,1)S(1)}, u32[]{:S(2)}, u32[]{:S(2)}) collective-permute-start(bf16[2048,128]{0,1:T(8,128)(2,1)S(1)} %pad_maximum_fusion.2), channel_id=1, source_target_pairs={{0,128},{64,192},{128,0},{192,64},{256,384},{320,448},{384,256},{4... | collective-permute-start | bytes 1572872 | tf_op jit(solution)/shard_map/ppermute | solution.py:12
  20.4 1.9 %collective-permute-start.3 = (bf16[2048,128]{0,1:T(8,128)(2,1)S(1)}, bf16[2048,128]{0,1:T(8,128)(2,1)S(1)}, u32[]{:S(2)}, u32[]{:S(2)}) collective-permute-start(bf16[2048,128]{0,1:T(8,128)(2,1)S(1)} %pad_maximum_fusion.2), channel_id=1, source_target_pairs={{0,1},{1,0},{2,3},{3,2},{4,5},{5,4},{6,7},{7,6},{8,9},{9,8},{10,11... | collective-permute-start | bytes 1572872 | tf_op jit(solution)/shard_map/ppermute | solution.py:12
  22.4 1.7 %fusion.9 = f32[1024,64]{0,1:T(8,128)S(1)} fusion(bf16[1024,64]{0,1:T(8,128)(2,1)S(1)} %get-tuple-element.7, f32[1024]{0:T(1024)S(1)} %multiply_reduce_fusion.5, f32[1024]{0:T(1024)S(1)} %get-tuple-element.6, bf16[1024,128]{0,1:T(8,128)(2,1)S(1)} %collective-permute-done), kind=kOutput, calls=%fused_computation.17 | convolution fusion | flops 274792448 | bytes 663552 | tf_op jit(solution)/shard_map/dot_general | solution.py:28
  24.1 1.0 convolution_bitcast_fusion.2
  25.0 6.3 %collective-permute-done.1 = bf16[2048,128]{0,1:T(8,128)(2,1)S(1)} collective-permute-done((bf16[2048,128]{0,1:T(8,128)(2,1)S(1)}, bf16[2048,128]{0,1:T(8,128)(2,1)S(1)}, u32[]{:S(2)}, u32[]{:S(2)}) %collective-permute-start.1) | collective-permute-done | bytes 524320 | tf_op jit(solution)/shard_map/ppermute | solution.py:12
  31.4 2.1 %collective-permute-start.4 = (bf16[2048,128]{0,1:T(8,128)(2,1)S(1)}, bf16[2048,128]{0,1:T(8,128)(2,1)}, u32[]{:S(2)}, u32[]{:S(2)}) collective-permute-start(bf16[2048,128]{0,1:T(8,128)(2,1)S(1)} %collective-permute-done.1), channel_id=1, source_target_pairs={{0,1},{1,0},{2,3},{3,2},{4,5},{5,4},{6,7},{7,6},{8,9},{9,8},{10,11... | collective-permute-start | bytes 1572872 | tf_op jit(solution)/shard_map/ppermute | solution.py:12
  33.5 0.1 pad_maximum_fusion
  33.6 0.1 multiply_reduce_fusion
  33.7 0.0 collective-permute-done.3
  33.7 0.1 multiply_reduce_fusion.2
  33.8 0.0 copy-start.3
  33.8 7.1 %fusion.11 = f32[1,1024,64]{1,2,0:T(8,128)S(1)} fusion(bf16[1024,64]{0,1:T(8,128)(2,1)} %copy-done.2, f32[4096]{0:T(1024)S(1)} %multiply_reduce_fusion, f32[1024]{0:T(1024)S(1)} %multiply_reduce_fusion.4, bf16[4096,128]{0,1:T(8,128)(2,1)S(1)} %pad_maximum_fusion), kind=kOutput, calls=%fused_computation.19 | convolution fusion | flops 1098907648 | bytes 1462272 | tf_op jit(solution)/shard_map/dot_general | solution.py:28
  40.9 3.2 %fusion.4 = f32[1024,64]{0,1:T(8,128)S(1)} fusion(bf16[1024,64]{0,1:T(8,128)(2,1)S(1)} %copy-done.3, f32[2048]{0:T(1024)S(1)} %multiply_reduce_fusion.2, f32[1024]{0:T(1024)S(1)} %multiply_reduce_fusion.4, bf16[2048,128]{0,1:T(8,128)(2,1)S(1)} %collective-permute-done.3), kind=kOutput, calls=%fused_computation.12 | convolution fusion | flops 549453824 | bytes 929792 | tf_op jit(solution)/shard_map/dot_general | solution.py:28
  44.0 0.1 multiply_reduce_fusion.3
  44.1 3.2 %fusion.10 = f32[1024,64]{0,1:T(8,128)S(1)} fusion(bf16[1024,64]{0,1:T(8,128)(2,1)S(1)} %get-tuple-element.7, f32[2048]{0:T(1024)S(1)} %multiply_reduce_fusion.3, f32[1024]{0:T(1024)S(1)} %get-tuple-element.6, bf16[2048,128]{0,1:T(8,128)(2,1)S(1)} %collective-permute-done.1), kind=kOutput, calls=%fused_computation.18 | convolution fusion | flops 549519360 | bytes 929792 | tf_op jit(solution)/shard_map/dot_general | solution.py:28
  47.3 0.0 collective-permute-done.4
  47.3 1.0 %multiply_reduce_fusion.1 = f32[2048]{0:T(1024)S(1)} fusion(bf16[2048,128]{0,1:T(8,128)(2,1)} %collective-permute-done.4), kind=kLoop, calls=%fused_computation.33 | loop fusion | flops 391168 | bytes 270336 | tf_op jit(solution)/shard_map/reduce_sum | solution.py:16
  48.3 4.4 %add_bitcast_fusion = f32[1,1024,64]{1,2,0:T(8,128)S(1)} fusion(f32[1024,64]{0,1:T(8,128)S(1)} %fusion.4, bf16[2048,128]{0,1:T(8,128)(2,1)} %collective-permute-done.4, bf16[1024,64]{0,1:T(8,128)(2,1)S(1)} %copy-done.3, f32[2048]{0:T(1024)S(1)} %multiply_reduce_fusion.1, f32[1024]{0:T(1024)S(1)} %multiply_reduce_fusion.4), kind=kOutput, calls=%fused_computation.42 | convolution fusion | flops 549519360 | bytes 1191936 | tf_op jit(solution)/shard_map/dot_general | solution.py:28
  52.8 3.1 %collective-permute-start.5 = (f32[2,1024,64]{1,2,0:T(8,128)S(1)}, f32[2,1024,64]{1,2,0:T(8,128)S(1)}, u32[]{:S(2)}, u32[]{:S(2)}) collective-permute-start(f32[2,1024,64]{1,2,0:T(8,128)S(1)} %pad_maximum_fusion.3), channel_id=1, source_target_pairs={{0,256},{64,320},{128,384},{192,448},{256,0},{320,64},{384,128},{4... | collective-permute-start | bytes 1572872 | tf_op jit(solution)/shard_map/ppermute | solution.py:12
  56.0 0.4 fusion.63
  56.3 2.4 %collective-permute-start.6 = (f32[64,64]{1,0:T(8,128)S(1)}, f32[64,64]{1,0:T(8,128)S(1)}, u32[]{:S(2)}, u32[]{:S(2)}) collective-permute-start(f32[64,64]{1,0:T(8,128)S(1)} %fusion.63), channel_id=1, source_target_pairs={{0,64},{64,0},{128,192},{192,128},{256,320},{320,256},{384,448},{4... | collective-permute-start | bytes 49160 | tf_op jit(solution)/shard_map/ppermute | solution.py:12
  58.8 3.2 %fusion.6 = f32[1024,64]{0,1:T(8,128)S(1)} fusion(bf16[1024,64]{0,1:T(8,128)(2,1)S(1)} %get-tuple-element.7, f32[2048]{0:T(1024)S(1)} %multiply_reduce_fusion.2, f32[1024]{0:T(1024)S(1)} %get-tuple-element.6, bf16[2048,128]{0,1:T(8,128)(2,1)S(1)} %collective-permute-done.3), kind=kOutput, calls=%fused_computation.14 | convolution fusion | flops 549453824 | bytes 929792 | tf_op jit(solution)/shard_map/dot_general | solution.py:28
  61.9 8.6 %collective-permute-done.5 = f32[2,1024,64]{1,2,0:T(8,128)S(1)} collective-permute-done((f32[2,1024,64]{1,2,0:T(8,128)S(1)}, f32[2,1024,64]{1,2,0:T(8,128)S(1)}, u32[]{:S(2)}, u32[]{:S(2)}) %collective-permute-start.5) | collective-permute-done | bytes 524320 | tf_op jit(solution)/shard_map/ppermute | solution.py:12
  70.5 4.2 %fusion.14 = f32[1024,64]{0,1:T(8,128)S(1)} fusion(f32[1024,64]{0,1:T(8,128)S(1)} %fusion.6, bf16[1024,64]{0,1:T(8,128)(2,1)S(1)} %get-tuple-element.7, f32[2048]{0:T(1024)S(1)} %multiply_reduce_fusion.1, f32[1024]{0:T(1024)S(1)} %get-tuple-element.6, f32[2,1024,64]{1,2,0:T(8,128)S(1)} %collective-permute-done.5, bf16[2048,128]{0,1:T(8,128)(2,1)} %collective-permute-done.4), kind=kOutput, calls=%fused_computation.22 | convolution fusion | flops 549650432 | bytes 1454080 | tf_op jit(solution)/shard_map/dot_general | solution.py:28
  74.7 0.4 convolution_bitcast_fusion
  75.1 0.4 convolution_bitcast_fusion.1
  75.5 2.4 %collective-permute-start.7 = (f32[2,64,64]{2,1,0:T(8,128)S(1)}, f32[2,64,64]{2,1,0:T(8,128)S(1)}, u32[]{:S(2)}, u32[]{:S(2)}) collective-permute-start(f32[2,64,64]{2,1,0:T(8,128)S(1)} %pad_maximum_fusion.5), channel_id=1, source_target_pairs={{0,64},{64,0},{128,192},{192,128},{256,320},{320,256},{384,448},{4... | collective-permute-start | bytes 98312 | tf_op jit(solution)/shard_map/ppermute | solution.py:12
  77.9 0.0 collective-permute-done.6
  77.9 3.7 %collective-permute-done.7 = f32[2,64,64]{2,1,0:T(8,128)S(1)} collective-permute-done((f32[2,64,64]{2,1,0:T(8,128)S(1)}, f32[2,64,64]{2,1,0:T(8,128)S(1)}, u32[]{:S(2)}, u32[]{:S(2)}) %collective-permute-start.7) | collective-permute-done | bytes 32800 | tf_op jit(solution)/shard_map/ppermute | solution.py:12
  81.7 4.6 %collective-permute-start.8 = (f32[2,64,64]{2,1,0:T(8,128)S(1)}, f32[2,64,64]{2,1,0:T(8,128)S(1)}, u32[]{:S(2)}, u32[]{:S(2)}) collective-permute-start(f32[2,64,64]{2,1,0:T(8,128)S(1)} %fusion.61), channel_id=1, source_target_pairs={{0,128},{64,192},{128,0},{192,64},{256,384},{320,448},{384,256},{4... | collective-permute-start | bytes 98312 | tf_op jit(solution)/shard_map/ppermute | solution.py:12
  86.3 3.0 %collective-permute-done.8 = f32[2,64,64]{2,1,0:T(8,128)S(1)} collective-permute-done((f32[2,64,64]{2,1,0:T(8,128)S(1)}, f32[2,64,64]{2,1,0:T(8,128)S(1)}, u32[]{:S(2)}, u32[]{:S(2)}) %collective-permute-start.8) | collective-permute-done | bytes 32800 | tf_op jit(solution)/shard_map/ppermute | solution.py:12
  89.3 3.1 %collective-permute-start.9 = (f32[64,64]{1,0:T(8,128)S(1)}, f32[64,64]{1,0:T(8,128)S(1)}, u32[]{:S(2)}, u32[]{:S(2)}) collective-permute-start(f32[64,64]{1,0:T(8,128)S(1)} %get-tuple-element.5), channel_id=1, source_target_pairs={{0,256},{64,320},{128,384},{192,448},{256,0},{320,64},{384,128},{4... | collective-permute-start | bytes 49160 | tf_op jit(solution)/shard_map/ppermute | solution.py:12
  92.5 0.1 pad_maximum_fusion.1
  92.6 0.0 copy-start.5
  92.6 1.3 %copy.6 = f32[1024,256]{1,0:T(8,128)} copy(f32[1024,256]{0,1:T(8,128)S(1)} %pad_maximum_fusion.1) | data formatting | bytes 2097152
  93.9 2.7 %collective-permute-done.9 = f32[64,64]{1,0:T(8,128)S(1)} collective-permute-done((f32[64,64]{1,0:T(8,128)S(1)}, f32[64,64]{1,0:T(8,128)S(1)}, u32[]{:S(2)}, u32[]{:S(2)}) %collective-permute-start.9) | collective-permute-done | bytes 16416 | tf_op jit(solution)/shard_map/ppermute | solution.py:12
  96.7 0.0 copy-done.4
  96.7 0.7 maximum_multiply_fusion
  (16 shorter events, 0.3 us)
Async XLA Ops:
  0.6 0.9 copy-start
  0.6 2.6 %copy-start.1 = (bf16[1024,64]{0,1:T(8,128)(2,1)S(1)}, bf16[1024,64]{0,1:T(8,128)(2,1)}, u32[]{:S(2)}) copy-start(bf16[1024,64]{0,1:T(8,128)(2,1)} %param.5) | copy-start | bytes 393220
  3.3 11.8 %collective-permute-start = (bf16[1024,128]{0,1:T(8,128)(2,1)S(1)}, bf16[1024,128]{0,1:T(8,128)(2,1)S(1)}, u32[]{:S(2)}, u32[]{:S(2)}) collective-permute-start(bf16[1024,128]{0,1:T(8,128)(2,1)S(1)} %pad_maximum_fusion.4), channel_id=1, source_target_pairs={{0,64},{64,0},{128,192},{192,128},{256,320},{320,256},{384,448},{4... | collective-permute-start | bytes 786440 | tf_op jit(solution)/shard_map/ppermute | solution.py:12
  6.7 8.4 %collective-permute-start.2 = (bf16[1024,64]{0,1:T(8,128)(2,1)S(1)}, bf16[1024,64]{0,1:T(8,128)(2,1)S(1)}, u32[]{:S(2)}, u32[]{:S(2)}) collective-permute-start(bf16[1024,64]{0,1:T(8,128)(2,1)S(1)} %get-tuple-element.7), channel_id=1, source_target_pairs={{0,256},{64,320},{128,384},{192,448},{256,0},{320,64},{384,128},{4... | collective-permute-start | bytes 393224 | tf_op jit(solution)/shard_map/ppermute | solution.py:12
  15.1 0.7 copy-start.2
  15.8 15.6 %collective-permute-start.1 = (bf16[2048,128]{0,1:T(8,128)(2,1)S(1)}, bf16[2048,128]{0,1:T(8,128)(2,1)S(1)}, u32[]{:S(2)}, u32[]{:S(2)}) collective-permute-start(bf16[2048,128]{0,1:T(8,128)(2,1)S(1)} %pad_maximum_fusion.2), channel_id=1, source_target_pairs={{0,128},{64,192},{128,0},{192,64},{256,384},{320,448},{384,256},{4... | collective-permute-start | bytes 1572872 | tf_op jit(solution)/shard_map/ppermute | solution.py:12
  20.4 13.3 %collective-permute-start.3 = (bf16[2048,128]{0,1:T(8,128)(2,1)S(1)}, bf16[2048,128]{0,1:T(8,128)(2,1)S(1)}, u32[]{:S(2)}, u32[]{:S(2)}) collective-permute-start(bf16[2048,128]{0,1:T(8,128)(2,1)S(1)} %pad_maximum_fusion.2), channel_id=1, source_target_pairs={{0,1},{1,0},{2,3},{3,2},{4,5},{5,4},{6,7},{7,6},{8,9},{9,8},{10,11... | collective-permute-start | bytes 1572872 | tf_op jit(solution)/shard_map/ppermute | solution.py:12
  31.4 15.9 %collective-permute-start.4 = (bf16[2048,128]{0,1:T(8,128)(2,1)S(1)}, bf16[2048,128]{0,1:T(8,128)(2,1)}, u32[]{:S(2)}, u32[]{:S(2)}) collective-permute-start(bf16[2048,128]{0,1:T(8,128)(2,1)S(1)} %collective-permute-done.1), channel_id=1, source_target_pairs={{0,1},{1,0},{2,3},{3,2},{4,5},{5,4},{6,7},{7,6},{8,9},{9,8},{10,11... | collective-permute-start | bytes 1572872 | tf_op jit(solution)/shard_map/ppermute | solution.py:12
  33.8 7.1 %copy-start.3 = (bf16[1024,64]{0,1:T(8,128)(2,1)S(1)}, bf16[1024,64]{0,1:T(8,128)(2,1)}, u32[]{:S(2)}) copy-start(bf16[1024,64]{0,1:T(8,128)(2,1)} %copy-done.2) | copy-start | bytes 393220
  52.8 17.7 %collective-permute-start.5 = (f32[2,1024,64]{1,2,0:T(8,128)S(1)}, f32[2,1024,64]{1,2,0:T(8,128)S(1)}, u32[]{:S(2)}, u32[]{:S(2)}) collective-permute-start(f32[2,1024,64]{1,2,0:T(8,128)S(1)} %pad_maximum_fusion.3), channel_id=1, source_target_pairs={{0,256},{64,320},{128,384},{192,448},{256,0},{320,64},{384,128},{4... | collective-permute-start | bytes 1572872 | tf_op jit(solution)/shard_map/ppermute | solution.py:12
  56.3 21.6 %collective-permute-start.6 = (f32[64,64]{1,0:T(8,128)S(1)}, f32[64,64]{1,0:T(8,128)S(1)}, u32[]{:S(2)}, u32[]{:S(2)}) collective-permute-start(f32[64,64]{1,0:T(8,128)S(1)} %fusion.63), channel_id=1, source_target_pairs={{0,64},{64,0},{128,192},{192,128},{256,320},{320,256},{384,448},{4... | collective-permute-start | bytes 49160 | tf_op jit(solution)/shard_map/ppermute | solution.py:12
  75.5 6.2 %collective-permute-start.7 = (f32[2,64,64]{2,1,0:T(8,128)S(1)}, f32[2,64,64]{2,1,0:T(8,128)S(1)}, u32[]{:S(2)}, u32[]{:S(2)}) collective-permute-start(f32[2,64,64]{2,1,0:T(8,128)S(1)} %pad_maximum_fusion.5), channel_id=1, source_target_pairs={{0,64},{64,0},{128,192},{192,128},{256,320},{320,256},{384,448},{4... | collective-permute-start | bytes 98312 | tf_op jit(solution)/shard_map/ppermute | solution.py:12
  81.7 7.7 %collective-permute-start.8 = (f32[2,64,64]{2,1,0:T(8,128)S(1)}, f32[2,64,64]{2,1,0:T(8,128)S(1)}, u32[]{:S(2)}, u32[]{:S(2)}) collective-permute-start(f32[2,64,64]{2,1,0:T(8,128)S(1)} %fusion.61), channel_id=1, source_target_pairs={{0,128},{64,192},{128,0},{192,64},{256,384},{320,448},{384,256},{4... | collective-permute-start | bytes 98312 | tf_op jit(solution)/shard_map/ppermute | solution.py:12
  89.3 7.3 %collective-permute-start.9 = (f32[64,64]{1,0:T(8,128)S(1)}, f32[64,64]{1,0:T(8,128)S(1)}, u32[]{:S(2)}, u32[]{:S(2)}) collective-permute-start(f32[64,64]{1,0:T(8,128)S(1)} %get-tuple-element.5), channel_id=1, source_target_pairs={{0,256},{64,320},{128,384},{192,448},{256,0},{320,64},{384,128},{4... | collective-permute-start | bytes 49160 | tf_op jit(solution)/shard_map/ppermute | solution.py:12
  92.6 4.1 %copy-start.4 = (f32[1,1,64,64]{3,2,1,0:T(8,128)S(1)}, f32[1,1,64,64]{3,2,1,0:T(8,128)}, u32[]{:S(2)}) copy-start(f32[1,1,64,64]{3,2,1,0:T(8,128)} %convolution_bitcast_fusion.2) | copy-start | bytes 49156
  92.6 4.1 %copy-start.5 = (f32[4]{0:T(128)S(1)}, f32[4]{0:T(128)}, u32[]{:S(2)}) copy-start(f32[4]{0:T(128)} %constant.7) | copy-start | bytes 52

commit v5 on v4

--- a/solution.py
+++ b/solution.py
@@ -51,17 +51,20 @@
     other_pieces = []
     results = []
     grams = []
+    partner_near = None
     for tier_num in range(top):
         sib = swapped(cluster, "leaf", tier_num)
         if tier_num == 0:
-            other_pieces.append(swapped(jnp.concatenate([packed, sib]), "pair", 0))
+            first = jnp.concatenate([packed, sib])
+            other_pieces.append(swapped(first, "pair", 0))
+            partner_near = raw_product(y_rows, y_sq, first, dim)
         else:
             other_pieces.append(swapped(sib, "pair", 0))
+            partner_near = partner_near + raw_product(y_rows, y_sq, sib, dim)
         product = raw_product(located, row_sq, sib, dim) / math.sqrt(sib.shape[0])
         results.append(product)
         grams.append(gram_of(product))
         cluster = jnp.concatenate([cluster, sib])
-    partner_near = raw_product(y_rows, y_sq, cluster, dim)
     partner_far = None
     for piece in other_pieces:
         part = raw_product(y_rows, y_sq, piece, dim)

time: 99.2 us -> 105 us (1.058)
  the two profiles are of different devices: /device:TPU:504 before, /device:TPU:2 now
where the time goes in v5:
time: 105 us; the launch traced here: 104 us
  waiting for transfers between devices  43.9 us (42%)
  matrix products  29.3 us (28%)
  starting transfers between devices  25.8 us (25%)
  other arithmetic  2.3 us (2%)
  local copies, waits for them, and re-layouts  2.22 us (2%)
    ppermute x10, waiting for transfers between devices, swapped(): return lax.ppermute(value, axis, pairs)  43.9 us
    dot_general x8, matrix products, raw_product(): return jnp.dot(kernel, col_sketch, preferred_element_type=jnp.float32)  26.2 us
    ppermute x10, starting transfers between devices, swapped(): return lax.ppermute(value, axis, pairs)  25.8 us
    unnamed x7, local copies, waits for them, and re-layouts  2.21 us
  transfers between devices with their start and end apart: 10, of which 6 were waited for; matrix products, arithmetic and copies ran while one was open for 26% of the time, Pallas kernels for 0%

profile of v5, /device:TPU:2, one launch (start us, length us, event | category | flops | bytes accessed | tf_op | source)
XLA Modules:
  0.0 104.5 jit_solution(13971326522518850970)
XLA Ops:
  0.6 0.0 copy-start
  0.6 0.0 copy-start.1
  0.7 0.9 copy-done
  1.5 1.7 %multiply_reduce_fusion.6 = (f32[1024]{0:T(1024)S(1)}, bf16[1024,64]{0,1:T(8,128)(2,1)S(1)}) fusion(bf16[1024,64]{0,1:T(8,128)(2,1)S(1)} %copy-done, s32[1024]{0:T(1024)} %bitcast.43), kind=kOutput, calls=%fused_computation.45 | convolution fusion | flops 135527424 | bytes 270336 | tf_op jit(solution)/shard_map/dot_general | solution.py:41
  3.3 0.0 copy-done.1
  3.3 7.8 %collective-permute-start = (bf16[1024,128]{0,1:T(8,128)(2,1)S(1)}, bf16[1024,128]{0,1:T(8,128)(2,1)S(1)}, u32[]{:S(2)}, u32[]{:S(2)}) collective-permute-start(bf16[1024,128]{0,1:T(8,128)(2,1)S(1)} %pad_maximum_fusion.3), channel_id=1, source_target_pairs={{0,64},{64,0},{128,192},{192,128},{256,320},{320,256},{384,448},{4... | collective-permute-start | bytes 786440 | tf_op jit(solution)/shard_map/ppermute | solution.py:12
  11.1 1.9 %collective-permute-start.2 = (bf16[1024,64]{0,1:T(8,128)(2,1)S(1)}, bf16[1024,64]{0,1:T(8,128)(2,1)S(1)}, u32[]{:S(2)}, u32[]{:S(2)}) collective-permute-start(bf16[1024,64]{0,1:T(8,128)(2,1)S(1)} %get-tuple-element.7), channel_id=1, source_target_pairs={{0,256},{64,320},{128,384},{192,448},{256,0},{320,64},{384,128},{4... | collective-permute-start | bytes 393224 | tf_op jit(solution)/shard_map/ppermute | solution.py:12
  13.0 6.4 %collective-permute-done.2 = bf16[1024,64]{0,1:T(8,128)(2,1)S(1)} collective-permute-done((bf16[1024,64]{0,1:T(8,128)(2,1)S(1)}, bf16[1024,64]{0,1:T(8,128)(2,1)S(1)}, u32[]{:S(2)}, u32[]{:S(2)}) %collective-permute-start.2) | collective-permute-done | bytes 131104 | tf_op jit(solution)/shard_map/ppermute | solution.py:12
  19.5 0.0 collective-permute-done
  19.6 0.1 multiply_reduce_fusion.2
  19.6 1.9 %collective-permute-start.3 = (bf16[2048,128]{0,1:T(8,128)(2,1)S(1)}, bf16[2048,128]{0,1:T(8,128)(2,1)S(1)}, u32[]{:S(2)}, u32[]{:S(2)}) collective-permute-start(bf16[2048,128]{0,1:T(8,128)(2,1)S(1)} %pad_maximum_fusion.1), channel_id=1, source_target_pairs={{0,1},{1,0},{2,3},{3,2},{4,5},{5,4},{6,7},{7,6},{8,9},{9,8},{10,11... | collective-permute-start | bytes 1572872 | tf_op jit(solution)/shard_map/ppermute | solution.py:12
  21.6 1.9 %collective-permute-start.1 = (bf16[2048,128]{0,1:T(8,128)(2,1)S(1)}, bf16[2048,128]{0,1:T(8,128)(2,1)}, u32[]{:S(2)}, u32[]{:S(2)}) collective-permute-start(bf16[2048,128]{0,1:T(8,128)(2,1)S(1)} %pad_maximum_fusion.1), channel_id=1, source_target_pairs={{0,128},{64,192},{128,0},{192,64},{256,384},{320,448},{384,256},{4... | collective-permute-start | bytes 1572872 | tf_op jit(solution)/shard_map/ppermute | solution.py:12
  23.5 1.7 %fusion.10 = f32[1024,64]{0,1:T(8,128)S(1)} fusion(bf16[1024,64]{0,1:T(8,128)(2,1)S(1)} %get-tuple-element.7, f32[1024]{0:T(1024)S(1)} %multiply_reduce_fusion.5, f32[1024]{0:T(1024)S(1)} %get-tuple-element.6, bf16[1024,128]{0,1:T(8,128)(2,1)S(1)} %collective-permute-done), kind=kOutput, calls=%fused_computation.19 | convolution fusion | flops 274792448 | bytes 663552 | tf_op jit(solution)/shard_map/dot_general | solution.py:28
  25.2 0.4 convolution_bitcast_fusion.2
  25.6 13.8 %collective-permute-done.1 = bf16[2048,128]{0,1:T(8,128)(2,1)} collective-permute-done((bf16[2048,128]{0,1:T(8,128)(2,1)S(1)}, bf16[2048,128]{0,1:T(8,128)(2,1)}, u32[]{:S(2)}, u32[]{:S(2)}) %collective-permute-start.1) | collective-permute-done | bytes 524320 | tf_op jit(solution)/shard_map/ppermute | solution.py:12
  39.4 2.1 %collective-permute-start.4 = (bf16[2048,128]{0,1:T(8,128)(2,1)}, bf16[2048,128]{0,1:T(8,128)(2,1)S(1)}, u32[]{:S(2)}, u32[]{:S(2)}) collective-permute-start(bf16[2048,128]{0,1:T(8,128)(2,1)} %collective-permute-done.1), channel_id=1, source_target_pairs={{0,1},{1,0},{2,3},{3,2},{4,5},{5,4},{6,7},{7,6},{8,9},{9,8},{10,11... | collective-permute-start | bytes 1572872 | tf_op jit(solution)/shard_map/ppermute | solution.py:12
  41.5 1.0 multiply_reduce_fusion.3
  42.5 0.0 collective-permute-done.3
  42.5 0.1 multiply_reduce_fusion.1
  42.6 4.2 %fusion.11 = f32[1024,64]{0,1:T(8,128)S(1)} fusion(bf16[1024,64]{0,1:T(8,128)(2,1)S(1)} %get-tuple-element.7, f32[2048]{0:T(1024)S(1)} %multiply_reduce_fusion.3, f32[1024]{0:T(1024)S(1)} %get-tuple-element.6, bf16[2048,128]{0,1:T(8,128)(2,1)} %collective-permute-done.1), kind=kOutput, calls=%fused_computation.20 | convolution fusion | flops 549519360 | bytes 929792 | tf_op jit(solution)/shard_map/dot_general | solution.py:28
  46.8 4.2 %fusion.4 = f32[1024,64]{0,1:T(8,128)S(1)} fusion(bf16[1024,64]{0,1:T(8,128)(2,1)S(1)} %collective-permute-done.2, f32[1024]{0:T(1024)S(1)} %multiply_reduce_fusion.4, f32[2048]{0:T(1024)S(1)} %multiply_reduce_fusion.3, bf16[2048,128]{0,1:T(8,128)(2,1)} %collective-permute-done.1), kind=kOutput, calls=%fused_computation.13 | convolution fusion | flops 549453824 | bytes 929792 | tf_op jit(solution)/shard_map/dot_general | solution.py:28
  51.0 3.2 %fusion.5 = f32[1024,64]{0,1:T(8,128)S(1)} fusion(bf16[1024,64]{0,1:T(8,128)(2,1)S(1)} %collective-permute-done.2, f32[2048]{0:T(1024)S(1)} %multiply_reduce_fusion.1, f32[1024]{0:T(1024)S(1)} %multiply_reduce_fusion.4, bf16[2048,128]{0,1:T(8,128)(2,1)S(1)} %collective-permute-done.3), kind=kOutput, calls=%fused_computation.14 | convolution fusion | flops 549453824 | bytes 929792 | tf_op jit(solution)/shard_map/dot_general | solution.py:28
  54.2 3.2 %fusion.16 = f32[1,1024,64]{1,2,0:T(8,128)S(1)} fusion(f32[1024,64]{0,1:T(8,128)S(1)} %fusion.4, bf16[1024,64]{0,1:T(8,128)(2,1)S(1)} %collective-permute-done.2, f32[2048]{0:T(1024)S(1)} %multiply_reduce_fusion.2, f32[1024]{0:T(1024)S(1)} %multiply_reduce_fusion.4, bf16[2048,128]{0,1:T(8,128)(2,1)S(1)} %pad_maximum_fusion.1), kind=kOutput, calls=%fused_computation.25 | convolution fusion | flops 549519360 | bytes 1191936 | tf_op jit(solution)/shard_map/dot_general | solution.py:28
  57.3 0.0 collective-permute-done.4
  57.3 0.1 multiply_reduce_fusion
  57.4 3.4 %add_bitcast_fusion = f32[1,1024,64]{1,2,0:T(8,128)S(1)} fusion(f32[1024,64]{0,1:T(8,128)S(1)} %fusion.5, bf16[2048,128]{0,1:T(8,128)(2,1)S(1)} %collective-permute-done.4, bf16[1024,64]{0,1:T(8,128)(2,1)S(1)} %collective-permute-done.2, f32[2048]{0:T(1024)S(1)} %multiply_reduce_fusion, f32[1024]{0:T(1024)S(1)} %multiply_reduce_fusion.4), kind=kOutput, calls=%fused_computation.42 | convolution fusion | flops 549519360 | bytes 1191936 | tf_op jit(solution)/shard_map/dot_general | solution.py:28
  60.9 1.9 %collective-permute-start.5 = (f32[2,1024,64]{1,2,0:T(8,128)S(1)}, f32[2,1024,64]{1,2,0:T(8,128)S(1)}, u32[]{:S(2)}, u32[]{:S(2)}) collective-permute-start(f32[2,1024,64]{1,2,0:T(8,128)S(1)} %pad_maximum_fusion.2), channel_id=1, source_target_pairs={{0,256},{64,320},{128,384},{192,448},{256,0},{320,64},{384,128},{4... | collective-permute-start | bytes 1572872 | tf_op jit(solution)/shard_map/ppermute | solution.py:12
  62.8 0.4 fusion.71
  63.2 1.9 %collective-permute-start.6 = (f32[64,64]{1,0:T(8,128)S(1)}, f32[64,64]{1,0:T(8,128)S(1)}, u32[]{:S(2)}, u32[]{:S(2)}) collective-permute-start(f32[64,64]{1,0:T(8,128)S(1)} %fusion.71), channel_id=1, source_target_pairs={{0,64},{64,0},{128,192},{192,128},{256,320},{320,256},{384,448},{4... | collective-permute-start | bytes 49160 | tf_op jit(solution)/shard_map/ppermute | solution.py:12
  65.1 3.2 %fusion.7 = f32[1024,64]{0,1:T(8,128)S(1)} fusion(bf16[1024,64]{0,1:T(8,128)(2,1)S(1)} %get-tuple-element.7, f32[2048]{0:T(1024)S(1)} %multiply_reduce_fusion.1, f32[1024]{0:T(1024)S(1)} %get-tuple-element.6, bf16[2048,128]{0,1:T(8,128)(2,1)S(1)} %collective-permute-done.3), kind=kOutput, calls=%fused_computation.16 | convolution fusion | flops 549453824 | bytes 929792 | tf_op jit(solution)/shard_map/dot_general | solution.py:28
  68.3 10.3 %collective-permute-done.5 = f32[2,1024,64]{1,2,0:T(8,128)S(1)} collective-permute-done((f32[2,1024,64]{1,2,0:T(8,128)S(1)}, f32[2,1024,64]{1,2,0:T(8,128)S(1)}, u32[]{:S(2)}, u32[]{:S(2)}) %collective-permute-start.5) | collective-permute-done | bytes 524320 | tf_op jit(solution)/shard_map/ppermute | solution.py:12
  78.6 3.2 %fusion.14 = f32[1024,64]{0,1:T(8,128)S(1)} fusion(f32[1024,64]{0,1:T(8,128)S(1)} %fusion.7, bf16[1024,64]{0,1:T(8,128)(2,1)S(1)} %get-tuple-element.7, f32[2048]{0:T(1024)S(1)} %multiply_reduce_fusion, f32[1024]{0:T(1024)S(1)} %get-tuple-element.6, f32[2,1024,64]{1,2,0:T(8,128)S(1)} %collective-permute-done.5, bf16[2048,128]{0,1:T(8,128)(2,1)S(1)} %collective-permute-done.4), kind=kOutput, calls=%fused_computation.23 | convolution fusion | flops 549650432 | bytes 1454080 | tf_op jit(solution)/shard_map/dot_general | solution.py:28
  81.8 0.4 convolution_bitcast_fusion
  82.2 0.4 convolution_bitcast_fusion.1
  82.5 1.9 %collective-permute-start.7 = (f32[2,64,64]{2,1,0:T(8,128)S(1)}, f32[2,64,64]{2,1,0:T(8,128)S(1)}, u32[]{:S(2)}, u32[]{:S(2)}) collective-permute-start(f32[2,64,64]{2,1,0:T(8,128)S(1)} %pad_maximum_fusion.4), channel_id=1, source_target_pairs={{0,64},{64,0},{128,192},{192,128},{256,320},{320,256},{384,448},{4... | collective-permute-start | bytes 98312 | tf_op jit(solution)/shard_map/ppermute | solution.py:12
  84.5 0.0 collective-permute-done.6
  84.5 4.2 %collective-permute-done.7 = f32[2,64,64]{2,1,0:T(8,128)S(1)} collective-permute-done((f32[2,64,64]{2,1,0:T(8,128)S(1)}, f32[2,64,64]{2,1,0:T(8,128)S(1)}, u32[]{:S(2)}, u32[]{:S(2)}) %collective-permute-start.7) | collective-permute-done | bytes 32800 | tf_op jit(solution)/shard_map/ppermute | solution.py:12
  88.7 2.2 %collective-permute-start.8 = (f32[2,64,64]{2,1,0:T(8,128)S(1)}, f32[2,64,64]{2,1,0:T(8,128)S(1)}, u32[]{:S(2)}, u32[]{:S(2)}) collective-permute-start(f32[2,64,64]{2,1,0:T(8,128)S(1)} %fusion.69), channel_id=1, source_target_pairs={{0,128},{64,192},{128,0},{192,64},{256,384},{320,448},{384,256},{4... | collective-permute-start | bytes 98312 | tf_op jit(solution)/shard_map/ppermute | solution.py:12
  91.0 5.4 %collective-permute-done.8 = f32[2,64,64]{2,1,0:T(8,128)S(1)} collective-permute-done((f32[2,64,64]{2,1,0:T(8,128)S(1)}, f32[2,64,64]{2,1,0:T(8,128)S(1)}, u32[]{:S(2)}, u32[]{:S(2)}) %collective-permute-start.8) | collective-permute-done | bytes 32800 | tf_op jit(solution)/shard_map/ppermute | solution.py:12
  96.4 2.2 %collective-permute-start.9 = (f32[64,64]{1,0:T(8,128)S(1)}, f32[64,64]{1,0:T(8,128)S(1)}, u32[]{:S(2)}, u32[]{:S(2)}) collective-permute-start(f32[64,64]{1,0:T(8,128)S(1)} %get-tuple-element.5), channel_id=1, source_target_pairs={{0,256},{64,320},{128,384},{192,448},{256,0},{320,64},{384,128},{4... | collective-permute-start | bytes 49160 | tf_op jit(solution)/shard_map/ppermute | solution.py:12
  98.6 0.1 pad_maximum_fusion
  98.7 0.0 copy-start.2
  98.7 1.3 %copy.6 = f32[1024,256]{1,0:T(8,128)} copy(f32[1024,256]{0,1:T(8,128)S(1)} %pad_maximum_fusion) | data formatting | bytes 2097152
  100.0 3.7 %collective-permute-done.9 = f32[64,64]{1,0:T(8,128)S(1)} collective-permute-done((f32[64,64]{1,0:T(8,128)S(1)}, f32[64,64]{1,0:T(8,128)S(1)}, u32[]{:S(2)}, u32[]{:S(2)}) %collective-permute-start.9) | collective-permute-done | bytes 16416 | tf_op jit(solution)/shard_map/ppermute | solution.py:12
  103.7 0.0 copy-done.2
  103.7 0.7 maximum_multiply_fusion
  (12 shorter events, 0.3 us)
Async XLA Ops:
  0.6 0.9 copy-start
  0.6 2.6 %copy-start.1 = (bf16[1024,64]{0,1:T(8,128)(2,1)S(1)}, bf16[1024,64]{0,1:T(8,128)(2,1)}, u32[]{:S(2)}) copy-start(bf16[1024,64]{0,1:T(8,128)(2,1)} %param.5) | copy-start | bytes 393220
  3.3 16.2 %collective-permute-start = (bf16[1024,128]{0,1:T(8,128)(2,1)S(1)}, bf16[1024,128]{0,1:T(8,128)(2,1)S(1)}, u32[]{:S(2)}, u32[]{:S(2)}) collective-permute-start(bf16[1024,128]{0,1:T(8,128)(2,1)S(1)} %pad_maximum_fusion.3), channel_id=1, source_target_pairs={{0,64},{64,0},{128,192},{192,128},{256,320},{320,256},{384,448},{4... | collective-permute-start | bytes 786440 | tf_op jit(solution)/shard_map/ppermute | solution.py:12
  11.1 8.4 %collective-permute-start.2 = (bf16[1024,64]{0,1:T(8,128)(2,1)S(1)}, bf16[1024,64]{0,1:T(8,128)(2,1)S(1)}, u32[]{:S(2)}, u32[]{:S(2)}) collective-permute-start(bf16[1024,64]{0,1:T(8,128)(2,1)S(1)} %get-tuple-element.7), channel_id=1, source_target_pairs={{0,256},{64,320},{128,384},{192,448},{256,0},{320,64},{384,128},{4... | collective-permute-start | bytes 393224 | tf_op jit(solution)/shard_map/ppermute | solution.py:12
  19.6 22.9 %collective-permute-start.3 = (bf16[2048,128]{0,1:T(8,128)(2,1)S(1)}, bf16[2048,128]{0,1:T(8,128)(2,1)S(1)}, u32[]{:S(2)}, u32[]{:S(2)}) collective-permute-start(bf16[2048,128]{0,1:T(8,128)(2,1)S(1)} %pad_maximum_fusion.1), channel_id=1, source_target_pairs={{0,1},{1,0},{2,3},{3,2},{4,5},{5,4},{6,7},{7,6},{8,9},{9,8},{10,11... | collective-permute-start | bytes 1572872 | tf_op jit(solution)/shard_map/ppermute | solution.py:12
  21.6 17.8 %collective-permute-start.1 = (bf16[2048,128]{0,1:T(8,128)(2,1)S(1)}, bf16[2048,128]{0,1:T(8,128)(2,1)}, u32[]{:S(2)}, u32[]{:S(2)}) collective-permute-start(bf16[2048,128]{0,1:T(8,128)(2,1)S(1)} %pad_maximum_fusion.1), channel_id=1, source_target_pairs={{0,128},{64,192},{128,0},{192,64},{256,384},{320,448},{384,256},{4... | collective-permute-start | bytes 1572872 | tf_op jit(solution)/shard_map/ppermute | solution.py:12
  39.4 17.9 %collective-permute-start.4 = (bf16[2048,128]{0,1:T(8,128)(2,1)}, bf16[2048,128]{0,1:T(8,128)(2,1)S(1)}, u32[]{:S(2)}, u32[]{:S(2)}) collective-permute-start(bf16[2048,128]{0,1:T(8,128)(2,1)} %collective-permute-done.1), channel_id=1, source_target_pairs={{0,1},{1,0},{2,3},{3,2},{4,5},{5,4},{6,7},{7,6},{8,9},{9,8},{10,11... | collective-permute-start | bytes 1572872 | tf_op jit(solution)/shard_map/ppermute | solution.py:12
  60.9 17.7 %collective-permute-start.5 = (f32[2,1024,64]{1,2,0:T(8,128)S(1)}, f32[2,1024,64]{1,2,0:T(8,128)S(1)}, u32[]{:S(2)}, u32[]{:S(2)}) collective-permute-start(f32[2,1024,64]{1,2,0:T(8,128)S(1)} %pad_maximum_fusion.2), channel_id=1, source_target_pairs={{0,256},{64,320},{128,384},{192,448},{256,0},{320,64},{384,128},{4... | collective-permute-start | bytes 1572872 | tf_op jit(solution)/shard_map/ppermute | solution.py:12
  63.2 21.3 %collective-permute-start.6 = (f32[64,64]{1,0:T(8,128)S(1)}, f32[64,64]{1,0:T(8,128)S(1)}, u32[]{:S(2)}, u32[]{:S(2)}) collective-permute-start(f32[64,64]{1,0:T(8,128)S(1)} %fusion.71), channel_id=1, source_target_pairs={{0,64},{64,0},{128,192},{192,128},{256,320},{320,256},{384,448},{4... | collective-permute-start | bytes 49160 | tf_op jit(solution)/shard_map/ppermute | solution.py:12
  82.5 6.2 %collective-permute-start.7 = (f32[2,64,64]{2,1,0:T(8,128)S(1)}, f32[2,64,64]{2,1,0:T(8,128)S(1)}, u32[]{:S(2)}, u32[]{:S(2)}) collective-permute-start(f32[2,64,64]{2,1,0:T(8,128)S(1)} %pad_maximum_fusion.4), channel_id=1, source_target_pairs={{0,64},{64,0},{128,192},{192,128},{256,320},{320,256},{384,448},{4... | collective-permute-start | bytes 98312 | tf_op jit(solution)/shard_map/ppermute | solution.py:12
  88.7 7.7 %collective-permute-start.8 = (f32[2,64,64]{2,1,0:T(8,128)S(1)}, f32[2,64,64]{2,1,0:T(8,128)S(1)}, u32[]{:S(2)}, u32[]{:S(2)}) collective-permute-start(f32[2,64,64]{2,1,0:T(8,128)S(1)} %fusion.69), channel_id=1, source_target_pairs={{0,128},{64,192},{128,0},{192,64},{256,384},{320,448},{384,256},{4... | collective-permute-start | bytes 98312 | tf_op jit(solution)/shard_map/ppermute | solution.py:12
  96.4 7.3 %collective-permute-start.9 = (f32[64,64]{1,0:T(8,128)S(1)}, f32[64,64]{1,0:T(8,128)S(1)}, u32[]{:S(2)}, u32[]{:S(2)}) collective-permute-start(f32[64,64]{1,0:T(8,128)S(1)} %get-tuple-element.5), channel_id=1, source_target_pairs={{0,256},{64,320},{128,384},{192,448},{256,0},{320,64},{384,128},{4... | collective-permute-start | bytes 49160 | tf_op jit(solution)/shard_map/ppermute | solution.py:12
  98.7 5.0 %copy-start.2 = (f32[4]{0:T(128)S(1)}, f32[4]{0:T(128)}, u32[]{:S(2)}) copy-start(f32[4]{0:T(128)} %constant.26) | copy-start | bytes 52

commit v6 on v4

--- a/solution.py
+++ b/solution.py
@@ -7,7 +7,10 @@
 
 
 def swapped(value, axis, stride):
-    mask = 2**stride
+    return exchanged(value, axis, 2**stride)
+
+
+def exchanged(value, axis, mask):
     pairs = [(source, source ^ mask) for source in range(lax.axis_size(axis))]
     return lax.ppermute(value, axis, pairs)
 
@@ -47,12 +50,13 @@
     top = leaf_bits - 1
     y_rows = swapped(located, "leaf", top)
     y_sq = squares_of(y_rows)
-    cluster = packed
+    cluster = [packed]
     other_pieces = []
     results = []
     grams = []
     for tier_num in range(top):
-        sib = swapped(cluster, "leaf", tier_num)
+        sibs = [exchanged(packed, "leaf", mask) for mask in range(1 << tier_num, 2 << tier_num)]
+        sib = jnp.concatenate(sibs) if len(sibs) > 1 else sibs[0]
         if tier_num == 0:
             other_pieces.append(swapped(jnp.concatenate([packed, sib]), "pair", 0))
         else:
@@ -60,14 +64,16 @@
         product = raw_product(located, row_sq, sib, dim) / math.sqrt(sib.shape[0])
         results.append(product)
         grams.append(gram_of(product))
-        cluster = jnp.concatenate([cluster, sib])
+        cluster.append(sib)
+    cluster = jnp.concatenate(cluster)
     partner_near = raw_product(y_rows, y_sq, cluster, dim)
     partner_far = None
     for piece in other_pieces:
         part = raw_product(y_rows, y_sq, piece, dim)
         partner_far = part if partner_far is None else partner_far + part
-    back = swapped(jnp.stack([partner_near, partner_far]), "leaf", top)
-    product = back[0] / math.sqrt(cluster.shape[0])
+    back = swapped(jnp.concatenate([partner_near, partner_far], axis=1), "leaf", top)
+    rank = partner_near.shape[1]
+    product = back[:, :rank] / math.sqrt(cluster.shape[0])
     results.append(product)
     grams.append(gram_of(product))
     own_far = None
@@ -76,7 +82,7 @@
         part = raw_product(located, row_sq, piece, dim)
         own_far = part if own_far is None else own_far + part
         far_rows += piece.shape[0]
-    product = (own_far + back[1]) / math.sqrt(2 * far_rows)
+    product = (own_far + back[:, rank:]) / math.sqrt(2 * far_rows)
     results.append(product)
     grams.append(gram_of(product))
     n_tiers = len(grams)

time: 99.2 us -> 97.9 us (0.987)
  the two profiles are of different devices: /device:TPU:504 before, /device:TPU:2 now
where the time goes in v6:
time: 97.9 us; the launch traced here: 97.3 us
  starting transfers between devices  35.9 us (37%)
  matrix products  31 us (32%)
  waiting for transfers between devices  23.8 us (24%)
  other arithmetic  3.39 us (3%)
  local copies, waits for them, and re-layouts  2.27 us (2%)
  between operations  0.98 us (1%)
    ppermute x11, starting transfers between devices, exchanged(): return lax.ppermute(value, axis, pairs)  35.9 us
    dot_general x7, matrix products, raw_product(): return jnp.dot(kernel, col_sketch, preferred_element_type=jnp.float32)  27.9 us
    ppermute x11, waiting for transfers between devices, exchanged(): return lax.ppermute(value, axis, pairs)  23.8 us
    reduce_sum x6, other arithmetic, squares_of(): return jnp.sum(jnp.square(coords.astype(jnp.float32)), axis=-1)  2.33 us
    unnamed x12, local copies, waits for them, and re-layouts  2.24 us
  transfers between devices with their start and end apart: 11, of which 6 were waited for; matrix products, arithmetic and copies ran while one was open for 34% of the time, Pallas kernels for 0%

profile of v6, /device:TPU:2, one launch (start us, length us, event | category | flops | bytes accessed | tf_op | source)
XLA Modules:
  0.0 97.3 jit_solution(1840741756091871736)
XLA Ops:
  0.6 0.0 copy-start
  0.6 0.0 copy-start.1
  0.7 0.9 copy-done
  1.5 1.7 %multiply_reduce_fusion.6 = (f32[1024]{0:T(1024)S(1)}, bf16[1024,64]{0,1:T(8,128)(2,1)S(1)}) fusion(bf16[1024,64]{0,1:T(8,128)(2,1)S(1)} %copy-done, s32[1024]{0:T(1024)} %bitcast.31), kind=kOutput, calls=%fused_computation.42 | convolution fusion | flops 135527424 | bytes 270336 | tf_op jit(solution)/shard_map/dot_general | solution.py:44
  3.3 4.0 %collective-permute-start.1 = (bf16[1024,128]{0,1:T(8,128)(2,1)S(1)}, bf16[1024,128]{0,1:T(8,128)(2,1)S(1)}, u32[]{:S(2)}, u32[]{:S(2)}) collective-permute-start(bf16[1024,128]{0,1:T(8,128)(2,1)S(1)} %pad_maximum_fusion.4), channel_id=1, source_target_pairs={{0,128},{64,192},{128,0},{192,64},{256,384},{320,448},{384,256},{4... | collective-permute-start | bytes 786440 | tf_op jit(solution)/shard_map/ppermute | solution.py:15
  7.3 5.1 %collective-permute-start.3 = (bf16[1024,64]{0,1:T(8,128)(2,1)S(1)}, bf16[1024,64]{0,1:T(8,128)(2,1)S(1)}, u32[]{:S(2)}, u32[]{:S(2)}) collective-permute-start(bf16[1024,64]{0,1:T(8,128)(2,1)S(1)} %get-tuple-element.7), channel_id=1, source_target_pairs={{0,256},{64,320},{128,384},{192,448},{256,0},{320,64},{384,128},{4... | collective-permute-start | bytes 393224 | tf_op jit(solution)/shard_map/ppermute | solution.py:15
  12.4 3.9 %collective-permute-start.2 = (bf16[1024,128]{0,1:T(8,128)(2,1)S(1)}, bf16[1024,128]{0,1:T(8,128)(2,1)S(1)}, u32[]{:S(2)}, u32[]{:S(2)}) collective-permute-start(bf16[1024,128]{0,1:T(8,128)(2,1)S(1)} %pad_maximum_fusion.4), channel_id=1, source_target_pairs={{0,192},{64,128},{128,64},{192,0},{256,448},{320,384},{384,320},{4... | collective-permute-start | bytes 786440 | tf_op jit(solution)/shard_map/ppermute | solution.py:15
  16.4 2.4 %collective-permute-start = (bf16[1024,128]{0,1:T(8,128)(2,1)S(1)}, bf16[1024,128]{0,1:T(8,128)(2,1)S(1)}, u32[]{:S(2)}, u32[]{:S(2)}) collective-permute-start(bf16[1024,128]{0,1:T(8,128)(2,1)S(1)} %pad_maximum_fusion.4), channel_id=1, source_target_pairs={{0,64},{64,0},{128,192},{192,128},{256,320},{320,256},{384,448},{4... | collective-permute-start | bytes 786440 | tf_op jit(solution)/shard_map/ppermute | solution.py:15
  18.9 0.0 collective-permute-done.3
  18.9 0.0 copy-start.2
  18.9 0.0 collective-permute-done.1
  19.0 2.9 %collective-permute-done.2 = bf16[1024,128]{0,1:T(8,128)(2,1)S(1)} collective-permute-done((bf16[1024,128]{0,1:T(8,128)(2,1)S(1)}, bf16[1024,128]{0,1:T(8,128)(2,1)S(1)}, u32[]{:S(2)}, u32[]{:S(2)}) %collective-permute-start.2) | collective-permute-done | bytes 262176 | tf_op jit(solution)/shard_map/ppermute | solution.py:15
  21.8 1.9 %collective-permute-start.5 = (bf16[2048,128]{0,1:T(8,128)(2,1)S(1)}, bf16[2048,128]{0,1:T(8,128)(2,1)}, u32[]{:S(2)}, u32[]{:S(2)}) collective-permute-start(bf16[2048,128]{0,1:T(8,128)(2,1)S(1)} %constant_dynamic-update-slice_fusion), channel_id=1, source_target_pairs={{0,1},{1,0},{2,3},{3,2},{4,5},{5,4},{6,7},{7,6},{8,9},{9,8},{10,11... | collective-permute-start | bytes 1572872 | tf_op jit(solution)/shard_map/ppermute | solution.py:15
  23.8 0.1 multiply_reduce_fusion.3
  23.8 0.8 collective-permute-done
  24.7 0.1 pad_maximum_fusion
  24.7 0.1 multiply_reduce_fusion
  24.9 1.9 %collective-permute-start.4 = (bf16[2048,128]{0,1:T(8,128)(2,1)S(1)}, bf16[2048,128]{0,1:T(8,128)(2,1)}, u32[]{:S(2)}, u32[]{:S(2)}) collective-permute-start(bf16[2048,128]{0,1:T(8,128)(2,1)S(1)} %pad_maximum_fusion.2), channel_id=1, source_target_pairs={{0,1},{1,0},{2,3},{3,2},{4,5},{5,4},{6,7},{7,6},{8,9},{9,8},{10,11... | collective-permute-start | bytes 1572872 | tf_op jit(solution)/shard_map/ppermute | solution.py:15
  26.9 3.2 %fusion.10 = f32[1024,64]{0,1:T(8,128)S(1)} fusion(bf16[1024,64]{0,1:T(8,128)(2,1)S(1)} %get-tuple-element.7, f32[2048]{0:T(1024)S(1)} %multiply_reduce_fusion.3, f32[1024]{0:T(1024)S(1)} %get-tuple-element.6, bf16[2048,128]{0,1:T(8,128)(2,1)S(1)} %constant_dynamic-update-slice_fusion), kind=kOutput, calls=%fused_computation.18 | convolution fusion | flops 549519360 | bytes 929792 | tf_op jit(solution)/shard_map/dot_general | solution.py:31
  30.0 0.4 fusion.59
  30.4 4.5 %collective-permute-start.7 = (f32[64,64]{1,0:T(8,128)S(1)}, f32[64,64]{1,0:T(8,128)S(1)}, u32[]{:S(2)}, u32[]{:S(2)}) collective-permute-start(f32[64,64]{1,0:T(8,128)S(1)} %fusion.59), channel_id=1, source_target_pairs={{0,64},{64,0},{128,192},{192,128},{256,320},{320,256},{384,448},{4... | collective-permute-start | bytes 49160 | tf_op jit(solution)/shard_map/ppermute | solution.py:15
  34.9 6.1 %fusion.2 = f32[1024,64]{0,1:T(8,128)S(1)} fusion(bf16[1024,64]{0,1:T(8,128)(2,1)S(1)} %collective-permute-done.3, f32[4096]{0:T(1024)S(1)} %multiply_reduce_fusion, f32[1024]{0:T(1024)S(1)} %multiply_reduce_fusion.4, bf16[4096,128]{0,1:T(8,128)(2,1)S(1)} %pad_maximum_fusion), kind=kOutput, calls=%fused_computation.10 | convolution fusion | flops 1098907648 | bytes 1462272 | tf_op jit(solution)/shard_map/dot_general | solution.py:31
  41.0 0.0 copy-start.3
  41.0 1.7 %fusion.9 = f32[1024,64]{0,1:T(8,128)S(1)} fusion(bf16[1024,64]{0,1:T(8,128)(2,1)S(1)} %get-tuple-element.7, f32[1024]{0:T(1024)S(1)} %multiply_reduce_fusion.5, f32[1024]{0:T(1024)S(1)} %get-tuple-element.6, bf16[1024,128]{0,1:T(8,128)(2,1)S(1)} %collective-permute-done), kind=kOutput, calls=%fused_computation.17 | convolution fusion | flops 274792448 | bytes 663552 | tf_op jit(solution)/shard_map/dot_general | solution.py:31
  42.7 0.0 collective-permute-done.5
  42.8 1.0 %multiply_reduce_fusion.1 = f32[2048]{0:T(1024)S(1)} fusion(bf16[2048,128]{0,1:T(8,128)(2,1)} %collective-permute-done.5), kind=kLoop, calls=%fused_computation.33 | loop fusion | flops 391168 | bytes 270336 | tf_op jit(solution)/shard_map/reduce_sum | solution.py:19
  43.8 4.2 %fusion.5 = f32[1024,64]{0,1:T(8,128)S(1)} fusion(bf16[1024,64]{0,1:T(8,128)(2,1)S(1)} %copy-done.3, f32[2048]{0:T(1024)S(1)} %multiply_reduce_fusion.1, f32[1024]{0:T(1024)S(1)} %multiply_reduce_fusion.4, bf16[2048,128]{0,1:T(8,128)(2,1)} %collective-permute-done.5), kind=kOutput, calls=%fused_computation.13 | convolution fusion | flops 549453824 | bytes 929792 | tf_op jit(solution)/shard_map/dot_general | solution.py:31
  48.0 0.0 collective-permute-done.4
  48.0 1.0 %multiply_reduce_fusion.2 = f32[2048]{0:T(1024)S(1)} fusion(bf16[2048,128]{0,1:T(8,128)(2,1)} %collective-permute-done.4), kind=kLoop, calls=%fused_computation.34 | loop fusion | flops 391168 | bytes 270336 | tf_op jit(solution)/shard_map/reduce_sum | solution.py:19
  49.0 4.4 %fusion.14 = f32[1024,64]{0,1:T(8,128)S(1)} fusion(f32[1024,64]{0,1:T(8,128)S(1)} %fusion.5, bf16[1024,64]{0,1:T(8,128)(2,1)S(1)} %copy-done.3, f32[2048]{0:T(1024)S(1)} %multiply_reduce_fusion.2, f32[1024]{0:T(1024)S(1)} %multiply_reduce_fusion.4, bf16[2048,128]{0,1:T(8,128)(2,1)} %collective-permute-done.4), kind=kOutput, calls=%fused_computation.22 | convolution fusion | flops 549519360 | bytes 1191936 | tf_op jit(solution)/shard_map/dot_general | solution.py:31
  53.4 3.4 %collective-permute-start.6 = (f32[1024,128]{0,1:T(8,128)S(1)}, f32[1024,128]{0,1:T(8,128)S(1)}, u32[]{:S(2)}, u32[]{:S(2)}) collective-permute-start(f32[1024,128]{0,1:T(8,128)S(1)} %pad_maximum_fusion.3), channel_id=1, source_target_pairs={{0,256},{64,320},{128,384},{192,448},{256,0},{320,64},{384,128},{4... | collective-permute-start | bytes 1572872 | tf_op jit(solution)/shard_map/ppermute | solution.py:15
  56.8 0.4 convolution_bitcast_fusion.2
  57.2 4.2 %fusion.7 = f32[1024,64]{0,1:T(8,128)S(1)} fusion(bf16[1024,64]{0,1:T(8,128)(2,1)S(1)} %get-tuple-element.7, f32[2048]{0:T(1024)S(1)} %multiply_reduce_fusion.1, f32[1024]{0:T(1024)S(1)} %get-tuple-element.6, bf16[2048,128]{0,1:T(8,128)(2,1)} %collective-permute-done.5), kind=kOutput, calls=%fused_computation.15 | convolution fusion | flops 549453824 | bytes 929792 | tf_op jit(solution)/shard_map/dot_general | solution.py:31
  61.4 9.0 %collective-permute-done.6 = f32[1024,128]{0,1:T(8,128)S(1)} collective-permute-done((f32[1024,128]{0,1:T(8,128)S(1)}, f32[1024,128]{0,1:T(8,128)S(1)}, u32[]{:S(2)}, u32[]{:S(2)}) %collective-permute-start.6) | collective-permute-done | bytes 524320 | tf_op jit(solution)/shard_map/ppermute | solution.py:15
  70.4 4.2 %fusion.13 = f32[1024,64]{0,1:T(8,128)S(1)} fusion(f32[1024,64]{0,1:T(8,128)S(1)} %fusion.7, bf16[1024,64]{0,1:T(8,128)(2,1)S(1)} %get-tuple-element.7, f32[2048]{0:T(1024)S(1)} %multiply_reduce_fusion.2, f32[1024]{0:T(1024)S(1)} %get-tuple-element.6, f32[1024,128]{0,1:T(8,128)S(1)} %collective-permute-done.6, bf16[2048,128]{0,1:T(8,128)(2,1)} %collective-permute-done.4), kind=kOutput, calls=%fused_computation.21 | convolution fusion | flops 549650432 | bytes 1454080 | tf_op jit(solution)/shard_map/dot_general | solution.py:31
  74.6 0.4 convolution_bitcast_fusion
  75.0 0.4 convolution_bitcast_fusion.1
  75.4 2.3 %collective-permute-start.8 = (f32[2,64,64]{2,1,0:T(8,128)S(1)}, f32[2,64,64]{2,1,0:T(8,128)S(1)}, u32[]{:S(2)}, u32[]{:S(2)}) collective-permute-start(f32[2,64,64]{2,1,0:T(8,128)S(1)} %pad_maximum_fusion.5), channel_id=1, source_target_pairs={{0,64},{64,0},{128,192},{192,128},{256,320},{320,256},{384,448},{4... | collective-permute-start | bytes 98312 | tf_op jit(solution)/shard_map/ppermute | solution.py:15
  77.6 0.0 collective-permute-done.7
  77.7 3.9 %collective-permute-done.8 = f32[2,64,64]{2,1,0:T(8,128)S(1)} collective-permute-done((f32[2,64,64]{2,1,0:T(8,128)S(1)}, f32[2,64,64]{2,1,0:T(8,128)S(1)}, u32[]{:S(2)}, u32[]{:S(2)}) %collective-permute-start.8) | collective-permute-done | bytes 32800 | tf_op jit(solution)/shard_map/ppermute | solution.py:15
  81.5 2.6 %collective-permute-start.9 = (f32[2,64,64]{2,1,0:T(8,128)S(1)}, f32[2,64,64]{2,1,0:T(8,128)S(1)}, u32[]{:S(2)}, u32[]{:S(2)}) collective-permute-start(f32[2,64,64]{2,1,0:T(8,128)S(1)} %fusion.58), channel_id=1, source_target_pairs={{0,128},{64,192},{128,0},{192,64},{256,384},{320,448},{384,256},{4... | collective-permute-start | bytes 98312 | tf_op jit(solution)/shard_map/ppermute | solution.py:15
  84.1 5.1 %collective-permute-done.9 = f32[2,64,64]{2,1,0:T(8,128)S(1)} collective-permute-done((f32[2,64,64]{2,1,0:T(8,128)S(1)}, f32[2,64,64]{2,1,0:T(8,128)S(1)}, u32[]{:S(2)}, u32[]{:S(2)}) %collective-permute-start.9) | collective-permute-done | bytes 32800 | tf_op jit(solution)/shard_map/ppermute | solution.py:15
  89.2 3.8 %collective-permute-start.10 = (f32[64,64]{1,0:T(8,128)S(1)}, f32[64,64]{1,0:T(8,128)S(1)}, u32[]{:S(2)}, u32[]{:S(2)}) collective-permute-start(f32[64,64]{1,0:T(8,128)S(1)} %get-tuple-element.5), channel_id=1, source_target_pairs={{0,256},{64,320},{128,384},{192,448},{256,0},{320,64},{384,128},{4... | collective-permute-start | bytes 49160 | tf_op jit(solution)/shard_map/ppermute | solution.py:15
  93.0 0.1 pad_maximum_fusion.1
  93.1 0.0 copy-start.4
  93.1 1.3 %copy.6 = f32[1024,256]{1,0:T(8,128)} copy(f32[1024,256]{0,1:T(8,128)S(1)} %pad_maximum_fusion.1) | data formatting | bytes 2097152
  94.4 2.1 %collective-permute-done.10 = f32[64,64]{1,0:T(8,128)S(1)} collective-permute-done((f32[64,64]{1,0:T(8,128)S(1)}, f32[64,64]{1,0:T(8,128)S(1)}, u32[]{:S(2)}, u32[]{:S(2)}) %collective-permute-start.10) | collective-permute-done | bytes 16416 | tf_op jit(solution)/shard_map/ppermute | solution.py:15
  96.6 0.7 maximum_multiply_fusion
  (18 shorter events, 0.3 us)
Async XLA Ops:
  0.6 0.9 copy-start
  0.6 2.6 %copy-start.1 = (bf16[1024,64]{0,1:T(8,128)(2,1)S(1)}, bf16[1024,64]{0,1:T(8,128)(2,1)}, u32[]{:S(2)}) copy-start(bf16[1024,64]{0,1:T(8,128)(2,1)} %param.5) | copy-start | bytes 393220
  3.3 15.6 %collective-permute-start.1 = (bf16[1024,128]{0,1:T(8,128)(2,1)S(1)}, bf16[1024,128]{0,1:T(8,128)(2,1)S(1)}, u32[]{:S(2)}, u32[]{:S(2)}) collective-permute-start(bf16[1024,128]{0,1:T(8,128)(2,1)S(1)} %pad_maximum_fusion.4), channel_id=1, source_target_pairs={{0,128},{64,192},{128,0},{192,64},{256,384},{320,448},{384,256},{4... | collective-permute-start | bytes 786440 | tf_op jit(solution)/shard_map/ppermute | solution.py:15
  7.3 11.5 %collective-permute-start.3 = (bf16[1024,64]{0,1:T(8,128)(2,1)S(1)}, bf16[1024,64]{0,1:T(8,128)(2,1)S(1)}, u32[]{:S(2)}, u32[]{:S(2)}) collective-permute-start(bf16[1024,64]{0,1:T(8,128)(2,1)S(1)} %get-tuple-element.7), channel_id=1, source_target_pairs={{0,256},{64,320},{128,384},{192,448},{256,0},{320,64},{384,128},{4... | collective-permute-start | bytes 393224 | tf_op jit(solution)/shard_map/ppermute | solution.py:15
  12.4 9.4 %collective-permute-start.2 = (bf16[1024,128]{0,1:T(8,128)(2,1)S(1)}, bf16[1024,128]{0,1:T(8,128)(2,1)S(1)}, u32[]{:S(2)}, u32[]{:S(2)}) collective-permute-start(bf16[1024,128]{0,1:T(8,128)(2,1)S(1)} %pad_maximum_fusion.4), channel_id=1, source_target_pairs={{0,192},{64,128},{128,64},{192,0},{256,448},{320,384},{384,320},{4... | collective-permute-start | bytes 786440 | tf_op jit(solution)/shard_map/ppermute | solution.py:15
  16.4 8.3 %collective-permute-start = (bf16[1024,128]{0,1:T(8,128)(2,1)S(1)}, bf16[1024,128]{0,1:T(8,128)(2,1)S(1)}, u32[]{:S(2)}, u32[]{:S(2)}) collective-permute-start(bf16[1024,128]{0,1:T(8,128)(2,1)S(1)} %pad_maximum_fusion.4), channel_id=1, source_target_pairs={{0,64},{64,0},{128,192},{192,128},{256,320},{320,256},{384,448},{4... | collective-permute-start | bytes 786440 | tf_op jit(solution)/shard_map/ppermute | solution.py:15
  18.9 16.0 %copy-start.2 = (bf16[1024,64]{0,1:T(8,128)(2,1)}, bf16[1024,64]{0,1:T(8,128)(2,1)S(1)}, u32[]{:S(2)}) copy-start(bf16[1024,64]{0,1:T(8,128)(2,1)S(1)} %collective-permute-done.3) | copy-start | bytes 393220
  21.8 20.9 %collective-permute-start.5 = (bf16[2048,128]{0,1:T(8,128)(2,1)S(1)}, bf16[2048,128]{0,1:T(8,128)(2,1)}, u32[]{:S(2)}, u32[]{:S(2)}) collective-permute-start(bf16[2048,128]{0,1:T(8,128)(2,1)S(1)} %constant_dynamic-update-slice_fusion), channel_id=1, source_target_pairs={{0,1},{1,0},{2,3},{3,2},{4,5},{5,4},{6,7},{7,6},{8,9},{9,8},{10,11... | collective-permute-start | bytes 1572872 | tf_op jit(solution)/shard_map/ppermute | solution.py:15
  24.9 23.0 %collective-permute-start.4 = (bf16[2048,128]{0,1:T(8,128)(2,1)S(1)}, bf16[2048,128]{0,1:T(8,128)(2,1)}, u32[]{:S(2)}, u32[]{:S(2)}) collective-permute-start(bf16[2048,128]{0,1:T(8,128)(2,1)S(1)} %pad_maximum_fusion.2), channel_id=1, source_target_pairs={{0,1},{1,0},{2,3},{3,2},{4,5},{5,4},{6,7},{7,6},{8,9},{9,8},{10,11... | collective-permute-start | bytes 1572872 | tf_op jit(solution)/shard_map/ppermute | solution.py:15
  30.4 47.3 %collective-permute-start.7 = (f32[64,64]{1,0:T(8,128)S(1)}, f32[64,64]{1,0:T(8,128)S(1)}, u32[]{:S(2)}, u32[]{:S(2)}) collective-permute-start(f32[64,64]{1,0:T(8,128)S(1)} %fusion.59), channel_id=1, source_target_pairs={{0,64},{64,0},{128,192},{192,128},{256,320},{320,256},{384,448},{4... | collective-permute-start | bytes 49160 | tf_op jit(solution)/shard_map/ppermute | solution.py:15
  41.0 2.7 %copy-start.3 = (bf16[1024,64]{0,1:T(8,128)(2,1)S(1)}, bf16[1024,64]{0,1:T(8,128)(2,1)}, u32[]{:S(2)}) copy-start(bf16[1024,64]{0,1:T(8,128)(2,1)} %copy-done.2) | copy-start | bytes 393220
  53.4 17.0 %collective-permute-start.6 = (f32[1024,128]{0,1:T(8,128)S(1)}, f32[1024,128]{0,1:T(8,128)S(1)}, u32[]{:S(2)}, u32[]{:S(2)}) collective-permute-start(f32[1024,128]{0,1:T(8,128)S(1)} %pad_maximum_fusion.3), channel_id=1, source_target_pairs={{0,256},{64,320},{128,384},{192,448},{256,0},{320,64},{384,128},{4... | collective-permute-start | bytes 1572872 | tf_op jit(solution)/shard_map/ppermute | solution.py:15
  75.4 6.2 %collective-permute-start.8 = (f32[2,64,64]{2,1,0:T(8,128)S(1)}, f32[2,64,64]{2,1,0:T(8,128)S(1)}, u32[]{:S(2)}, u32[]{:S(2)}) collective-permute-start(f32[2,64,64]{2,1,0:T(8,128)S(1)} %pad_maximum_fusion.5), channel_id=1, source_target_pairs={{0,64},{64,0},{128,192},{192,128},{256,320},{320,256},{384,448},{4... | collective-permute-start | bytes 98312 | tf_op jit(solution)/shard_map/ppermute | solution.py:15
  81.5 7.7 %collective-permute-start.9 = (f32[2,64,64]{2,1,0:T(8,128)S(1)}, f32[2,64,64]{2,1,0:T(8,128)S(1)}, u32[]{:S(2)}, u32[]{:S(2)}) collective-permute-start(f32[2,64,64]{2,1,0:T(8,128)S(1)} %fusion.58), channel_id=1, source_target_pairs={{0,128},{64,192},{128,0},{192,64},{256,384},{320,448},{384,256},{4... | collective-permute-start | bytes 98312 | tf_op jit(solution)/shard_map/ppermute | solution.py:15
  89.2 7.3 %collective-permute-start.10 = (f32[64,64]{1,0:T(8,128)S(1)}, f32[64,64]{1,0:T(8,128)S(1)}, u32[]{:S(2)}, u32[]{:S(2)}) collective-permute-start(f32[64,64]{1,0:T(8,128)S(1)} %get-tuple-element.5), channel_id=1, source_target_pairs={{0,256},{64,320},{128,384},{192,448},{256,0},{320,64},{384,128},{4... | collective-permute-start | bytes 49160 | tf_op jit(solution)/shard_map/ppermute | solution.py:15
  93.1 3.4 %copy-start.4 = (f32[4]{0:T(128)S(1)}, f32[4]{0:T(128)}, u32[]{:S(2)}) copy-start(f32[4]{0:T(128)} %constant.7) | copy-start | bytes 52

commit v7 on v6

--- a/solution.py
+++ b/solution.py
@@ -37,7 +37,7 @@
     )
 
 
-def per_device(points, sketch_matrix, leaf_order):
+def device_body(points, sketch_matrix, leaf_order):
     dim = points.shape[1]
     rows_n = points.shape[0]
     picks = leaf_order[0][:, None] == jnp.arange(rows_n, dtype=leaf_order.dtype)[None, :]
@@ -57,15 +57,12 @@
     for tier_num in range(top):
         sibs = [exchanged(packed, "leaf", mask) for mask in range(1 << tier_num, 2 << tier_num)]
         sib = jnp.concatenate(sibs) if len(sibs) > 1 else sibs[0]
-        if tier_num == 0:
-            other_pieces.append(swapped(jnp.concatenate([packed, sib]), "pair", 0))
-        else:
-            other_pieces.append(swapped(sib, "pair", 0))
         product = raw_product(located, row_sq, sib, dim) / math.sqrt(sib.shape[0])
         results.append(product)
         grams.append(gram_of(product))
         cluster.append(sib)
     cluster = jnp.concatenate(cluster)
+    other_pieces = [swapped(cluster, "pair", 0)]
     partner_near = raw_product(y_rows, y_sq, cluster, dim)
     partner_far = None
     for piece in other_pieces:
@@ -79,7 +76,7 @@
     own_far = None
     far_rows = 0
     for piece in other_pieces:
-        part = raw_product(located, row_sq, piece, dim)
+        part = lax.optimization_barrier(raw_product(located, row_sq, piece, dim))
         own_far = part if own_far is None else own_far + part
         far_rows += piece.shape[0]
     product = (own_far + back[:, rank:]) / math.sqrt(2 * far_rows)
@@ -115,5 +112,5 @@
     in_specs = (P(axes, None), P(axes, None), P(axes, None))
     out_specs = (P(axes, None), P(axes, None, None, None))
     return jax.shard_map(
-        per_device, mesh=fine, in_specs=in_specs, out_specs=out_specs, check_vma=False
+        device_body, mesh=fine, in_specs=in_specs, out_specs=out_specs, check_vma=False
     )

time: 97.9 us -> 88.8 us (0.907)
  the two profiles are of different devices: /device:TPU:2 before, /device:TPU:416 now
where the time goes in v7:
time: 88.8 us; the launch traced here: 88.2 us
  starting transfers between devices  31 us (35%)
  matrix products  28.8 us (32%)
  waiting for transfers between devices  22.7 us (26%)
  other arithmetic  2.52 us (3%)
  local copies, waits for them, and re-layouts  2.25 us (3%)
  between operations  0.93 us (1%)
    ppermute x10, starting transfers between devices, exchanged(): return lax.ppermute(value, axis, pairs)  31 us
    dot_general x5, matrix products, raw_product(): return jnp.dot(kernel, col_sketch, preferred_element_type=jnp.float32)  25.7 us
    ppermute x10, waiting for transfers between devices, exchanged(): return lax.ppermute(value, axis, pairs)  22.7 us
    unnamed x8, local copies, waits for them, and re-layouts  2.23 us
  transfers between devices with their start and end apart: 10, of which 5 were waited for; matrix products, arithmetic and copies ran while one was open for 23% of the time, Pallas kernels for 0%

profile of v7, /device:TPU:416, one launch (start us, length us, event | category | flops | bytes accessed | tf_op | source)
XLA Modules:
  0.0 88.2 jit_solution(7173551850897541207)
XLA Ops:
  0.6 0.0 copy-start
  0.6 0.0 copy-start.1
  0.7 0.9 %copy-done = bf16[1024,64]{0,1:T(8,128)(2,1)S(1)} copy-done((bf16[1024,64]{0,1:T(8,128)(2,1)S(1)}, bf16[1024,64]{0,1:T(8,128)(2,1)}, u32[]{:S(2)}) %copy-start) | copy-done | bytes 131096
  1.5 1.7 %multiply_reduce_fusion.5 = (f32[1024]{0:T(1024)S(1)}, bf16[1024,64]{0,1:T(8,128)(2,1)S(1)}) fusion(bf16[1024,64]{0,1:T(8,128)(2,1)S(1)} %copy-done, s32[1024]{0:T(1024)} %bitcast.29), kind=kOutput, calls=%fused_computation.38 | convolution fusion | flops 135527424 | bytes 270336 | tf_op jit(solution)/shard_map/dot_general | solution.py:44
  3.3 0.0 copy-done.1
  3.3 4.9 %collective-permute-start.1 = (bf16[1024,128]{0,1:T(8,128)(2,1)S(1)}, bf16[1024,128]{0,1:T(8,128)(2,1)S(1)}, u32[]{:S(2)}, u32[]{:S(2)}) collective-permute-start(bf16[1024,128]{0,1:T(8,128)(2,1)S(1)} %pad_maximum_fusion.3), channel_id=1, source_target_pairs={{0,128},{64,192},{128,0},{192,64},{256,384},{320,448},{384,256},{4... | collective-permute-start | bytes 786440 | tf_op jit(solution)/shard_map/ppermute | solution.py:15
  8.2 5.1 %collective-permute-start.3 = (bf16[1024,64]{0,1:T(8,128)(2,1)S(1)}, bf16[1024,64]{0,1:T(8,128)(2,1)S(1)}, u32[]{:S(2)}, u32[]{:S(2)}) collective-permute-start(bf16[1024,64]{0,1:T(8,128)(2,1)S(1)} %get-tuple-element.9), channel_id=1, source_target_pairs={{0,256},{64,320},{128,384},{192,448},{256,0},{320,64},{384,128},{4... | collective-permute-start | bytes 393224 | tf_op jit(solution)/shard_map/ppermute | solution.py:15
  13.3 3.1 %collective-permute-start.2 = (bf16[1024,128]{0,1:T(8,128)(2,1)S(1)}, bf16[1024,128]{0,1:T(8,128)(2,1)S(1)}, u32[]{:S(2)}, u32[]{:S(2)}) collective-permute-start(bf16[1024,128]{0,1:T(8,128)(2,1)S(1)} %pad_maximum_fusion.3), channel_id=1, source_target_pairs={{0,192},{64,128},{128,64},{192,0},{256,448},{320,384},{384,320},{4... | collective-permute-start | bytes 786440 | tf_op jit(solution)/shard_map/ppermute | solution.py:15
  16.4 1.9 %collective-permute-start = (bf16[1024,128]{0,1:T(8,128)(2,1)S(1)}, bf16[1024,128]{0,1:T(8,128)(2,1)S(1)}, u32[]{:S(2)}, u32[]{:S(2)}) collective-permute-start(bf16[1024,128]{0,1:T(8,128)(2,1)S(1)} %pad_maximum_fusion.3), channel_id=1, source_target_pairs={{0,64},{64,0},{128,192},{192,128},{256,320},{320,256},{384,448},{4... | collective-permute-start | bytes 786440 | tf_op jit(solution)/shard_map/ppermute | solution.py:15
  18.3 0.0 collective-permute-done.3
  18.4 0.0 collective-permute-done.1
  18.4 5.5 %collective-permute-done.2 = bf16[1024,128]{0,1:T(8,128)(2,1)S(1)} collective-permute-done((bf16[1024,128]{0,1:T(8,128)(2,1)S(1)}, bf16[1024,128]{0,1:T(8,128)(2,1)S(1)}, u32[]{:S(2)}, u32[]{:S(2)}) %collective-permute-start.2) | collective-permute-done | bytes 262176 | tf_op jit(solution)/shard_map/ppermute | solution.py:15
  24.0 0.1 multiply_reduce_fusion.2
  24.0 1.5 %collective-permute-done = bf16[1024,128]{0,1:T(8,128)(2,1)S(1)} collective-permute-done((bf16[1024,128]{0,1:T(8,128)(2,1)S(1)}, bf16[1024,128]{0,1:T(8,128)(2,1)S(1)}, u32[]{:S(2)}, u32[]{:S(2)}) %collective-permute-start) | collective-permute-done | bytes 262176 | tf_op jit(solution)/shard_map/ppermute | solution.py:15
  25.5 0.1 pad_maximum_fusion
  25.6 1.9 %collective-permute-start.4 = (bf16[4096,128]{0,1:T(8,128)(2,1)S(1)}, bf16[4096,128]{0,1:T(8,128)(2,1)}, u32[]{:S(2)}, u32[]{:S(2)}) collective-permute-start(bf16[4096,128]{0,1:T(8,128)(2,1)S(1)} %pad_maximum_fusion), channel_id=1, source_target_pairs={{0,1},{1,0},{2,3},{3,2},{4,5},{5,4},{6,7},{7,6},{8,9},{9,8},{10,11... | collective-permute-start | bytes 3145736 | tf_op jit(solution)/shard_map/ppermute | solution.py:15
  27.5 3.2 %fusion.8 = f32[1024,64]{0,1:T(8,128)S(1)} fusion(bf16[1024,64]{0,1:T(8,128)(2,1)S(1)} %get-tuple-element.9, f32[2048]{0:T(1024)S(1)} %multiply_reduce_fusion.2, f32[1024]{0:T(1024)S(1)} %get-tuple-element.8, bf16[2048,128]{0,1:T(8,128)(2,1)S(1)} %constant_dynamic-update-slice_fusion), kind=kOutput, calls=%fused_computation.14 | convolution fusion | flops 549519360 | bytes 929792 | tf_op jit(solution)/shard_map/dot_general | solution.py:31
  30.7 1.7 %fusion.7 = f32[1024,64]{0,1:T(8,128)S(1)} fusion(bf16[1024,64]{0,1:T(8,128)(2,1)S(1)} %get-tuple-element.9, f32[1024]{0:T(1024)S(1)} %multiply_reduce_fusion.4, f32[1024]{0:T(1024)S(1)} %get-tuple-element.8, bf16[1024,128]{0,1:T(8,128)(2,1)S(1)} %collective-permute-done), kind=kOutput, calls=%fused_computation.13 | convolution fusion | flops 274792448 | bytes 663552 | tf_op jit(solution)/shard_map/dot_general | solution.py:31
  32.4 0.4 fusion.42
  32.8 0.1 multiply_reduce_fusion.1
  32.9 6.1 %fusion.2 = f32[1024,64]{0,1:T(8,128)S(1)} fusion(bf16[1024,64]{0,1:T(8,128)(2,1)S(1)} %collective-permute-done.3, f32[4096]{0:T(1024)S(1)} %multiply_reduce_fusion.1, f32[1024]{0:T(1024)S(1)} %multiply_reduce_fusion.3, bf16[4096,128]{0,1:T(8,128)(2,1)S(1)} %pad_maximum_fusion), kind=kOutput, calls=%fused_computation.8 | convolution fusion | flops 1098907648 | bytes 1462272 | tf_op jit(solution)/shard_map/dot_general | solution.py:31
  39.0 0.0 collective-permute-done.4
  39.0 1.2 %multiply_reduce_fusion = f32[4096]{0:T(1024)S(1)} fusion(bf16[4096,128]{0,1:T(8,128)(2,1)} %collective-permute-done.4), kind=kLoop, calls=%fused_computation.21 | loop fusion | flops 782336 | bytes 540672 | tf_op jit(solution)/shard_map/reduce_sum | solution.py:19
  40.2 7.5 %fusion.3 = f32[1024,64]{0,1:T(8,128)S(1)} fusion(bf16[1024,64]{0,1:T(8,128)(2,1)S(1)} %collective-permute-done.3, f32[4096]{0:T(1024)S(1)} %multiply_reduce_fusion, f32[1024]{0:T(1024)S(1)} %multiply_reduce_fusion.3, bf16[4096,128]{0,1:T(8,128)(2,1)} %collective-permute-done.4), kind=kOutput, calls=%fused_computation.9 | convolution fusion | flops 1098907648 | bytes 1462272 | tf_op jit(solution)/shard_map/dot_general | solution.py:31
  47.7 2.2 %collective-permute-start.5 = (f32[1024,128]{0,1:T(8,128)S(1)}, f32[1024,128]{0,1:T(8,128)S(1)}, u32[]{:S(2)}, u32[]{:S(2)}) collective-permute-start(f32[1024,128]{0,1:T(8,128)S(1)} %pad_maximum_fusion.2), channel_id=1, source_target_pairs={{0,256},{64,320},{128,384},{192,448},{256,0},{320,64},{384,128},{4... | collective-permute-start | bytes 1572872 | tf_op jit(solution)/shard_map/ppermute | solution.py:15
  49.9 7.3 %fusion.4 = f32[1024,64]{0,1:T(8,128)S(1)} fusion(bf16[1024,64]{0,1:T(8,128)(2,1)S(1)} %get-tuple-element.9, f32[1024]{0:T(1024)S(1)} %get-tuple-element.8, f32[4096]{0:T(1024)S(1)} %multiply_reduce_fusion, bf16[4096,128]{0,1:T(8,128)(2,1)} %collective-permute-done.4), kind=kOutput, calls=%fused_computation.10 | convolution fusion | flops 1098907648 | bytes 1462272 | tf_op jit(solution)/shard_map/dot_general | solution.py:31
  57.2 8.2 %collective-permute-done.5 = f32[1024,128]{0,1:T(8,128)S(1)} collective-permute-done((f32[1024,128]{0,1:T(8,128)S(1)}, f32[1024,128]{0,1:T(8,128)S(1)}, u32[]{:S(2)}, u32[]{:S(2)}) %collective-permute-start.5) | collective-permute-done | bytes 524320 | tf_op jit(solution)/shard_map/ppermute | solution.py:15
  65.4 0.1 slice_multiply_fusion
  65.5 0.4 convolution_bitcast_fusion
  65.9 0.4 convolution_bitcast_fusion.1
  66.2 2.2 %collective-permute-start.7 = (f32[2,64,64]{2,1,0:T(8,128)S(1)}, f32[2,64,64]{2,1,0:T(8,128)S(1)}, u32[]{:S(2)}, u32[]{:S(2)}) collective-permute-start(f32[2,64,64]{2,1,0:T(8,128)S(1)} %pad_maximum_fusion.4), channel_id=1, source_target_pairs={{0,64},{64,0},{128,192},{192,128},{256,320},{320,256},{384,448},{4... | collective-permute-start | bytes 98312 | tf_op jit(solution)/shard_map/ppermute | solution.py:15
  68.4 0.4 convolution_bitcast_fusion.2
  68.8 3.6 %collective-permute-start.6 = (f32[64,64]{1,0:T(8,128)S(1)}, f32[64,64]{1,0:T(8,128)S(1)}, u32[]{:S(2)}, u32[]{:S(2)}) collective-permute-start(f32[64,64]{1,0:T(8,128)S(1)} %fusion.42), channel_id=1, source_target_pairs={{0,64},{64,0},{128,192},{192,128},{256,320},{320,256},{384,448},{4... | collective-permute-start | bytes 49160 | tf_op jit(solution)/shard_map/ppermute | solution.py:15
  72.5 0.0 collective-permute-done.7
  72.5 3.7 %collective-permute-start.8 = (f32[2,64,64]{2,1,0:T(8,128)S(1)}, f32[2,64,64]{2,1,0:T(8,128)S(1)}, u32[]{:S(2)}, u32[]{:S(2)}) collective-permute-start(f32[2,64,64]{2,1,0:T(8,128)S(1)} %fusion.41), channel_id=1, source_target_pairs={{0,128},{64,192},{128,0},{192,64},{256,384},{320,448},{384,256},{4... | collective-permute-start | bytes 98312 | tf_op jit(solution)/shard_map/ppermute | solution.py:15
  76.2 0.0 collective-permute-done.6
  76.3 3.9 %collective-permute-done.8 = f32[2,64,64]{2,1,0:T(8,128)S(1)} collective-permute-done((f32[2,64,64]{2,1,0:T(8,128)S(1)}, f32[2,64,64]{2,1,0:T(8,128)S(1)}, u32[]{:S(2)}, u32[]{:S(2)}) %collective-permute-start.8) | collective-permute-done | bytes 32800 | tf_op jit(solution)/shard_map/ppermute | solution.py:15
  80.2 2.2 %collective-permute-start.9 = (f32[64,64]{1,0:T(8,128)S(1)}, f32[64,64]{1,0:T(8,128)S(1)}, u32[]{:S(2)}, u32[]{:S(2)}) collective-permute-start(f32[64,64]{1,0:T(8,128)S(1)} %get-tuple-element.7), channel_id=1, source_target_pairs={{0,256},{64,320},{128,384},{192,448},{256,0},{320,64},{384,128},{4... | collective-permute-start | bytes 49160 | tf_op jit(solution)/shard_map/ppermute | solution.py:15
  82.4 0.1 pad_maximum_fusion.1
  82.5 0.0 copy-start.2
  82.5 1.3 %copy.6 = f32[1024,256]{1,0:T(8,128)} copy(f32[1024,256]{0,1:T(8,128)S(1)} %pad_maximum_fusion.1) | data formatting | bytes 2097152
  83.8 3.7 %collective-permute-done.9 = f32[64,64]{1,0:T(8,128)S(1)} collective-permute-done((f32[64,64]{1,0:T(8,128)S(1)}, f32[64,64]{1,0:T(8,128)S(1)}, u32[]{:S(2)}, u32[]{:S(2)}) %collective-permute-start.9) | collective-permute-done | bytes 16416 | tf_op jit(solution)/shard_map/ppermute | solution.py:15
  87.5 0.0 copy-done.2
  87.5 0.7 maximum_multiply_fusion
  (12 shorter events, 0.2 us)
Async XLA Ops:
  0.6 0.9 %copy-start = (bf16[1024,64]{0,1:T(8,128)(2,1)S(1)}, bf16[1024,64]{0,1:T(8,128)(2,1)}, u32[]{:S(2)}) copy-start(bf16[1024,64]{0,1:T(8,128)(2,1)} %param.4) | copy-start | bytes 393220
  0.6 2.6 %copy-start.1 = (bf16[1024,64]{0,1:T(8,128)(2,1)S(1)}, bf16[1024,64]{0,1:T(8,128)(2,1)}, u32[]{:S(2)}) copy-start(bf16[1024,64]{0,1:T(8,128)(2,1)} %param.5) | copy-start | bytes 393220
  3.3 15.1 %collective-permute-start.1 = (bf16[1024,128]{0,1:T(8,128)(2,1)S(1)}, bf16[1024,128]{0,1:T(8,128)(2,1)S(1)}, u32[]{:S(2)}, u32[]{:S(2)}) collective-permute-start(bf16[1024,128]{0,1:T(8,128)(2,1)S(1)} %pad_maximum_fusion.3), channel_id=1, source_target_pairs={{0,128},{64,192},{128,0},{192,64},{256,384},{320,448},{384,256},{4... | collective-permute-start | bytes 786440 | tf_op jit(solution)/shard_map/ppermute | solution.py:15
  8.2 10.1 %collective-permute-start.3 = (bf16[1024,64]{0,1:T(8,128)(2,1)S(1)}, bf16[1024,64]{0,1:T(8,128)(2,1)S(1)}, u32[]{:S(2)}, u32[]{:S(2)}) collective-permute-start(bf16[1024,64]{0,1:T(8,128)(2,1)S(1)} %get-tuple-element.9), channel_id=1, source_target_pairs={{0,256},{64,320},{128,384},{192,448},{256,0},{320,64},{384,128},{4... | collective-permute-start | bytes 393224 | tf_op jit(solution)/shard_map/ppermute | solution.py:15
  13.3 10.6 %collective-permute-start.2 = (bf16[1024,128]{0,1:T(8,128)(2,1)S(1)}, bf16[1024,128]{0,1:T(8,128)(2,1)S(1)}, u32[]{:S(2)}, u32[]{:S(2)}) collective-permute-start(bf16[1024,128]{0,1:T(8,128)(2,1)S(1)} %pad_maximum_fusion.3), channel_id=1, source_target_pairs={{0,192},{64,128},{128,64},{192,0},{256,448},{320,384},{384,320},{4... | collective-permute-start | bytes 786440 | tf_op jit(solution)/shard_map/ppermute | solution.py:15
  16.4 9.1 %collective-permute-start = (bf16[1024,128]{0,1:T(8,128)(2,1)S(1)}, bf16[1024,128]{0,1:T(8,128)(2,1)S(1)}, u32[]{:S(2)}, u32[]{:S(2)}) collective-permute-start(bf16[1024,128]{0,1:T(8,128)(2,1)S(1)} %pad_maximum_fusion.3), channel_id=1, source_target_pairs={{0,64},{64,0},{128,192},{192,128},{256,320},{320,256},{384,448},{4... | collective-permute-start | bytes 786440 | tf_op jit(solution)/shard_map/ppermute | solution.py:15
  25.6 13.4 %collective-permute-start.4 = (bf16[4096,128]{0,1:T(8,128)(2,1)S(1)}, bf16[4096,128]{0,1:T(8,128)(2,1)}, u32[]{:S(2)}, u32[]{:S(2)}) collective-permute-start(bf16[4096,128]{0,1:T(8,128)(2,1)S(1)} %pad_maximum_fusion), channel_id=1, source_target_pairs={{0,1},{1,0},{2,3},{3,2},{4,5},{5,4},{6,7},{7,6},{8,9},{9,8},{10,11... | collective-permute-start | bytes 3145736 | tf_op jit(solution)/shard_map/ppermute | solution.py:15
  47.7 17.7 %collective-permute-start.5 = (f32[1024,128]{0,1:T(8,128)S(1)}, f32[1024,128]{0,1:T(8,128)S(1)}, u32[]{:S(2)}, u32[]{:S(2)}) collective-permute-start(f32[1024,128]{0,1:T(8,128)S(1)} %pad_maximum_fusion.2), channel_id=1, source_target_pairs={{0,256},{64,320},{128,384},{192,448},{256,0},{320,64},{384,128},{4... | collective-permute-start | bytes 1572872 | tf_op jit(solution)/shard_map/ppermute | solution.py:15
  66.2 6.2 %collective-permute-start.7 = (f32[2,64,64]{2,1,0:T(8,128)S(1)}, f32[2,64,64]{2,1,0:T(8,128)S(1)}, u32[]{:S(2)}, u32[]{:S(2)}) collective-permute-start(f32[2,64,64]{2,1,0:T(8,128)S(1)} %pad_maximum_fusion.4), channel_id=1, source_target_pairs={{0,64},{64,0},{128,192},{192,128},{256,320},{320,256},{384,448},{4... | collective-permute-start | bytes 98312 | tf_op jit(solution)/shard_map/ppermute | solution.py:15
  68.8 7.4 %collective-permute-start.6 = (f32[64,64]{1,0:T(8,128)S(1)}, f32[64,64]{1,0:T(8,128)S(1)}, u32[]{:S(2)}, u32[]{:S(2)}) collective-permute-start(f32[64,64]{1,0:T(8,128)S(1)} %fusion.42), channel_id=1, source_target_pairs={{0,64},{64,0},{128,192},{192,128},{256,320},{320,256},{384,448},{4... | collective-permute-start | bytes 49160 | tf_op jit(solution)/shard_map/ppermute | solution.py:15
  72.5 7.7 %collective-permute-start.8 = (f32[2,64,64]{2,1,0:T(8,128)S(1)}, f32[2,64,64]{2,1,0:T(8,128)S(1)}, u32[]{:S(2)}, u32[]{:S(2)}) collective-permute-start(f32[2,64,64]{2,1,0:T(8,128)S(1)} %fusion.41), channel_id=1, source_target_pairs={{0,128},{64,192},{128,0},{192,64},{256,384},{320,448},{384,256},{4... | collective-permute-start | bytes 98312 | tf_op jit(solution)/shard_map/ppermute | solution.py:15
  80.2 7.3 %collective-permute-start.9 = (f32[64,64]{1,0:T(8,128)S(1)}, f32[64,64]{1,0:T(8,128)S(1)}, u32[]{:S(2)}, u32[]{:S(2)}) collective-permute-start(f32[64,64]{1,0:T(8,128)S(1)} %get-tuple-element.7), channel_id=1, source_target_pairs={{0,256},{64,320},{128,384},{192,448},{256,0},{320,64},{384,128},{4... | collective-permute-start | bytes 49160 | tf_op jit(solution)/shard_map/ppermute | solution.py:15
  82.5 5.0 %copy-start.2 = (f32[4]{0:T(128)S(1)}, f32[4]{0:T(128)}, u32[]{:S(2)}) copy-start(f32[4]{0:T(128)} %constant.7) | copy-start | bytes 52

commit v8 on v7

--- a/solution.py
+++ b/solution.py
@@ -83,19 +83,13 @@
     results.append(product)
     grams.append(gram_of(product))
     n_tiers = len(grams)
-    done = [grams[0]]
-    for tier_num in range(1, n_tiers - 1):
-        if tier_num == n_tiers - 2:
-            break
-        local = grams[tier_num]
-        for bit_num in range(tier_num):
-            local = local + swapped(local, "leaf", bit_num)
-        done.append(local)
-    tail = jnp.stack(grams[n_tiers - 2:])
-    for bit_num in range(n_tiers - 2):
+    first = jnp.stack(grams[1:])
+    first = first + swapped(first, "leaf", 0)
+    tail = first[1:]
+    for bit_num in range(1, n_tiers - 2):
         tail = tail + swapped(tail, "leaf", bit_num)
-    last = tail[1] + swapped(tail[1], "leaf", n_tiers - 2)
-    done.extend([tail[0], last])
+    last = tail[-1] + swapped(tail[-1], "leaf", n_tiers - 2)
+    done = [grams[0], first[0], tail[0], last]
     stacked = jnp.stack(done)
     divisors = jnp.asarray(
         [float((1 << tier_num) * rows_n) for tier_num in range(len(grams))], jnp.float32

time: 88.8 us -> 89 us (level)
  waiting for transfers between devices: 22.7 us -> 26.7 us
  starting transfers between devices: 31 us -> 27.3 us
    ppermute x10 -> x9, waiting for transfers between devices: 22.7 us -> 26.7 us  [exchanged(): return lax.ppermute(value, axis, pairs)]
    ppermute x10 -> x9, starting transfers between devices: 31 us -> 27.3 us  [exchanged(): return lax.ppermute(value, axis, pairs)]
  transfers between devices with their start and end apart: 10 -> 9, of which waited for: 5 -> 6; matrix products, arithmetic and copies ran while one was open for 23% -> 23% of each run, Pallas kernels for 0% -> 0%
where the time goes in v8:
time: 89 us; the launch traced here: 88.5 us
  matrix products  28.8 us (32%)
  starting transfers between devices  27.3 us (31%)
  waiting for transfers between devices  26.7 us (30%)
  other arithmetic  2.51 us (3%)
  local copies, waits for them, and re-layouts  2.27 us (3%)
  between operations  0.91 us (1%)
    ppermute x9, starting transfers between devices, exchanged(): return lax.ppermute(value, axis, pairs)  27.3 us
    ppermute x9, waiting for transfers between devices, exchanged(): return lax.ppermute(value, axis, pairs)  26.7 us
    dot_general x5, matrix products, raw_product(): return jnp.dot(kernel, col_sketch, preferred_element_type=jnp.float32)  25.7 us
    unnamed x8, local copies, waits for them, and re-layouts  2.23 us
  transfers between devices with their start and end apart: 9, of which 6 were waited for; matrix products, arithmetic and copies ran while one was open for 23% of the time, Pallas kernels for 0%

profile of v8, /device:TPU:416, one launch (start us, length us, event | category | flops | bytes accessed | tf_op | source)
XLA Modules:
  0.0 88.5 jit_solution(9319440288072453804)
XLA Ops:
  0.6 0.0 copy-start
  0.6 0.0 copy-start.1
  0.7 0.9 copy-done
  1.5 1.7 %multiply_reduce_fusion.5 = (f32[1024]{0:T(1024)S(1)}, bf16[1024,64]{0,1:T(8,128)(2,1)S(1)}) fusion(bf16[1024,64]{0,1:T(8,128)(2,1)S(1)} %copy-done, s32[1024]{0:T(1024)} %bitcast.31), kind=kOutput, calls=%fused_computation.39 | convolution fusion | flops 135527424 | bytes 270336 | tf_op jit(solution)/shard_map/dot_general | solution.py:44
  3.3 0.0 copy-done.1
  3.3 4.9 %collective-permute-start.1 = (bf16[1024,128]{0,1:T(8,128)(2,1)S(1)}, bf16[1024,128]{0,1:T(8,128)(2,1)S(1)}, u32[]{:S(2)}, u32[]{:S(2)}) collective-permute-start(bf16[1024,128]{0,1:T(8,128)(2,1)S(1)} %pad_maximum_fusion.3), channel_id=1, source_target_pairs={{0,128},{64,192},{128,0},{192,64},{256,384},{320,448},{384,256},{4... | collective-permute-start | bytes 786440 | tf_op jit(solution)/shard_map/ppermute | solution.py:15
  8.2 5.1 %collective-permute-start.3 = (bf16[1024,64]{0,1:T(8,128)(2,1)S(1)}, bf16[1024,64]{0,1:T(8,128)(2,1)S(1)}, u32[]{:S(2)}, u32[]{:S(2)}) collective-permute-start(bf16[1024,64]{0,1:T(8,128)(2,1)S(1)} %get-tuple-element.9), channel_id=1, source_target_pairs={{0,256},{64,320},{128,384},{192,448},{256,0},{320,64},{384,128},{4... | collective-permute-start | bytes 393224 | tf_op jit(solution)/shard_map/ppermute | solution.py:15
  13.3 3.1 %collective-permute-start.2 = (bf16[1024,128]{0,1:T(8,128)(2,1)S(1)}, bf16[1024,128]{0,1:T(8,128)(2,1)S(1)}, u32[]{:S(2)}, u32[]{:S(2)}) collective-permute-start(bf16[1024,128]{0,1:T(8,128)(2,1)S(1)} %pad_maximum_fusion.3), channel_id=1, source_target_pairs={{0,192},{64,128},{128,64},{192,0},{256,448},{320,384},{384,320},{4... | collective-permute-start | bytes 786440 | tf_op jit(solution)/shard_map/ppermute | solution.py:15
  16.4 1.9 %collective-permute-start = (bf16[1024,128]{0,1:T(8,128)(2,1)S(1)}, bf16[1024,128]{0,1:T(8,128)(2,1)S(1)}, u32[]{:S(2)}, u32[]{:S(2)}) collective-permute-start(bf16[1024,128]{0,1:T(8,128)(2,1)S(1)} %pad_maximum_fusion.3), channel_id=1, source_target_pairs={{0,64},{64,0},{128,192},{192,128},{256,320},{320,256},{384,448},{4... | collective-permute-start | bytes 786440 | tf_op jit(solution)/shard_map/ppermute | solution.py:15
  18.3 0.0 collective-permute-done.3
  18.4 0.0 collective-permute-done.1
  18.4 5.5 %collective-permute-done.2 = bf16[1024,128]{0,1:T(8,128)(2,1)S(1)} collective-permute-done((bf16[1024,128]{0,1:T(8,128)(2,1)S(1)}, bf16[1024,128]{0,1:T(8,128)(2,1)S(1)}, u32[]{:S(2)}, u32[]{:S(2)}) %collective-permute-start.2) | collective-permute-done | bytes 262176 | tf_op jit(solution)/shard_map/ppermute | solution.py:15
  24.0 0.1 multiply_reduce_fusion.2
  24.0 1.5 %collective-permute-done = bf16[1024,128]{0,1:T(8,128)(2,1)S(1)} collective-permute-done((bf16[1024,128]{0,1:T(8,128)(2,1)S(1)}, bf16[1024,128]{0,1:T(8,128)(2,1)S(1)}, u32[]{:S(2)}, u32[]{:S(2)}) %collective-permute-start) | collective-permute-done | bytes 262176 | tf_op jit(solution)/shard_map/ppermute | solution.py:15
  25.5 0.1 pad_maximum_fusion
  25.6 1.9 %collective-permute-start.4 = (bf16[4096,128]{0,1:T(8,128)(2,1)S(1)}, bf16[4096,128]{0,1:T(8,128)(2,1)}, u32[]{:S(2)}, u32[]{:S(2)}) collective-permute-start(bf16[4096,128]{0,1:T(8,128)(2,1)S(1)} %pad_maximum_fusion), channel_id=1, source_target_pairs={{0,1},{1,0},{2,3},{3,2},{4,5},{5,4},{6,7},{7,6},{8,9},{9,8},{10,11... | collective-permute-start | bytes 3145736 | tf_op jit(solution)/shard_map/ppermute | solution.py:15
  27.5 3.2 %fusion.8 = f32[1024,64]{0,1:T(8,128)S(1)} fusion(bf16[1024,64]{0,1:T(8,128)(2,1)S(1)} %get-tuple-element.9, f32[2048]{0:T(1024)S(1)} %multiply_reduce_fusion.2, f32[1024]{0:T(1024)S(1)} %get-tuple-element.8, bf16[2048,128]{0,1:T(8,128)(2,1)S(1)} %constant_dynamic-update-slice_fusion), kind=kOutput, calls=%fused_computation.14 | convolution fusion | flops 549519360 | bytes 929792 | tf_op jit(solution)/shard_map/dot_general | solution.py:31
  30.7 1.7 %fusion.7 = f32[1024,64]{0,1:T(8,128)S(1)} fusion(bf16[1024,64]{0,1:T(8,128)(2,1)S(1)} %get-tuple-element.9, f32[1024]{0:T(1024)S(1)} %multiply_reduce_fusion.4, f32[1024]{0:T(1024)S(1)} %get-tuple-element.8, bf16[1024,128]{0,1:T(8,128)(2,1)S(1)} %collective-permute-done), kind=kOutput, calls=%fused_computation.13 | convolution fusion | flops 274792448 | bytes 663552 | tf_op jit(solution)/shard_map/dot_general | solution.py:31
  32.4 0.4 convolution_bitcast_fusion.2
  32.8 0.1 multiply_reduce_fusion.1
  32.9 6.1 %fusion.2 = f32[1024,64]{0,1:T(8,128)S(1)} fusion(bf16[1024,64]{0,1:T(8,128)(2,1)S(1)} %collective-permute-done.3, f32[4096]{0:T(1024)S(1)} %multiply_reduce_fusion.1, f32[1024]{0:T(1024)S(1)} %multiply_reduce_fusion.3, bf16[4096,128]{0,1:T(8,128)(2,1)S(1)} %pad_maximum_fusion), kind=kOutput, calls=%fused_computation.8 | convolution fusion | flops 1098907648 | bytes 1462272 | tf_op jit(solution)/shard_map/dot_general | solution.py:31
  39.0 0.0 collective-permute-done.4
  39.0 1.2 %multiply_reduce_fusion = f32[4096]{0:T(1024)S(1)} fusion(bf16[4096,128]{0,1:T(8,128)(2,1)} %collective-permute-done.4), kind=kLoop, calls=%fused_computation.22 | loop fusion | flops 782336 | bytes 540672 | tf_op jit(solution)/shard_map/reduce_sum | solution.py:19
  40.2 7.5 %fusion.3 = f32[1024,64]{0,1:T(8,128)S(1)} fusion(bf16[1024,64]{0,1:T(8,128)(2,1)S(1)} %collective-permute-done.3, f32[4096]{0:T(1024)S(1)} %multiply_reduce_fusion, f32[1024]{0:T(1024)S(1)} %multiply_reduce_fusion.3, bf16[4096,128]{0,1:T(8,128)(2,1)} %collective-permute-done.4), kind=kOutput, calls=%fused_computation.9 | convolution fusion | flops 1098907648 | bytes 1462272 | tf_op jit(solution)/shard_map/dot_general | solution.py:31
  47.7 2.2 %collective-permute-start.5 = (f32[1024,128]{0,1:T(8,128)S(1)}, f32[1024,128]{0,1:T(8,128)S(1)}, u32[]{:S(2)}, u32[]{:S(2)}) collective-permute-start(f32[1024,128]{0,1:T(8,128)S(1)} %pad_maximum_fusion.2), channel_id=1, source_target_pairs={{0,256},{64,320},{128,384},{192,448},{256,0},{320,64},{384,128},{4... | collective-permute-start | bytes 1572872 | tf_op jit(solution)/shard_map/ppermute | solution.py:15
  49.9 7.3 %fusion.4 = f32[1024,64]{0,1:T(8,128)S(1)} fusion(bf16[1024,64]{0,1:T(8,128)(2,1)S(1)} %get-tuple-element.9, f32[1024]{0:T(1024)S(1)} %get-tuple-element.8, f32[4096]{0:T(1024)S(1)} %multiply_reduce_fusion, bf16[4096,128]{0,1:T(8,128)(2,1)} %collective-permute-done.4), kind=kOutput, calls=%fused_computation.10 | convolution fusion | flops 1098907648 | bytes 1462272 | tf_op jit(solution)/shard_map/dot_general | solution.py:31
  57.2 8.2 %collective-permute-done.5 = f32[1024,128]{0,1:T(8,128)S(1)} collective-permute-done((f32[1024,128]{0,1:T(8,128)S(1)}, f32[1024,128]{0,1:T(8,128)S(1)}, u32[]{:S(2)}, u32[]{:S(2)}) %collective-permute-start.5) | collective-permute-done | bytes 524320 | tf_op jit(solution)/shard_map/ppermute | solution.py:15
  65.4 0.1 slice_multiply_fusion
  65.5 0.4 convolution_bitcast_fusion
  65.9 0.4 convolution_bitcast_fusion.1
  66.2 2.2 %collective-permute-start.6 = (f32[3,64,64]{2,1,0:T(8,128)S(1)}, f32[3,64,64]{2,1,0:T(8,128)S(1)}, u32[]{:S(2)}, u32[]{:S(2)}) collective-permute-start(f32[3,64,64]{2,1,0:T(8,128)S(1)} %pad_maximum_fusion.4), channel_id=1, source_target_pairs={{0,64},{64,0},{128,192},{192,128},{256,320},{320,256},{384,448},{4... | collective-permute-start | bytes 147464 | tf_op jit(solution)/shard_map/ppermute | solution.py:15
  68.4 0.4 convolution_bitcast_fusion.3
  68.8 3.9 %collective-permute-done.6 = f32[3,64,64]{2,1,0:T(8,128)S(1)} collective-permute-done((f32[3,64,64]{2,1,0:T(8,128)S(1)}, f32[3,64,64]{2,1,0:T(8,128)S(1)}, u32[]{:S(2)}, u32[]{:S(2)}) %collective-permute-start.6) | collective-permute-done | bytes 49184 | tf_op jit(solution)/shard_map/ppermute | solution.py:15
  72.8 3.7 %collective-permute-start.7 = (f32[2,64,64]{2,1,0:T(8,128)S(1)}, f32[2,64,64]{2,1,0:T(8,128)S(1)}, u32[]{:S(2)}, u32[]{:S(2)}) collective-permute-start(f32[2,64,64]{2,1,0:T(8,128)S(1)} %slice.70), channel_id=1, source_target_pairs={{0,128},{64,192},{128,0},{192,64},{256,384},{320,448},{384,256},{4... | collective-permute-start | bytes 98312 | tf_op jit(solution)/shard_map/ppermute | solution.py:15
  76.5 0.1 pad_maximum_fusion.1
  76.6 0.0 copy-start.2
  76.6 1.3 %copy.6 = f32[1024,256]{1,0:T(8,128)} copy(f32[1024,256]{0,1:T(8,128)S(1)} %pad_maximum_fusion.1) | data formatting | bytes 2097152
  77.9 2.5 %collective-permute-done.7 = f32[2,64,64]{2,1,0:T(8,128)S(1)} collective-permute-done((f32[2,64,64]{2,1,0:T(8,128)S(1)}, f32[2,64,64]{2,1,0:T(8,128)S(1)}, u32[]{:S(2)}, u32[]{:S(2)}) %collective-permute-start.7) | collective-permute-done | bytes 32800 | tf_op jit(solution)/shard_map/ppermute | solution.py:15
  80.5 2.2 %collective-permute-start.8 = (f32[64,64]{1,0:T(8,128)S(1)}, f32[64,64]{1,0:T(8,128)S(1)}, u32[]{:S(2)}, u32[]{:S(2)}) collective-permute-start(f32[64,64]{1,0:T(8,128)S(1)} %get-tuple-element.7), channel_id=1, source_target_pairs={{0,256},{64,320},{128,384},{192,448},{256,0},{320,64},{384,128},{4... | collective-permute-start | bytes 49160 | tf_op jit(solution)/shard_map/ppermute | solution.py:15
  82.7 5.1 %collective-permute-done.8 = f32[64,64]{1,0:T(8,128)S(1)} collective-permute-done((f32[64,64]{1,0:T(8,128)S(1)}, f32[64,64]{1,0:T(8,128)S(1)}, u32[]{:S(2)}, u32[]{:S(2)}) %collective-permute-start.8) | collective-permute-done | bytes 16416 | tf_op jit(solution)/shard_map/ppermute | solution.py:15
  87.8 0.0 copy-done.2
  87.8 0.7 maximum_multiply_fusion
  (13 shorter events, 0.2 us)
Async XLA Ops:
  0.6 0.9 %copy-start = (bf16[1024,64]{0,1:T(8,128)(2,1)S(1)}, bf16[1024,64]{0,1:T(8,128)(2,1)}, u32[]{:S(2)}) copy-start(bf16[1024,64]{0,1:T(8,128)(2,1)} %param.4) | copy-start | bytes 393220
  0.6 2.6 %copy-start.1 = (bf16[1024,64]{0,1:T(8,128)(2,1)S(1)}, bf16[1024,64]{0,1:T(8,128)(2,1)}, u32[]{:S(2)}) copy-start(bf16[1024,64]{0,1:T(8,128)(2,1)} %param.5) | copy-start | bytes 393220
  3.3 15.1 %collective-permute-start.1 = (bf16[1024,128]{0,1:T(8,128)(2,1)S(1)}, bf16[1024,128]{0,1:T(8,128)(2,1)S(1)}, u32[]{:S(2)}, u32[]{:S(2)}) collective-permute-start(bf16[1024,128]{0,1:T(8,128)(2,1)S(1)} %pad_maximum_fusion.3), channel_id=1, source_target_pairs={{0,128},{64,192},{128,0},{192,64},{256,384},{320,448},{384,256},{4... | collective-permute-start | bytes 786440 | tf_op jit(solution)/shard_map/ppermute | solution.py:15
  8.2 10.1 %collective-permute-start.3 = (bf16[1024,64]{0,1:T(8,128)(2,1)S(1)}, bf16[1024,64]{0,1:T(8,128)(2,1)S(1)}, u32[]{:S(2)}, u32[]{:S(2)}) collective-permute-start(bf16[1024,64]{0,1:T(8,128)(2,1)S(1)} %get-tuple-element.9), channel_id=1, source_target_pairs={{0,256},{64,320},{128,384},{192,448},{256,0},{320,64},{384,128},{4... | collective-permute-start | bytes 393224 | tf_op jit(solution)/shard_map/ppermute | solution.py:15
  13.3 10.6 %collective-permute-start.2 = (bf16[1024,128]{0,1:T(8,128)(2,1)S(1)}, bf16[1024,128]{0,1:T(8,128)(2,1)S(1)}, u32[]{:S(2)}, u32[]{:S(2)}) collective-permute-start(bf16[1024,128]{0,1:T(8,128)(2,1)S(1)} %pad_maximum_fusion.3), channel_id=1, source_target_pairs={{0,192},{64,128},{128,64},{192,0},{256,448},{320,384},{384,320},{4... | collective-permute-start | bytes 786440 | tf_op jit(solution)/shard_map/ppermute | solution.py:15
  16.4 9.1 %collective-permute-start = (bf16[1024,128]{0,1:T(8,128)(2,1)S(1)}, bf16[1024,128]{0,1:T(8,128)(2,1)S(1)}, u32[]{:S(2)}, u32[]{:S(2)}) collective-permute-start(bf16[1024,128]{0,1:T(8,128)(2,1)S(1)} %pad_maximum_fusion.3), channel_id=1, source_target_pairs={{0,64},{64,0},{128,192},{192,128},{256,320},{320,256},{384,448},{4... | collective-permute-start | bytes 786440 | tf_op jit(solution)/shard_map/ppermute | solution.py:15
  25.6 13.4 %collective-permute-start.4 = (bf16[4096,128]{0,1:T(8,128)(2,1)S(1)}, bf16[4096,128]{0,1:T(8,128)(2,1)}, u32[]{:S(2)}, u32[]{:S(2)}) collective-permute-start(bf16[4096,128]{0,1:T(8,128)(2,1)S(1)} %pad_maximum_fusion), channel_id=1, source_target_pairs={{0,1},{1,0},{2,3},{3,2},{4,5},{5,4},{6,7},{7,6},{8,9},{9,8},{10,11... | collective-permute-start | bytes 3145736 | tf_op jit(solution)/shard_map/ppermute | solution.py:15
  47.7 17.7 %collective-permute-start.5 = (f32[1024,128]{0,1:T(8,128)S(1)}, f32[1024,128]{0,1:T(8,128)S(1)}, u32[]{:S(2)}, u32[]{:S(2)}) collective-permute-start(f32[1024,128]{0,1:T(8,128)S(1)} %pad_maximum_fusion.2), channel_id=1, source_target_pairs={{0,256},{64,320},{128,384},{192,448},{256,0},{320,64},{384,128},{4... | collective-permute-start | bytes 1572872 | tf_op jit(solution)/shard_map/ppermute | solution.py:15
  66.2 6.5 %collective-permute-start.6 = (f32[3,64,64]{2,1,0:T(8,128)S(1)}, f32[3,64,64]{2,1,0:T(8,128)S(1)}, u32[]{:S(2)}, u32[]{:S(2)}) collective-permute-start(f32[3,64,64]{2,1,0:T(8,128)S(1)} %pad_maximum_fusion.4), channel_id=1, source_target_pairs={{0,64},{64,0},{128,192},{192,128},{256,320},{320,256},{384,448},{4... | collective-permute-start | bytes 147464 | tf_op jit(solution)/shard_map/ppermute | solution.py:15
  72.8 7.7 %collective-permute-start.7 = (f32[2,64,64]{2,1,0:T(8,128)S(1)}, f32[2,64,64]{2,1,0:T(8,128)S(1)}, u32[]{:S(2)}, u32[]{:S(2)}) collective-permute-start(f32[2,64,64]{2,1,0:T(8,128)S(1)} %slice.70), channel_id=1, source_target_pairs={{0,128},{64,192},{128,0},{192,64},{256,384},{320,448},{384,256},{4... | collective-permute-start | bytes 98312 | tf_op jit(solution)/shard_map/ppermute | solution.py:15
  76.6 11.2 %copy-start.2 = (f32[4]{0:T(128)S(1)}, f32[4]{0:T(128)}, u32[]{:S(2)}) copy-start(f32[4]{0:T(128)} %constant.7) | copy-start | bytes 52
  80.5 7.3 %collective-permute-start.8 = (f32[64,64]{1,0:T(8,128)S(1)}, f32[64,64]{1,0:T(8,128)S(1)}, u32[]{:S(2)}, u32[]{:S(2)}) collective-permute-start(f32[64,64]{1,0:T(8,128)S(1)} %get-tuple-element.7), channel_id=1, source_target_pairs={{0,256},{64,320},{128,384},{192,448},{256,0},{320,64},{384,128},{4... | collective-permute-start | bytes 49160 | tf_op jit(solution)/shard_map/ppermute | solution.py:15
